TPU v7x, 512 devices: a whole 4x4x16 slice. The times are simulated.
512 devices in a mesh: lon: 32 (over y_lo, z), lat: 16 (over x, y_hi, core).
Axes of the slice: x: 4, y: 4 (y_hi: 2, y_lo: 2; y = y_hi * 2 + y_lo), z: 16, core: 2. Of those that a mesh axis runs over, the one named last changes fastest.
Arguments:
- control: float32 [80, 512, 4096], P(None, 'lat', 'lon'), may hold values from -6 to 6
- diffusivity: float32 [512, 4096], P('lat', 'lon'), may hold values from 0.02 to 0.12
- land_mask: int32 [512, 4096], P('lat', 'lon'), may hold values 0 or 1
- innovations: float32 [16, 80, 4096], P('lat', None, 'lon'), may hold values from -6 to 6
- obs_sigma: float32 [16, 80, 4096], P('lat', None, 'lon'), may hold values from 0.5 to 2
- obs_row: int32 [16, 4096], P('lat', 'lon'), may hold values from 0 to 31
- obs_col: int32 [16, 4096], P('lat', 'lon'), may hold values from 0 to 127
- obs_frac: float32 [16, 2, 4096], P('lat', None, 'lon'), may hold values from 0 to 1
- obs_counts: int32 [16, 32], P('lat', 'lon'), may hold values from 32 to 128, as said below
Outputs:
- obs_gradient: float32 [80, 512, 4096], P(None, 'lat', 'lon')
- departures: float32 [16, 80, 4096], P('lat', None, 'lon')
Inputs may be any that keep to these rules, and one draw needn't show every extreme that they name: `obs_counts`: every tile holds between 32 and 128 live profiles in its first slots; some tile holds exactly 128.
All inputs are finite; a program needn't handle non-finite values. No bound on the sum of `land_mask` on one device may be relied on, other than what follows from the above.
Results may differ from a plain program's by a relative error of at most 0.00002.
Values sent between devices are 32-bit elements; how exact they have to be, the bound alone decides.
No kernel may reach another device: no remote copies, remote signals or barrier semaphores. Data moves between devices by JAX's collectives and lax.ppermute only.
A program may use at most 64 MiB of HBM per device.

v0:
```python
import jax
import jax.numpy as jnp
from jax import lax
from jax.sharding import PartitionSpec as P


def with_halo(block, sides, width, periodic):
    for axis, dim in sides:
        count = lax.axis_size(axis)
        forward = [(i, i + 1) for i in range(count - 1)]
        if periodic:
            forward.append((count - 1, 0))
        backward = [(target, source) for source, target in forward]
        low = lax.ppermute(
            lax.slice_in_dim(block, block.shape[dim] - width, None, axis=dim), axis, forward
        )
        high = lax.ppermute(lax.slice_in_dim(block, 0, width, axis=dim), axis, backward)
        block = jnp.concatenate([low, block, high], axis=dim)
    return block


def shifted(block, axis, distance):
    devices = range(lax.axis_size(axis))
    route = [(i - distance, i) for i in devices if i - distance in devices]
    return lax.ppermute(block, axis, route)


def passed_along(value, axis, steps):
    count = lax.axis_size(axis)
    pairs = [(source, (source + steps) % count) for source in range(count)]
    return lax.ppermute(value, axis, pairs)


def window(array, offset_y, offset_x):
    return array[
        ...,
        1 + offset_y : array.shape[-2] - 1 + offset_y,
        1 + offset_x : array.shape[-1] - 1 + offset_x,
    ]


def diffuse(padded, kappa_pad, mask_pad):
    center = window(padded, 0, 0)
    kappa_mid = window(kappa_pad, 0, 0)
    mask_mid = window(mask_pad, 0, 0)
    result = center
    for offset_y, offset_x in ((0, 1), (0, -1), (1, 0), (-1, 0)):
        weight = (
            0.5
            * (kappa_mid + window(kappa_pad, offset_y, offset_x))
            * mask_mid
            * window(mask_pad, offset_y, offset_x)
        )
        result = result + weight * (window(padded, offset_y, offset_x) - center)
    return result


def pad_tile(field, width):
    lon_padded = with_halo(field, (("lon", 2),), width, True)
    return with_halo(lon_padded, (("lat", 1),), width, False)


def on_device(
    control, diffusivity, land_mask, innovations, obs_sigma, obs_row, obs_col, obs_frac, obs_counts
):
    depth = 1
    coeff = jnp.stack([diffusivity, land_mask.astype(jnp.float32)])
    coeff_pad = pad_tile(coeff, depth)

    def smooth(field):
        for repeat in range(2):
            field = diffuse(pad_tile(field, 1), coeff_pad[0], coeff_pad[1])
        return field

    padded = pad_tile(smooth(control), 1)
    channels = padded.shape[0]
    cols_pad = padded.shape[2]
    flat = padded.reshape(channels, -1)
    base = (obs_row[0] + 1) * cols_pad + obs_col[0] + 1
    offsets = jnp.stack([base, base + 1, base + cols_pad, base + cols_pad + 1])
    frac_y = obs_frac[0, 0]
    frac_x = obs_frac[0, 1]
    weights = jnp.stack(
        [
            (1.0 - frac_y) * (1.0 - frac_x),
            (1.0 - frac_y) * frac_x,
            frac_y * (1.0 - frac_x),
            frac_y * frac_x,
        ]
    )
    sample = jnp.sum(weights[None] * flat[:, offsets], axis=1)
    slots = jnp.arange(obs_row.shape[1], dtype=jnp.int32)
    valid = (slots < obs_counts[0, 0]).astype(jnp.float32)
    departure = valid * (sample - innovations[0])
    weighted = departure / (obs_sigma[0] * obs_sigma[0])
    spread = (weights[None] * weighted[:, None, :]).reshape(channels, -1)
    adjoint = jnp.zeros_like(flat).at[:, offsets.reshape(-1)].add(spread).reshape(padded.shape)
    north = shifted(adjoint[:, -1, :], "lat", 1)
    adjoint = adjoint.at[:, 1, :].add(north)
    east = passed_along(adjoint[:, 1:-1, -1], "lon", 1)
    inner = adjoint[:, 1:-1, 1:-1].at[:, :, 0].add(east)
    return (smooth(inner), departure[None])


def solution(mesh):
    in_specs = (
        P(None, "lat", "lon"),
        P("lat", "lon"),
        P("lat", "lon"),
        P("lat", None, "lon"),
        P("lat", None, "lon"),
        P("lat", "lon"),
        P("lat", "lon"),
        P("lat", None, "lon"),
        P("lat", "lon"),
    )
    out_specs = (P(None, "lat", "lon"), P("lat", None, "lon"))
    return jax.shard_map(
        on_device, mesh=mesh, in_specs=in_specs, out_specs=out_specs, check_vma=False
    )
```

profile of v0, /device:TPU:6, one launch (start us, length us, event | category | flops | bytes accessed | tf_op | source)
XLA Modules:
  0.0 173.6 jit_solution(16293287463476126858)
XLA Ops:
  2.3 3.8 %collective-permute-start = (f32[2,32,1]{2,1,0:T(8,128)S(1)}, f32[2,32,1]{2,1,0:T(8,128)S(1)}, u32[]{:S(2)}, u32[]{:S(2)}) collective-permute-start(f32[2,32,1]{2,1,0:T(8,128)S(1)} %get-tuple-element.60), channel_id=1, source_target_pairs={{0,16},{16,32},{32,48},{48,64},{64,80},{80,96},{96,112},{112,128},... | collective-permute-start | bytes 776 | tf_op jit(solution)/shard_map/ppermute | solution.py:14
  6.1 10.5 %collective-permute-start.1 = (f32[2,32,1]{2,1,0:T(8,128)S(1)}, f32[2,32,1]{2,1,0:T(8,128)S(1)}, u32[]{:S(2)}, u32[]{:S(2)}) collective-permute-start(f32[2,32,1]{2,1,0:T(8,128)S(1)} %get-tuple-element.61), channel_id=1, source_target_pairs={{16,0},{32,16},{48,32},{64,48},{80,64},{96,80},{112,96},{128,112},... | collective-permute-start | bytes 776 | tf_op jit(solution)/shard_map/ppermute | solution.py:17
  20.4 6.0 %collective-permute-start.4 = (f32[80,32,1]{0,2,1:T(1,128)S(1)}, f32[80,32,1]{0,2,1:T(1,128)S(1)}, u32[]{:S(2)}, u32[]{:S(2)}) collective-permute-start(f32[80,32,1]{0,2,1:T(1,128)S(1)} %get-tuple-element.51), channel_id=1, source_target_pairs={{16,0},{32,16},{48,32},{64,48},{80,64},{96,80},{112,96},{128,112},... | collective-permute-start | bytes 30728 | tf_op jit(solution)/shard_map/ppermute | solution.py:17
  28.6 6.0 %collective-permute-start.3 = (f32[2,1,130]{2,1,0:T(1,128)S(1)}, f32[2,1,130]{2,1,0:T(1,128)S(1)}, u32[]{:S(2)}, u32[]{:S(2)}) collective-permute-start(f32[2,1,130]{2,1,0:T(1,128)S(1)} %get-tuple-element.53), channel_id=1, source_target_pairs={{1,0},{2,1},{3,2},{4,3},{5,4},{6,5},{7,6},{8,7},{9,8},{10,9},{11,1... | collective-permute-start | bytes 3128 | tf_op jit(solution)/shard_map/ppermute | solution.py:17
  36.1 6.0 %collective-permute-start.6 = (f32[80,1,130]{0,2,1:T(8,128)S(1)}, f32[80,1,130]{0,2,1:T(8,128)S(1)}, u32[]{:S(2)}, u32[]{:S(2)}) collective-permute-start(f32[80,1,130]{0,2,1:T(8,128)S(1)} %get-tuple-element.42), channel_id=1, source_target_pairs={{1,0},{2,1},{3,2},{4,3},{5,4},{6,5},{7,6},{8,7},{9,8},{10,9},{11,1... | collective-permute-start | bytes 124808 | tf_op jit(solution)/shard_map/ppermute | solution.py:17
  44.2 6.0 %collective-permute-done.7 = f32[80,1,130]{0,2,1:T(8,128)S(1)} collective-permute-done((f32[80,1,130]{0,2,1:T(8,128)S(1)}, f32[80,1,130]{0,2,1:T(8,128)S(1)}, u32[]{:S(2)}, u32[]{:S(2)}) %collective-permute-start.7) | collective-permute-done | bytes 41632 | tf_op jit(solution)/shard_map/ppermute | solution.py:14
  50.1 3.4 %fusion.38 = f32[80,32,128]{0,2,1:T(8,128)S(1)} fusion(f32[80,32,128]{0,2,1:T(8,128)S(1)} %copy.50, f32[80,1,130]{0,2,1:T(8,128)S(1)} %collective-permute-done.7, f32[80,32,1]{0,2,1:T(1,128)S(1)} %collective-permute-done.4, f32[80,32,1]{0,2,1:T(1,128)S(1)} %collective-permute-done.5, f32[80,1,130]{0,2,1:T(8,128)S(1)} %collective-permute-done.6, ...), kind=kLoop, calls=%fused_computation.66 | loop fusion | flops 6553600 | bytes 2790656 | tf_op jit(solution)/shard_map/add | solution.py:54
  55.5 6.0 %collective-permute-start.8 = (f32[80,32,1]{0,2,1:T(1,128)S(1)}, f32[80,32,1]{0,2,1:T(1,128)S(1)}, u32[]{:S(2)}, u32[]{:S(2)}) collective-permute-start(f32[80,32,1]{0,2,1:T(1,128)S(1)} %get-tuple-element.49), channel_id=1, source_target_pairs={{16,0},{32,16},{48,32},{64,48},{80,64},{96,80},{112,96},{128,112},... | collective-permute-start | bytes 30728 | tf_op jit(solution)/shard_map/ppermute | solution.py:17
  65.0 2.4 %collective-permute-start.11 = (f32[80,1,130]{0,2,1:T(8,128)S(1)}, f32[80,1,130]{0,2,1:T(8,128)S(1)}, u32[]{:S(2)}, u32[]{:S(2)}) collective-permute-start(f32[80,1,130]{0,2,1:T(8,128)S(1)} %get-tuple-element.41), channel_id=1, source_target_pairs={{0,1},{1,2},{2,3},{3,4},{4,5},{5,6},{6,7},{7,8},{8,9},{9,10},{10,1... | collective-permute-start | bytes 124808 | tf_op jit(solution)/shard_map/ppermute | solution.py:14
  67.4 5.6 %collective-permute-done.11 = f32[80,1,130]{0,2,1:T(8,128)S(1)} collective-permute-done((f32[80,1,130]{0,2,1:T(8,128)S(1)}, f32[80,1,130]{0,2,1:T(8,128)S(1)}, u32[]{:S(2)}, u32[]{:S(2)}) %collective-permute-start.11) | collective-permute-done | bytes 41632 | tf_op jit(solution)/shard_map/ppermute | solution.py:14
  73.0 3.5 %fusion.26 = f32[80,32,128]{0,2,1:T(8,128)S(1)} fusion(f32[80,32,128]{0,2,1:T(8,128)S(1)} %fusion.38, f32[80,1,130]{0,2,1:T(8,128)S(1)} %collective-permute-done.11, f32[80,32,1]{0,2,1:T(1,128)S(1)} %collective-permute-done.8, f32[80,32,1]{0,2,1:T(1,128)S(1)} %collective-permute-done.9, f32[80,1,130]{0,2,1:T(8,128)S(1)} %collective-permute-done.10, ...), kind=kLoop, calls=%fused_computation.46 | loop fusion | flops 6553600 | bytes 2790656 | tf_op jit(solution)/shard_map/add | solution.py:54
  78.4 6.3 %collective-permute-start.13 = (f32[80,32,1]{0,2,1:T(1,128)S(1)}, f32[80,32,1]{0,2,1:T(1,128)S(1)}, u32[]{:S(2)}, u32[]{:S(2)}) collective-permute-start(f32[80,32,1]{0,2,1:T(1,128)S(1)} %get-tuple-element.47), channel_id=1, source_target_pairs={{16,0},{32,16},{48,32},{64,48},{80,64},{96,80},{112,96},{128,112},... | collective-permute-start | bytes 30728 | tf_op jit(solution)/shard_map/ppermute | solution.py:17
  88.1 6.0 %collective-permute-start.15 = (f32[80,1,130]{0,2,1:T(8,128)S(1)}, f32[80,1,130]{0,2,1:T(8,128)S(1)}, u32[]{:S(2)}, u32[]{:S(2)}) collective-permute-start(f32[80,1,130]{0,2,1:T(8,128)S(1)} %get-tuple-element.39), channel_id=1, source_target_pairs={{1,0},{2,1},{3,2},{4,3},{5,4},{6,5},{7,6},{8,7},{9,8},{10,9},{11,1... | collective-permute-start | bytes 124808 | tf_op jit(solution)/shard_map/ppermute | solution.py:17
  98.0 2.7 %gather_fusion = f32[512,80]{1,0:T(8,128)S(1)} fusion(f32[80,4420]{0,1:T(8,128)} %reshape.376, s32[1024]{0:T(1024)S(1)} %pad_clamp_fusion), kind=kCustom, calls=%fused_computation | custom fusion | bytes 329728 | tf_op jit(solution)/shard_map/gather | solution.py:91
  101.1 3.8 %scatter_custom_fusion = f32[80,4420]{0,1:T(8,128)} fusion(s32[512]{0:T(512)S(1)} %bitcast.79, f32[]{:T(128)} %constant.66.clone.1, f32[80,512]{0,1:T(8,128)S(1)} %bitcast_multiply_fusion), kind=kCustom, calls=%fused_computation.83 | custom fusion | flops 40960 | bytes 1676548 | tf_op jit(solution)/shard_map/scatter-add | solution.py:97
  109.2 6.2 %collective-permute-done.16 = f32[80,130]{0,1:T(8,128)S(1)} collective-permute-done((f32[80,130]{0,1:T(8,128)S(1)}, f32[80,130]{0,1:T(8,128)S(1)}, u32[]{:S(2)}, u32[]{:S(2)}) %collective-permute-start.16) | collective-permute-done | bytes 41632 | tf_op jit(solution)/shard_map/ppermute | solution.py:25
  120.6 4.2 %collective-permute-done.17 = f32[80,32]{0,1:T(8,128)S(1)} collective-permute-done((f32[80,32]{0,1:T(8,128)S(1)}, f32[80,32]{0,1:T(8,128)S(1)}, u32[]{:S(2)}, u32[]{:S(2)}) %collective-permute-start.17) | collective-permute-done | bytes 10272 | tf_op jit(solution)/shard_map/ppermute | solution.py:31
  127.8 6.0 %collective-permute-start.18 = (f32[80,32,1]{0,2,1:T(1,128)S(1)}, f32[80,32,1]{0,2,1:T(1,128)S(1)}, u32[]{:S(2)}, u32[]{:S(2)}) collective-permute-start(f32[80,32,1]{0,2,1:T(1,128)S(1)} %slice_add_fusion.1), channel_id=1, source_target_pairs={{16,0},{32,16},{48,32},{64,48},{80,64},{96,80},{112,96},{128,112},... | collective-permute-start | bytes 30728 | tf_op jit(solution)/shard_map/ppermute | solution.py:17
  137.2 2.4 %collective-permute-start.21 = (f32[80,1,130]{0,2,1:T(8,128)S(1)}, f32[80,1,130]{0,2,1:T(8,128)S(1)}, u32[]{:S(2)}, u32[]{:S(2)}) collective-permute-start(f32[80,1,130]{0,2,1:T(8,128)S(1)} %get-tuple-element.37), channel_id=1, source_target_pairs={{0,1},{1,2},{2,3},{3,4},{4,5},{5,6},{6,7},{7,8},{8,9},{9,10},{10,1... | collective-permute-start | bytes 124808 | tf_op jit(solution)/shard_map/ppermute | solution.py:14
  139.6 5.6 %collective-permute-done.21 = f32[80,1,130]{0,2,1:T(8,128)S(1)} collective-permute-done((f32[80,1,130]{0,2,1:T(8,128)S(1)}, f32[80,1,130]{0,2,1:T(8,128)S(1)}, u32[]{:S(2)}, u32[]{:S(2)}) %collective-permute-start.21) | collective-permute-done | bytes 41632 | tf_op jit(solution)/shard_map/ppermute | solution.py:14
  145.2 3.4 %fusion.14 = f32[80,32,128]{0,2,1:T(8,128)S(1)} fusion(f32[80,32,128]{0,2,1:T(8,128)S(1)} %scatter-add.19, f32[80,1,130]{0,2,1:T(8,128)S(1)} %collective-permute-done.21, f32[80,32,1]{0,2,1:T(1,128)S(1)} %collective-permute-done.18, f32[80,32,1]{0,2,1:T(1,128)S(1)} %collective-permute-done.19, f32[80,1,130]{0,2,1:T(8,128)S(1)} %collective-permute-done.20, ...), kind=kLoop, calls=%fused_computation.26 | loop fusion | flops 6553600 | bytes 2790656 | tf_op jit(solution)/shard_map/add | solution.py:54
  150.6 6.3 %collective-permute-start.22 = (f32[80,32,1]{0,2,1:T(1,128)S(1)}, f32[80,32,1]{0,2,1:T(1,128)S(1)}, u32[]{:S(2)}, u32[]{:S(2)}) collective-permute-start(f32[80,32,1]{0,2,1:T(1,128)S(1)} %get-tuple-element.45), channel_id=1, source_target_pairs={{16,0},{32,16},{48,32},{64,48},{80,64},{96,80},{112,96},{128,112},... | collective-permute-start | bytes 30728 | tf_op jit(solution)/shard_map/ppermute | solution.py:17
  163.4 5.0 %collective-permute-done.25 = f32[80,1,130]{0,2,1:T(8,128)S(1)} collective-permute-done((f32[80,1,130]{0,2,1:T(8,128)S(1)}, f32[80,1,130]{0,2,1:T(8,128)S(1)}, u32[]{:S(2)}, u32[]{:S(2)}) %collective-permute-start.25) | collective-permute-done | bytes 41632 | tf_op jit(solution)/shard_map/ppermute | solution.py:14
  168.3 3.5 %fusion.2 = f32[80,32,128]{0,2,1:T(8,128)S(1)} fusion(f32[80,32,128]{0,2,1:T(8,128)S(1)} %fusion.14, f32[80,1,130]{0,2,1:T(8,128)S(1)} %collective-permute-done.25, f32[80,32,1]{0,2,1:T(1,128)S(1)} %collective-permute-done.22, f32[80,32,1]{0,2,1:T(1,128)S(1)} %collective-permute-done.23, f32[80,1,130]{0,2,1:T(8,128)S(1)} %collective-permute-done.24, ...), kind=kLoop, calls=%fused_computation.6 | loop fusion | flops 6553600 | bytes 2790656 | tf_op jit(solution)/shard_map/add | solution.py:54
  (90 shorter events, 50.9 us)
Async XLA Ops:
  2.3 24.3 %collective-permute-start = (f32[2,32,1]{2,1,0:T(8,128)S(1)}, f32[2,32,1]{2,1,0:T(8,128)S(1)}, u32[]{:S(2)}, u32[]{:S(2)}) collective-permute-start(f32[2,32,1]{2,1,0:T(8,128)S(1)} %get-tuple-element.60), channel_id=1, source_target_pairs={{0,16},{16,32},{32,48},{48,64},{64,80},{80,96},{96,112},{112,128},... | collective-permute-start | bytes 776 | tf_op jit(solution)/shard_map/ppermute | solution.py:14
  6.1 20.5 %collective-permute-start.1 = (f32[2,32,1]{2,1,0:T(8,128)S(1)}, f32[2,32,1]{2,1,0:T(8,128)S(1)}, u32[]{:S(2)}, u32[]{:S(2)}) collective-permute-start(f32[2,32,1]{2,1,0:T(8,128)S(1)} %get-tuple-element.61), channel_id=1, source_target_pairs={{16,0},{32,16},{48,32},{64,48},{80,64},{96,80},{112,96},{128,112},... | collective-permute-start | bytes 776 | tf_op jit(solution)/shard_map/ppermute | solution.py:17
  18.5 17.6 %collective-permute-start.5 = (f32[80,32,1]{0,2,1:T(1,128)S(1)}, f32[80,32,1]{0,2,1:T(1,128)S(1)}, u32[]{:S(2)}, u32[]{:S(2)}) collective-permute-start(f32[80,32,1]{0,2,1:T(1,128)S(1)} %get-tuple-element.50), channel_id=1, source_target_pairs={{0,16},{16,32},{32,48},{48,64},{64,80},{80,96},{96,112},{112,128},... | collective-permute-start | bytes 30728 | tf_op jit(solution)/shard_map/ppermute | solution.py:14
  20.4 15.6 %collective-permute-start.4 = (f32[80,32,1]{0,2,1:T(1,128)S(1)}, f32[80,32,1]{0,2,1:T(1,128)S(1)}, u32[]{:S(2)}, u32[]{:S(2)}) collective-permute-start(f32[80,32,1]{0,2,1:T(1,128)S(1)} %get-tuple-element.51), channel_id=1, source_target_pairs={{16,0},{32,16},{48,32},{64,48},{80,64},{96,80},{112,96},{128,112},... | collective-permute-start | bytes 30728 | tf_op jit(solution)/shard_map/ppermute | solution.py:17
  26.6 8.0 %collective-permute-start.2 = (f32[2,1,130]{2,1,0:T(1,128)S(1)}, f32[2,1,130]{2,1,0:T(1,128)S(1)}, u32[]{:S(2)}, u32[]{:S(2)}) collective-permute-start(f32[2,1,130]{2,1,0:T(1,128)S(1)} %get-tuple-element.52), channel_id=1, source_target_pairs={{0,1},{1,2},{2,3},{3,4},{4,5},{5,6},{6,7},{7,8},{8,9},{9,10},{10,1... | collective-permute-start | bytes 3128 | tf_op jit(solution)/shard_map/ppermute | solution.py:14
  28.6 7.3 %collective-permute-start.3 = (f32[2,1,130]{2,1,0:T(1,128)S(1)}, f32[2,1,130]{2,1,0:T(1,128)S(1)}, u32[]{:S(2)}, u32[]{:S(2)}) collective-permute-start(f32[2,1,130]{2,1,0:T(1,128)S(1)} %get-tuple-element.53), channel_id=1, source_target_pairs={{1,0},{2,1},{3,2},{4,3},{5,4},{6,5},{7,6},{8,7},{9,8},{10,9},{11,1... | collective-permute-start | bytes 3128 | tf_op jit(solution)/shard_map/ppermute | solution.py:17
  36.1 8.1 %collective-permute-start.6 = (f32[80,1,130]{0,2,1:T(8,128)S(1)}, f32[80,1,130]{0,2,1:T(8,128)S(1)}, u32[]{:S(2)}, u32[]{:S(2)}) collective-permute-start(f32[80,1,130]{0,2,1:T(8,128)S(1)} %get-tuple-element.42), channel_id=1, source_target_pairs={{1,0},{2,1},{3,2},{4,3},{5,4},{6,5},{7,6},{8,7},{9,8},{10,9},{11,1... | collective-permute-start | bytes 124808 | tf_op jit(solution)/shard_map/ppermute | solution.py:17
  42.1 8.0 %collective-permute-start.7 = (f32[80,1,130]{0,2,1:T(8,128)S(1)}, f32[80,1,130]{0,2,1:T(8,128)S(1)}, u32[]{:S(2)}, u32[]{:S(2)}) collective-permute-start(f32[80,1,130]{0,2,1:T(8,128)S(1)} %get-tuple-element.43), channel_id=1, source_target_pairs={{0,1},{1,2},{2,3},{3,4},{4,5},{5,6},{6,7},{7,8},{8,9},{9,10},{10,1... | collective-permute-start | bytes 124808 | tf_op jit(solution)/shard_map/ppermute | solution.py:14
  53.6 8.0 %collective-permute-start.9 = (f32[80,32,1]{0,2,1:T(1,128)S(1)}, f32[80,32,1]{0,2,1:T(1,128)S(1)}, u32[]{:S(2)}, u32[]{:S(2)}) collective-permute-start(f32[80,32,1]{0,2,1:T(1,128)S(1)} %get-tuple-element.48), channel_id=1, source_target_pairs={{0,16},{16,32},{32,48},{48,64},{64,80},{80,96},{96,112},{112,128},... | collective-permute-start | bytes 30728 | tf_op jit(solution)/shard_map/ppermute | solution.py:14
  55.5 7.5 %collective-permute-start.8 = (f32[80,32,1]{0,2,1:T(1,128)S(1)}, f32[80,32,1]{0,2,1:T(1,128)S(1)}, u32[]{:S(2)}, u32[]{:S(2)}) collective-permute-start(f32[80,32,1]{0,2,1:T(1,128)S(1)} %get-tuple-element.49), channel_id=1, source_target_pairs={{16,0},{32,16},{48,32},{64,48},{80,64},{96,80},{112,96},{128,112},... | collective-permute-start | bytes 30728 | tf_op jit(solution)/shard_map/ppermute | solution.py:17
  65.0 8.0 %collective-permute-start.11 = (f32[80,1,130]{0,2,1:T(8,128)S(1)}, f32[80,1,130]{0,2,1:T(8,128)S(1)}, u32[]{:S(2)}, u32[]{:S(2)}) collective-permute-start(f32[80,1,130]{0,2,1:T(8,128)S(1)} %get-tuple-element.41), channel_id=1, source_target_pairs={{0,1},{1,2},{2,3},{3,4},{4,5},{5,6},{6,7},{7,8},{8,9},{9,10},{10,1... | collective-permute-start | bytes 124808 | tf_op jit(solution)/shard_map/ppermute | solution.py:14
  76.5 8.9 %collective-permute-start.12 = (f32[80,32,1]{0,2,1:T(1,128)S(1)}, f32[80,32,1]{0,2,1:T(1,128)S(1)}, u32[]{:S(2)}, u32[]{:S(2)}) collective-permute-start(f32[80,32,1]{0,2,1:T(1,128)S(1)} %get-tuple-element.46), channel_id=1, source_target_pairs={{0,16},{16,32},{32,48},{48,64},{64,80},{80,96},{96,112},{112,128},... | collective-permute-start | bytes 30728 | tf_op jit(solution)/shard_map/ppermute | solution.py:14
  78.4 7.7 %collective-permute-start.13 = (f32[80,32,1]{0,2,1:T(1,128)S(1)}, f32[80,32,1]{0,2,1:T(1,128)S(1)}, u32[]{:S(2)}, u32[]{:S(2)}) collective-permute-start(f32[80,32,1]{0,2,1:T(1,128)S(1)} %get-tuple-element.47), channel_id=1, source_target_pairs={{16,0},{32,16},{48,32},{64,48},{80,64},{96,80},{112,96},{128,112},... | collective-permute-start | bytes 30728 | tf_op jit(solution)/shard_map/ppermute | solution.py:17
  86.2 8.0 %collective-permute-start.14 = (f32[80,1,130]{0,2,1:T(8,128)S(1)}, f32[80,1,130]{0,2,1:T(8,128)S(1)}, u32[]{:S(2)}, u32[]{:S(2)}) collective-permute-start(f32[80,1,130]{0,2,1:T(8,128)S(1)} %get-tuple-element.38), channel_id=1, source_target_pairs={{0,1},{1,2},{2,3},{3,4},{4,5},{5,6},{6,7},{7,8},{8,9},{9,10},{10,1... | collective-permute-start | bytes 124808 | tf_op jit(solution)/shard_map/ppermute | solution.py:14
  88.1 8.0 %collective-permute-start.15 = (f32[80,1,130]{0,2,1:T(8,128)S(1)}, f32[80,1,130]{0,2,1:T(8,128)S(1)}, u32[]{:S(2)}, u32[]{:S(2)}) collective-permute-start(f32[80,1,130]{0,2,1:T(8,128)S(1)} %get-tuple-element.39), channel_id=1, source_target_pairs={{1,0},{2,1},{3,2},{4,3},{5,4},{6,5},{7,6},{8,7},{9,8},{10,9},{11,1... | collective-permute-start | bytes 124808 | tf_op jit(solution)/shard_map/ppermute | solution.py:17
  107.2 8.1 %collective-permute-start.16 = (f32[80,130]{0,1:T(8,128)S(1)}, f32[80,130]{0,1:T(8,128)S(1)}, u32[]{:S(2)}, u32[]{:S(2)}) collective-permute-start(f32[80,130]{0,1:T(8,128)S(1)} %slice_bitcast_fusion), channel_id=1, source_target_pairs={{0,1},{1,2},{2,3},{3,4},{4,5},{5,6},{6,7},{7,8},{8,9},{9,10},{10,1... | collective-permute-start | bytes 124808 | tf_op jit(solution)/shard_map/ppermute | solution.py:25
  116.8 8.0 %collective-permute-start.17 = (f32[80,32]{0,1:T(8,128)S(1)}, f32[80,32]{0,1:T(8,128)S(1)}, u32[]{:S(2)}, u32[]{:S(2)}) collective-permute-start(f32[80,32]{0,1:T(8,128)S(1)} %bitcast.76), channel_id=1, source_target_pairs={{0,16},{16,32},{32,48},{48,64},{64,80},{80,96},{96,112},{112,128},... | collective-permute-start | bytes 30728 | tf_op jit(solution)/shard_map/ppermute | solution.py:31
  125.9 8.0 %collective-permute-start.19 = (f32[80,32,1]{0,2,1:T(1,128)S(1)}, f32[80,32,1]{0,2,1:T(1,128)S(1)}, u32[]{:S(2)}, u32[]{:S(2)}) collective-permute-start(f32[80,32,1]{0,2,1:T(1,128)S(1)} %slice.351), channel_id=1, source_target_pairs={{0,16},{16,32},{32,48},{48,64},{64,80},{80,96},{96,112},{112,128},... | collective-permute-start | bytes 30728 | tf_op jit(solution)/shard_map/ppermute | solution.py:14
  127.8 7.5 %collective-permute-start.18 = (f32[80,32,1]{0,2,1:T(1,128)S(1)}, f32[80,32,1]{0,2,1:T(1,128)S(1)}, u32[]{:S(2)}, u32[]{:S(2)}) collective-permute-start(f32[80,32,1]{0,2,1:T(1,128)S(1)} %slice_add_fusion.1), channel_id=1, source_target_pairs={{16,0},{32,16},{48,32},{64,48},{80,64},{96,80},{112,96},{128,112},... | collective-permute-start | bytes 30728 | tf_op jit(solution)/shard_map/ppermute | solution.py:17
  137.2 8.0 %collective-permute-start.21 = (f32[80,1,130]{0,2,1:T(8,128)S(1)}, f32[80,1,130]{0,2,1:T(8,128)S(1)}, u32[]{:S(2)}, u32[]{:S(2)}) collective-permute-start(f32[80,1,130]{0,2,1:T(8,128)S(1)} %get-tuple-element.37), channel_id=1, source_target_pairs={{0,1},{1,2},{2,3},{3,4},{4,5},{5,6},{6,7},{7,8},{8,9},{9,10},{10,1... | collective-permute-start | bytes 124808 | tf_op jit(solution)/shard_map/ppermute | solution.py:14
  148.7 8.3 %collective-permute-start.23 = (f32[80,32,1]{0,2,1:T(1,128)S(1)}, f32[80,32,1]{0,2,1:T(1,128)S(1)}, u32[]{:S(2)}, u32[]{:S(2)}) collective-permute-start(f32[80,32,1]{0,2,1:T(1,128)S(1)} %get-tuple-element.44), channel_id=1, source_target_pairs={{0,16},{16,32},{32,48},{48,64},{64,80},{80,96},{96,112},{112,128},... | collective-permute-start | bytes 30728 | tf_op jit(solution)/shard_map/ppermute | solution.py:14
  150.6 7.7 %collective-permute-start.22 = (f32[80,32,1]{0,2,1:T(1,128)S(1)}, f32[80,32,1]{0,2,1:T(1,128)S(1)}, u32[]{:S(2)}, u32[]{:S(2)}) collective-permute-start(f32[80,32,1]{0,2,1:T(1,128)S(1)} %get-tuple-element.45), channel_id=1, source_target_pairs={{16,0},{32,16},{48,32},{64,48},{80,64},{96,80},{112,96},{128,112},... | collective-permute-start | bytes 30728 | tf_op jit(solution)/shard_map/ppermute | solution.py:17
  158.4 5.0 %collective-permute-start.24 = (f32[80,1,130]{0,2,1:T(8,128)S(1)}, f32[80,1,130]{0,2,1:T(8,128)S(1)}, u32[]{:S(2)}, u32[]{:S(2)}) collective-permute-start(f32[80,1,130]{0,2,1:T(8,128)S(1)} %get-tuple-element.34), channel_id=1, source_target_pairs={{1,0},{2,1},{3,2},{4,3},{5,4},{6,5},{7,6},{8,7},{9,8},{10,9},{11,1... | collective-permute-start | bytes 124808 | tf_op jit(solution)/shard_map/ppermute | solution.py:17
  160.3 8.0 %collective-permute-start.25 = (f32[80,1,130]{0,2,1:T(8,128)S(1)}, f32[80,1,130]{0,2,1:T(8,128)S(1)}, u32[]{:S(2)}, u32[]{:S(2)}) collective-permute-start(f32[80,1,130]{0,2,1:T(8,128)S(1)} %get-tuple-element.35), channel_id=1, source_target_pairs={{0,1},{1,2},{2,3},{3,4},{4,5},{5,6},{6,7},{7,8},{8,9},{9,10},{10,1... | collective-permute-start | bytes 124808 | tf_op jit(solution)/shard_map/ppermute | solution.py:14
  (9 other events, 130.6 us)
where the time goes:
time: 175 us; the launch traced here: 174 us
  starting transfers between devices  95.3 us (54%)
  waiting for transfers between devices  40.7 us (23%)
  other arithmetic  21.7 us (12%)
  local copies, waits for them, and re-layouts  13.8 us (8%)
  between operations  1.97 us (1%)
    ppermute x12, starting transfers between devices, with_halo(): lax.ppermute(lax.slice_in_dim(block, 0, width, axis=dim), axis, backward)  65.1 us
    ppermute x12, starting transfers between devices, with_halo(): lax.ppermute(lax.slice_in_dim(block, block.shape[dim] - width, None, axis...  26.4 us
    ppermute x12, waiting for transfers between devices, with_halo(): lax.ppermute(lax.slice_in_dim(block, block.shape[dim] - width, None, axis...  22.2 us
    add x4, other arithmetic, diffuse(): result = result + weight * (window(padded, offset_y, offset_x) - center)  13.8 us
    ppermute x12, waiting for transfers between devices, with_halo(): lax.ppermute(lax.slice_in_dim(block, 0, width, axis=dim), axis, backward)  8.1 us
    ppermute x1, waiting for transfers between devices, shifted(): return lax.ppermute(block, axis, route)  6.16 us
    unnamed x16, local copies, waits for them, and re-layouts  5.01 us
    ppermute x1, waiting for transfers between devices, passed_along(): return lax.ppermute(value, axis, pairs)  4.21 us
  transfers between devices with their start and end apart: 26, of which 12 were waited for; matrix products, arithmetic and copies ran while one was open for 3% of the time, Pallas kernels for 0%

commit v1 on v0

v1 whole, which is shorter than its diff:
```python
import jax
import jax.numpy as jnp
from jax import lax
from jax.sharding import PartitionSpec as P

HN, HS, HW, HE = 3, 4, 3, 4
GN, GS, GW, GE = 2, 3, 2, 3


def neighbour_shift(block, dy, dx):
    n_lon = lax.axis_size("lon")
    n_lat = lax.axis_size("lat")
    if dy == 0:
        pairs = [((i + dx) % n_lon, i) for i in range(n_lon)]
        return lax.ppermute(block, "lon", pairs)
    if dx == 0:
        pairs = [(j + dy, j) for j in range(n_lat) if 0 <= j + dy < n_lat]
        return lax.ppermute(block, "lat", pairs)
    pairs = []
    for i in range(n_lon):
        for j in range(n_lat):
            if 0 <= j + dy < n_lat:
                source = ((i + dx) % n_lon) * n_lat + (j + dy)
                pairs.append((source, i * n_lat + j))
    return lax.ppermute(block, ("lon", "lat"), pairs)


def gather_halo(x, hn, hs, hw, he):
    rows, cols = x.shape[-2:]
    row_part = {-1: slice(rows - hn, rows), 0: slice(0, rows), 1: slice(0, hs)}
    col_part = {-1: slice(cols - hw, cols), 0: slice(0, cols), 1: slice(0, he)}
    grid = []
    for dy in (-1, 0, 1):
        line = []
        for dx in (-1, 0, 1):
            piece = x[..., row_part[dy], col_part[dx]]
            line.append(piece if dy == 0 and dx == 0 else neighbour_shift(piece, dy, dx))
        grid.append(jnp.concatenate(line, axis=-1))
    return jnp.concatenate(grid, axis=-2)


def scatter_halo(g, rows, cols, gn, gs, gw, ge):
    total = g[..., gn : gn + rows, gw : gw + cols]
    row_part = {-1: (slice(0, gn), slice(rows - gn, rows)),
                0: (slice(gn, gn + rows), slice(0, rows)),
                1: (slice(gn + rows, gn + rows + gs), slice(0, gs))}
    col_part = {-1: (slice(0, gw), slice(cols - gw, cols)),
                0: (slice(gw, gw + cols), slice(0, cols)),
                1: (slice(gw + cols, gw + cols + ge), slice(0, ge))}
    for dy in (-1, 0, 1):
        for dx in (-1, 0, 1):
            if dy == 0 and dx == 0:
                continue
            src_r, dst_r = row_part[dy]
            src_c, dst_c = col_part[dx]
            arrived = neighbour_shift(g[..., src_r, src_c], -dy, -dx)
            total = total.at[..., dst_r, dst_c].add(arrived)
    return total


def edge_weights(kappa, mask):
    mid = (slice(1, -1), slice(1, -1))
    kappa_mid = kappa[mid]
    mask_mid = mask[mid]
    out = []
    for oy, ox in ((0, 1), (0, -1), (1, 0), (-1, 0)):
        near = (slice(1 + oy, kappa.shape[0] - 1 + oy), slice(1 + ox, kappa.shape[1] - 1 + ox))
        out.append(0.5 * (kappa_mid + kappa[near]) * mask_mid * mask[near])
    return out


def diffuse(padded, weights):
    center = padded[..., 1:-1, 1:-1]
    result = center
    for (oy, ox), weight in zip(((0, 1), (0, -1), (1, 0), (-1, 0)), weights):
        near = padded[..., 1 + oy : padded.shape[-2] - 1 + oy, 1 + ox : padded.shape[-1] - 1 + ox]
        result = result + weight * (near - center)
    return result


def trim(weights, k):
    return [w[k : w.shape[0] - k, k : w.shape[1] - k] for w in weights]


def pad2(x, k):
    return jnp.pad(x, ((0, 0), (k, k), (k, k)))


def on_device(
    control, diffusivity, land_mask, innovations, obs_sigma, obs_row, obs_col, obs_frac, obs_counts
):
    channels, rows, cols = control.shape
    stacked = jnp.concatenate(
        [control, diffusivity[None], land_mask.astype(jnp.float32)[None]], axis=0
    )
    ext = gather_halo(stacked, HN, HS, HW, HE)
    field = ext[:channels]
    weights = edge_weights(ext[channels], ext[channels + 1])

    state = diffuse(diffuse(field, weights), trim(weights, 1))
    state = state[:, 1 : rows + 2, 1 : cols + 2]

    frac_y = obs_frac[0, 0]
    frac_x = obs_frac[0, 1]
    row_ids = lax.broadcasted_iota(jnp.int32, (rows + 1, obs_row.shape[1]), 0)
    col_ids = lax.broadcasted_iota(jnp.int32, (cols + 1, obs_col.shape[1]), 0)
    base_r = obs_row[0][None]
    base_c = obs_col[0][None]
    wy = jnp.where(row_ids == base_r, 1.0 - frac_y[None], 0.0) + jnp.where(
        row_ids == base_r + 1, frac_y[None], 0.0
    )
    wx = jnp.where(col_ids == base_c, 1.0 - frac_x[None], 0.0) + jnp.where(
        col_ids == base_c + 1, frac_x[None], 0.0
    )
    hi = lax.Precision.HIGHEST
    along = jnp.einsum("zrc,co->zro", state, wx, precision=hi)
    sample = jnp.sum(along * wy[None], axis=1)

    slots = jnp.arange(obs_row.shape[1], dtype=jnp.int32)
    valid = (slots < obs_counts[0, 0]).astype(jnp.float32)
    departure = valid * (sample - innovations[0])
    weighted = departure / (obs_sigma[0] * obs_sigma[0])

    spread = wy[None] * weighted[:, None, :]
    adjoint = jnp.einsum("zro,co->zrc", spread, wx, precision=hi)

    once = diffuse(pad2(adjoint, 2), trim(weights, 1))
    twice = diffuse(pad2(once, 2), weights)
    gradient = scatter_halo(twice, rows, cols, GN, GS, GW, GE)
    return gradient, departure[None]


def solution(mesh):
    in_specs = (
        P(None, "lat", "lon"),
        P("lat", "lon"),
        P("lat", "lon"),
        P("lat", None, "lon"),
        P("lat", None, "lon"),
        P("lat", "lon"),
        P("lat", "lon"),
        P("lat", None, "lon"),
        P("lat", "lon"),
    )
    out_specs = (P(None, "lat", "lon"), P("lat", None, "lon"))
    return jax.shard_map(
        on_device, mesh=mesh, in_specs=in_specs, out_specs=out_specs, check_vma=False
    )
```

time: 175 us -> 129 us (0.74)
  waiting for transfers between devices: 40.7 us -> 4.55 us
  starting transfers between devices: 95.3 us -> 68.8 us
  matrix products: 0 us -> 14 us
  local copies, waits for them, and re-layouts: 13.8 us -> 17.4 us
    ppermute x26 -> x16, waiting for transfers between devices: 40.7 us -> 4.55 us  [the longest x8 4.53 us: neighbour_shift(): return lax.ppermute(block, ('lon', 'lat'), pairs)]
    ppermute x26 -> x16, starting transfers between devices: 95.3 us -> 68.8 us  [the longest x8 42.1 us: neighbour_shift(): return lax.ppermute(block, ('lon', 'lat'), pairs)]
    dot_general x0 -> x2, matrix products: none -> 14 us  [the longest x1 10.7 us: on_device(): along = jnp.einsum('zrc,co->zro', state, wx, precision=hi)]
    slice x7 -> x19, local copies, waits for them, and re-layouts: 2.02 us -> 8.18 us  [the longest x1 4.12 us: on_device(): weights = edge_weights(ext[channels], ext[channels + 1])]
    concatenate x2, other arithmetic: 0.37 us -> 4.85 us  [the longest x1 4.77 us: gather_halo(): return jnp.concatenate(grid, axis=-2)]
    add x5 -> x8, other arithmetic: 14.7 us -> 10.8 us  [the longest x3 10.8 us: diffuse(): result = result + weight * (near - center)]
    reshape x2 -> x0, local copies, waits for them, and re-layouts: 3.85 us -> none  [the longest x1 2.31 us: on_device(): jnp.zeros_like(flat).at[:, offsets.reshape(-1)].add(spread)]
    scatter-add x2 -> x4, other arithmetic: 3.77 us -> 0.17 us  [scatter_halo(): total = total.at[..., dst_r, dst_c].add(arrived)]
  transfers between devices with their start and end apart: 26 -> 16, of which waited for: 12 -> 2; matrix products, arithmetic and copies ran while one was open for 3% -> 5% of each run, Pallas kernels for 0% -> 0%
where the time goes in v1:
time: 129 us
  starting transfers between devices  68.8 us (53%)
  other arithmetic  22.2 us (17%)
  local copies, waits for them, and re-layouts  17.4 us (13%)
  matrix products  14 us (11%)
  waiting for transfers between devices  4.55 us (4%)
  between operations  1.89 us (1%)
    ppermute x8, starting transfers between devices, neighbour_shift(): return lax.ppermute(block, ('lon', 'lat'), pairs)  42.1 us
    ppermute x4, starting transfers between devices, neighbour_shift(): return lax.ppermute(block, 'lon', pairs)  13.8 us
    ppermute x4, starting transfers between devices, neighbour_shift(): return lax.ppermute(block, 'lat', pairs)  13 us
    add x3, other arithmetic, diffuse(): result = result + weight * (near - center)  10.8 us
    dot_general x1, matrix products, on_device(): along = jnp.einsum('zrc,co->zro', state, wx, precision=hi)  10.7 us
    concatenate x1, other arithmetic, gather_halo(): return jnp.concatenate(grid, axis=-2)  4.77 us
    ppermute x8, waiting for transfers between devices, neighbour_shift(): return lax.ppermute(block, ('lon', 'lat'), pairs)  4.53 us
    slice x1, local copies, waits for them, and re-layouts, on_device(): weights = edge_weights(ext[channels], ext[channels + 1])  4.12 us
  transfers between devices with their start and end apart: 16, of which 2 were waited for; matrix products, arithmetic and copies ran while one was open for 5% of the time, Pallas kernels for 0%

profile of v1, /device:TPU:6, one launch (start us, length us, event | category | flops | bytes accessed | tf_op | source)
XLA Modules:
  0.0 128.8 jit_solution(5138079564951819543)
XLA Ops:
  3.9 2.0 %copy.19 = f32[1,32,128]{0,2,1:T(8,128)} copy(f32[1,32,128]{2,1,0:T(8,128)S(1)} %bitcast.38) | data formatting | bytes 32768 | tf_op jit(solution)/shard_map/broadcast_in_dim | solution.py:94
  7.3 4.9 %collective-permute-start.6 = (f32[82,4,128]{0,2,1:T(8,128)S(1)}, f32[82,4,128]{0,2,1:T(8,128)S(1)}, u32[]{:S(2)}, u32[]{:S(2)}) collective-permute-start(f32[82,4,128]{0,2,1:T(8,128)S(1)} %pad_maximum_fusion), channel_id=1, source_target_pairs={{1,0},{2,1},{3,2},{4,3},{5,4},{6,5},{7,6},{8,7},{9,8},{10,9},{11,1... | collective-permute-start | bytes 503816 | tf_op jit(solution)/shard_map/ppermute | solution.py:18
  12.4 1.9 %collective-permute-start.1 = (f32[82,3,128]{0,2,1:T(8,128)S(1)}, f32[82,3,128]{0,2,1:T(8,128)S(1)}, u32[]{:S(2)}, u32[]{:S(2)}) collective-permute-start(f32[82,3,128]{0,2,1:T(8,128)S(1)} %pad_maximum_fusion.1), channel_id=1, source_target_pairs={{0,1},{1,2},{2,3},{3,4},{4,5},{5,6},{6,7},{7,8},{8,9},{9,10},{10,1... | collective-permute-start | bytes 377864 | tf_op jit(solution)/shard_map/ppermute | solution.py:18
  14.4 7.4 %collective-permute-start.5 = (f32[82,4,3]{0,2,1:T(4,128)S(1)}, f32[82,4,3]{0,2,1:T(4,128)S(1)}, u32[]{:S(2)}, u32[]{:S(2)}) collective-permute-start(f32[82,4,3]{0,2,1:T(4,128)S(1)} %pad_maximum_fusion.6), channel_id=1, source_target_pairs={{497,0},{498,1},{499,2},{500,3},{501,4},{502,5},{503,6},{504,7},{5... | collective-permute-start | bytes 11816 | tf_op jit(solution)/shard_map/ppermute | solution.py:25
  23.9 6.7 %collective-permute-start.2 = (f32[82,3,4]{0,2,1:T(4,128)S(1)}, f32[82,3,4]{0,2,1:T(4,128)S(1)}, u32[]{:S(2)}, u32[]{:S(2)}) collective-permute-start(f32[82,3,4]{0,2,1:T(4,128)S(1)} %pad_maximum_fusion.7), channel_id=1, source_target_pairs={{16,1},{17,2},{18,3},{19,4},{20,5},{21,6},{22,7},{23,8},{24,9},{25... | collective-permute-start | bytes 11816 | tf_op jit(solution)/shard_map/ppermute | solution.py:25
  33.7 1.9 %collective-permute-start.3 = (f32[82,32,3]{0,2,1:T(4,128)S(1)}, f32[82,32,3]{0,2,1:T(4,128)S(1)}, u32[]{:S(2)}, u32[]{:S(2)}) collective-permute-start(f32[82,32,3]{0,2,1:T(4,128)S(1)} %pad_maximum_fusion.3), channel_id=1, source_target_pairs={{496,0},{0,16},{16,32},{32,48},{48,64},{64,80},{80,96},{96,112},{1... | collective-permute-start | bytes 94472 | tf_op jit(solution)/shard_map/ppermute | solution.py:15
  35.6 6.0 %collective-permute-start.4 = (f32[82,32,4]{0,2,1:T(4,128)S(1)}, f32[82,32,4]{0,2,1:T(4,128)S(1)}, u32[]{:S(2)}, u32[]{:S(2)}) collective-permute-start(f32[82,32,4]{0,2,1:T(4,128)S(1)} %pad_maximum_fusion.2), channel_id=1, source_target_pairs={{16,0},{32,16},{48,32},{64,48},{80,64},{96,80},{112,96},{128,112},... | collective-permute-start | bytes 125960 | tf_op jit(solution)/shard_map/ppermute | solution.py:15
  41.7 7.1 %collective-permute-start.7 = (f32[82,4,4]{0,2,1:T(4,128)S(1)}, f32[82,4,4]{0,2,1:T(4,128)S(1)}, u32[]{:S(2)}, u32[]{:S(2)}) collective-permute-start(f32[82,4,4]{0,2,1:T(4,128)S(1)} %pad_maximum_fusion.4), channel_id=1, source_target_pairs={{17,0},{18,1},{19,2},{20,3},{21,4},{22,5},{23,6},{24,7},{25,8},{26... | collective-permute-start | bytes 15752 | tf_op jit(solution)/shard_map/ppermute | solution.py:25
  49.9 4.8 %maximum_maximum_fusion = f32[82,39,135]{0,2,1:T(8,128)S(1)} fusion(f32[82,4,4]{0,2,1:T(4,128)S(1)} %collective-permute-done.7, f32[82,4,128]{0,2,1:T(8,128)S(1)} %collective-permute-done.6, f32[82,4,3]{0,2,1:T(4,128)S(1)} %collective-permute-done.5, f32[82,32,4]{0,2,1:T(4,128)S(1)} %collective-permute-done.4, f32[1,32,128]{0,2,1:T(8,128)S(1)} %copy.20, ...), kind=kLoop, calls=%fused_computation.2 | loop fusion | flops 4317300 | bytes 3453840 | tf_op jit(solution)/shard_map/concatenate | solution.py:39
  54.7 4.1 %slice_reduce_fusion.1 = (f32[39,135]{1,0:T(8,128)S(1)}, f32[39,135]{1,0:T(8,128)S(1)}) fusion(f32[82,39,135]{0,2,1:T(8,128)S(1)} %maximum_maximum_fusion), kind=kLoop, calls=%fused_computation.1 | loop fusion | bytes 84240 | tf_op jit(solution)/shard_map/slice | solution.py:98
  59.2 3.4 %fusion.13 = f32[80,37,133]{0,2,1:T(8,128)S(1)} fusion(f32[82,39,135]{0,2,1:T(8,128)S(1)} %maximum_maximum_fusion, f32[37,133]{1,0:T(8,128)S(1)} %get-tuple-element.118, f32[37,133]{1,0:T(8,128)S(1)} %get-tuple-element.116, f32[37,133]{1,0:T(8,128)S(1)} %get-tuple-element.117, f32[37,133]{1,0:T(8,128)S(1)} %get-tuple-element.115), kind=kLoop, calls=%fused_computation.22 | loop fusion | flops 4724160 | bytes 9527056 | tf_op jit(solution)/shard_map/add | solution.py:77
  63.1 3.1 %fusion.86 = (f32[80,35,131]{0,2,1:T(8,128)S(1)}, f32[80,35,131]{0,2,1:T(8,128)S(1)}, f32[80,35,131]{0,2,1:T(8,128)}, f32[80,35,131]{0,2,1:T(8,128)}, f32[80,35,131]{0,2,1:T(8,128)}) fusion(f32[80,37,133]{0,2,1:T(8,128)S(1)} %fusion.13), kind=kLoop, calls=%fused_computation.145 | loop fusion | bytes 14672000 | tf_op jit(solution)/shard_map/slice | solution.py:73
  66.2 10.7 %fusion.51 = f32[80,128]{1,0:T(8,128)S(1)} fusion(f32[80,35,131]{0,2,1:T(8,128)S(1)} %get-tuple-element.111, f32[80,35,131]{0,2,1:T(8,128)} %get-tuple-element.112, f32[80,35,131]{0,2,1:T(8,128)} %get-tuple-element.113, f32[80,35,131]{0,2,1:T(8,128)} %get-tuple-element.114, f32[80,35,131]{0,2,1:T(8,128)S(1)} %get-tuple-element.110, ...), kind=kOutput, calls=%fused_computation.66 | convolution fusion | flops 527935040 | bytes 11716608 | tf_op jit(solution)/shard_map/zrc,co->zro/dot_general | solution.py:116
  77.0 3.3 %fusion.49 = f32[80,33,129]{0,2,1:T(8,128)S(1)} fusion(f32[80,128]{1,0:T(8,128)S(1)} %bitcast_divide_fusion, f32[33,128]{1,0:T(8,128)S(1)} %select_add_fusion.3, f32[128]{0:T(128)S(1)} %get-tuple-element.121, s32[128]{0:T(128)S(1)} %add_bitcast_fusion, f32[128]{0:T(128)S(1)} %get-tuple-element.119, s32[128]{0:T(128)S(1)} %bitcast.41), kind=kOutput, calls=%fused_computation.64 | convolution fusion | flops 523520640 | bytes 1422144 | tf_op jit(solution)/shard_map/zro,co->zrc/dot_general | solution.py:125
  80.3 3.2 %fusion.25 = f32[80,35,131]{0,2,1:T(8,128)S(1)} fusion(f32[80,33,129]{0,2,1:T(8,128)S(1)} %fusion.49, f32[35,131]{1,0:T(8,128)S(1)} %slice.485, f32[35,131]{1,0:T(8,128)S(1)} %slice.483, f32[35,131]{1,0:T(8,128)S(1)} %slice.481, f32[35,131]{1,0:T(8,128)S(1)} %slice.479), kind=kLoop, calls=%fused_computation.42 | loop fusion | flops 4401600 | bytes 2902800 | tf_op jit(solution)/shard_map/add | solution.py:77
  83.5 4.1 %fusion.5 = f32[80,37,133]{0,2,1:T(8,128)S(1)} fusion(f32[80,35,131]{0,2,1:T(8,128)S(1)} %fusion.25, f32[37,133]{1,0:T(8,128)S(1)} %get-tuple-element.118, f32[37,133]{1,0:T(8,128)S(1)} %get-tuple-element.116, f32[37,133]{1,0:T(8,128)S(1)} %get-tuple-element.117, f32[37,133]{1,0:T(8,128)S(1)} %get-tuple-element.115), kind=kLoop, calls=%fused_computation.13 | loop fusion | flops 4724160 | bytes 3120656 | tf_op jit(solution)/shard_map/add | solution.py:77
  87.6 7.8 %collective-permute-start.8 = (f32[80,2,2]{0,2,1:T(2,128)S(1)}, f32[80,2,2]{0,2,1:T(2,128)S(1)}, u32[]{:S(2)}, u32[]{:S(2)}) collective-permute-start(f32[80,2,2]{0,2,1:T(2,128)S(1)} %slice.498), channel_id=1, source_target_pairs={{17,0},{18,1},{19,2},{20,3},{21,4},{22,5},{23,6},{24,7},{25,8},{26... | collective-permute-start | bytes 3848 | tf_op jit(solution)/shard_map/ppermute | solution.py:25
  96.5 1.9 %collective-permute-start.9 = (f32[80,2,128]{0,2,1:T(8,128)S(1)}, f32[80,2,128]{0,2,1:T(8,128)S(1)}, u32[]{:S(2)}, u32[]{:S(2)}) collective-permute-start(f32[80,2,128]{0,2,1:T(8,128)S(1)} %slice.500), channel_id=1, source_target_pairs={{1,0},{2,1},{3,2},{4,3},{5,4},{6,5},{7,6},{8,7},{9,8},{10,9},{11,1... | collective-permute-start | bytes 245768 | tf_op jit(solution)/shard_map/ppermute | solution.py:18
  98.4 1.9 %collective-permute-start.10 = (f32[80,2,3]{0,2,1:T(4,128)S(1)}, f32[80,2,3]{0,2,1:T(4,128)S(1)}, u32[]{:S(2)}, u32[]{:S(2)}) collective-permute-start(f32[80,2,3]{0,2,1:T(4,128)S(1)} %slice.502), channel_id=1, source_target_pairs={{497,0},{498,1},{499,2},{500,3},{501,4},{502,5},{503,6},{504,7},{5... | collective-permute-start | bytes 5768 | tf_op jit(solution)/shard_map/ppermute | solution.py:25
  100.4 3.6 %collective-permute-start.11 = (f32[80,32,2]{0,2,1:T(2,128)S(1)}, f32[80,32,2]{0,2,1:T(2,128)S(1)}, u32[]{:S(2)}, u32[]{:S(2)}) collective-permute-start(f32[80,32,2]{0,2,1:T(2,128)S(1)} %slice.504), channel_id=1, source_target_pairs={{16,0},{32,16},{48,32},{64,48},{80,64},{96,80},{112,96},{128,112},... | collective-permute-start | bytes 61448 | tf_op jit(solution)/shard_map/ppermute | solution.py:15
  104.0 2.3 %collective-permute-start.12 = (f32[80,32,3]{0,2,1:T(4,128)S(1)}, f32[80,32,3]{0,2,1:T(4,128)S(1)}, u32[]{:S(2)}, u32[]{:S(2)}) collective-permute-start(f32[80,32,3]{0,2,1:T(4,128)S(1)} %slice.506), channel_id=1, source_target_pairs={{496,0},{0,16},{16,32},{32,48},{48,64},{64,80},{80,96},{96,112},{1... | collective-permute-start | bytes 92168 | tf_op jit(solution)/shard_map/ppermute | solution.py:15
  106.2 7.3 %collective-permute-start.13 = (f32[80,3,2]{0,2,1:T(2,128)S(1)}, f32[80,3,2]{0,2,1:T(2,128)S(1)}, u32[]{:S(2)}, u32[]{:S(2)}) collective-permute-start(f32[80,3,2]{0,2,1:T(2,128)S(1)} %slice.507), channel_id=1, source_target_pairs={{16,1},{17,2},{18,3},{19,4},{20,5},{21,6},{22,7},{23,8},{24,9},{25... | collective-permute-start | bytes 5768 | tf_op jit(solution)/shard_map/ppermute | solution.py:25
  113.6 4.2 %collective-permute-start.14 = (f32[80,3,128]{0,2,1:T(8,128)S(1)}, f32[80,3,128]{0,2,1:T(8,128)S(1)}, u32[]{:S(2)}, u32[]{:S(2)}) collective-permute-start(f32[80,3,128]{0,2,1:T(8,128)S(1)} %slice.509), channel_id=1, source_target_pairs={{0,1},{1,2},{2,3},{3,4},{4,5},{5,6},{6,7},{7,8},{8,9},{9,10},{10,1... | collective-permute-start | bytes 368648 | tf_op jit(solution)/shard_map/ppermute | solution.py:18
  123.6 3.4 %collective-permute-done.15 = f32[80,3,3]{0,2,1:T(4,128)S(1)} collective-permute-done((f32[80,3,3]{0,2,1:T(4,128)S(1)}, f32[80,3,3]{0,2,1:T(4,128)S(1)}, u32[]{:S(2)}, u32[]{:S(2)}) %collective-permute-start.15) | collective-permute-done | bytes 2912 | tf_op jit(solution)/shard_map/ppermute | solution.py:25
  (90 shorter events, 19.9 us)
Async XLA Ops:
  0.6 1.5 %copy-start.2 = (f32[80,32,128]{2,1,0:T(8,128)S(1)}, f32[80,32,128]{2,1,0:T(8,128)}, u32[]{:S(2)}) copy-start(f32[80,32,128]{2,1,0:T(8,128)} %param.25) | copy-start | bytes 3932164
  1.5 2.4 %copy-start.5 = (f32[32,128]{1,0:T(8,128)S(1)}, f32[32,128]{1,0:T(8,128)}, u32[]{:S(2)}) copy-start(f32[32,128]{1,0:T(8,128)} %param.26) | copy-start | bytes 49156
  5.9 6.3 %copy-start = (f32[80,32,128]{0,2,1:T(8,128)S(1)}, f32[80,32,128]{0,2,1:T(8,128)}, u32[]{:S(2)}) copy-start(f32[80,32,128]{0,2,1:T(8,128)} %copy.18) | copy-start | bytes 3932164
  5.9 6.3 %copy-start.1 = (f32[1,32,128]{0,2,1:T(8,128)S(1)}, f32[1,32,128]{0,2,1:T(8,128)}, u32[]{:S(2)}) copy-start(f32[1,32,128]{0,2,1:T(8,128)} %copy.19) | copy-start | bytes 49156
  7.3 42.7 %collective-permute-start.6 = (f32[82,4,128]{0,2,1:T(8,128)S(1)}, f32[82,4,128]{0,2,1:T(8,128)S(1)}, u32[]{:S(2)}, u32[]{:S(2)}) collective-permute-start(f32[82,4,128]{0,2,1:T(8,128)S(1)} %pad_maximum_fusion), channel_id=1, source_target_pairs={{1,0},{2,1},{3,2},{4,3},{5,4},{6,5},{7,6},{8,7},{9,8},{10,9},{11,1... | collective-permute-start | bytes 503816 | tf_op jit(solution)/shard_map/ppermute | solution.py:18
  12.4 37.5 %collective-permute-start.1 = (f32[82,3,128]{0,2,1:T(8,128)S(1)}, f32[82,3,128]{0,2,1:T(8,128)S(1)}, u32[]{:S(2)}, u32[]{:S(2)}) collective-permute-start(f32[82,3,128]{0,2,1:T(8,128)S(1)} %pad_maximum_fusion.1), channel_id=1, source_target_pairs={{0,1},{1,2},{2,3},{3,4},{4,5},{5,6},{6,7},{7,8},{8,9},{9,10},{10,1... | collective-permute-start | bytes 377864 | tf_op jit(solution)/shard_map/ppermute | solution.py:18
  14.4 21.2 %collective-permute-start.5 = (f32[82,4,3]{0,2,1:T(4,128)S(1)}, f32[82,4,3]{0,2,1:T(4,128)S(1)}, u32[]{:S(2)}, u32[]{:S(2)}) collective-permute-start(f32[82,4,3]{0,2,1:T(4,128)S(1)} %pad_maximum_fusion.6), channel_id=1, source_target_pairs={{497,0},{498,1},{499,2},{500,3},{501,4},{502,5},{503,6},{504,7},{5... | collective-permute-start | bytes 11816 | tf_op jit(solution)/shard_map/ppermute | solution.py:25
  21.9 11.8 %collective-permute-start = (f32[82,3,3]{0,2,1:T(4,128)S(1)}, f32[82,3,3]{0,2,1:T(4,128)S(1)}, u32[]{:S(2)}, u32[]{:S(2)}) collective-permute-start(f32[82,3,3]{0,2,1:T(4,128)S(1)} %pad_maximum_fusion.8), channel_id=1, source_target_pairs={{496,1},{497,2},{498,3},{499,4},{500,5},{501,6},{502,7},{503,8},{5... | collective-permute-start | bytes 8864 | tf_op jit(solution)/shard_map/ppermute | solution.py:25
  23.9 17.8 %collective-permute-start.2 = (f32[82,3,4]{0,2,1:T(4,128)S(1)}, f32[82,3,4]{0,2,1:T(4,128)S(1)}, u32[]{:S(2)}, u32[]{:S(2)}) collective-permute-start(f32[82,3,4]{0,2,1:T(4,128)S(1)} %pad_maximum_fusion.7), channel_id=1, source_target_pairs={{16,1},{17,2},{18,3},{19,4},{20,5},{21,6},{22,7},{23,8},{24,9},{25... | collective-permute-start | bytes 11816 | tf_op jit(solution)/shard_map/ppermute | solution.py:25
  30.9 0.7 copy-start.9
  30.9 0.7 copy-start.8
  33.7 16.2 %collective-permute-start.3 = (f32[82,32,3]{0,2,1:T(4,128)S(1)}, f32[82,32,3]{0,2,1:T(4,128)S(1)}, u32[]{:S(2)}, u32[]{:S(2)}) collective-permute-start(f32[82,32,3]{0,2,1:T(4,128)S(1)} %pad_maximum_fusion.3), channel_id=1, source_target_pairs={{496,0},{0,16},{16,32},{32,48},{48,64},{64,80},{80,96},{96,112},{1... | collective-permute-start | bytes 94472 | tf_op jit(solution)/shard_map/ppermute | solution.py:15
  35.6 14.3 %collective-permute-start.4 = (f32[82,32,4]{0,2,1:T(4,128)S(1)}, f32[82,32,4]{0,2,1:T(4,128)S(1)}, u32[]{:S(2)}, u32[]{:S(2)}) collective-permute-start(f32[82,32,4]{0,2,1:T(4,128)S(1)} %pad_maximum_fusion.2), channel_id=1, source_target_pairs={{16,0},{32,16},{48,32},{64,48},{80,64},{96,80},{112,96},{128,112},... | collective-permute-start | bytes 125960 | tf_op jit(solution)/shard_map/ppermute | solution.py:15
  41.7 8.2 %collective-permute-start.7 = (f32[82,4,4]{0,2,1:T(4,128)S(1)}, f32[82,4,4]{0,2,1:T(4,128)S(1)}, u32[]{:S(2)}, u32[]{:S(2)}) collective-permute-start(f32[82,4,4]{0,2,1:T(4,128)S(1)} %pad_maximum_fusion.4), channel_id=1, source_target_pairs={{17,0},{18,1},{19,2},{20,3},{21,4},{22,5},{23,6},{24,7},{25,8},{26... | collective-permute-start | bytes 15752 | tf_op jit(solution)/shard_map/ppermute | solution.py:25
  66.2 10.7 %copy-start.3 = (f32[1,80,128]{2,1,0:T(8,128)S(1)}, f32[1,80,128]{2,1,0:T(8,128)}, u32[]{:S(2)}) copy-start(f32[1,80,128]{2,1,0:T(8,128)} %param.28) | copy-start | bytes 122884
  66.2 10.8 %copy-start.4 = (f32[1,80,128]{2,1,0:T(8,128)S(1)}, f32[1,80,128]{2,1,0:T(8,128)}, u32[]{:S(2)}) copy-start(f32[1,80,128]{2,1,0:T(8,128)} %param.29) | copy-start | bytes 122884
  87.6 18.6 %collective-permute-start.8 = (f32[80,2,2]{0,2,1:T(2,128)S(1)}, f32[80,2,2]{0,2,1:T(2,128)S(1)}, u32[]{:S(2)}, u32[]{:S(2)}) collective-permute-start(f32[80,2,2]{0,2,1:T(2,128)S(1)} %slice.498), channel_id=1, source_target_pairs={{17,0},{18,1},{19,2},{20,3},{21,4},{22,5},{23,6},{24,7},{25,8},{26... | collective-permute-start | bytes 3848 | tf_op jit(solution)/shard_map/ppermute | solution.py:25
  96.5 17.1 %collective-permute-start.9 = (f32[80,2,128]{0,2,1:T(8,128)S(1)}, f32[80,2,128]{0,2,1:T(8,128)S(1)}, u32[]{:S(2)}, u32[]{:S(2)}) collective-permute-start(f32[80,2,128]{0,2,1:T(8,128)S(1)} %slice.500), channel_id=1, source_target_pairs={{1,0},{2,1},{3,2},{4,3},{5,4},{6,5},{7,6},{8,7},{9,8},{10,9},{11,1... | collective-permute-start | bytes 245768 | tf_op jit(solution)/shard_map/ppermute | solution.py:18
  98.4 19.4 %collective-permute-start.10 = (f32[80,2,3]{0,2,1:T(4,128)S(1)}, f32[80,2,3]{0,2,1:T(4,128)S(1)}, u32[]{:S(2)}, u32[]{:S(2)}) collective-permute-start(f32[80,2,3]{0,2,1:T(4,128)S(1)} %slice.502), channel_id=1, source_target_pairs={{497,0},{498,1},{499,2},{500,3},{501,4},{502,5},{503,6},{504,7},{5... | collective-permute-start | bytes 5768 | tf_op jit(solution)/shard_map/ppermute | solution.py:25
  100.4 19.5 %collective-permute-start.11 = (f32[80,32,2]{0,2,1:T(2,128)S(1)}, f32[80,32,2]{0,2,1:T(2,128)S(1)}, u32[]{:S(2)}, u32[]{:S(2)}) collective-permute-start(f32[80,32,2]{0,2,1:T(2,128)S(1)} %slice.504), channel_id=1, source_target_pairs={{16,0},{32,16},{48,32},{64,48},{80,64},{96,80},{112,96},{128,112},... | collective-permute-start | bytes 61448 | tf_op jit(solution)/shard_map/ppermute | solution.py:15
  104.0 16.0 %collective-permute-start.12 = (f32[80,32,3]{0,2,1:T(4,128)S(1)}, f32[80,32,3]{0,2,1:T(4,128)S(1)}, u32[]{:S(2)}, u32[]{:S(2)}) collective-permute-start(f32[80,32,3]{0,2,1:T(4,128)S(1)} %slice.506), channel_id=1, source_target_pairs={{496,0},{0,16},{16,32},{32,48},{48,64},{64,80},{80,96},{96,112},{1... | collective-permute-start | bytes 92168 | tf_op jit(solution)/shard_map/ppermute | solution.py:15
  106.2 14.0 %collective-permute-start.13 = (f32[80,3,2]{0,2,1:T(2,128)S(1)}, f32[80,3,2]{0,2,1:T(2,128)S(1)}, u32[]{:S(2)}, u32[]{:S(2)}) collective-permute-start(f32[80,3,2]{0,2,1:T(2,128)S(1)} %slice.507), channel_id=1, source_target_pairs={{16,1},{17,2},{18,3},{19,4},{20,5},{21,6},{22,7},{23,8},{24,9},{25... | collective-permute-start | bytes 5768 | tf_op jit(solution)/shard_map/ppermute | solution.py:25
  113.6 10.0 %collective-permute-start.14 = (f32[80,3,128]{0,2,1:T(8,128)S(1)}, f32[80,3,128]{0,2,1:T(8,128)S(1)}, u32[]{:S(2)}, u32[]{:S(2)}) collective-permute-start(f32[80,3,128]{0,2,1:T(8,128)S(1)} %slice.509), channel_id=1, source_target_pairs={{0,1},{1,2},{2,3},{3,4},{4,5},{5,6},{6,7},{7,8},{8,9},{9,10},{10,1... | collective-permute-start | bytes 368648 | tf_op jit(solution)/shard_map/ppermute | solution.py:18
  117.8 9.2 %collective-permute-start.15 = (f32[80,3,3]{0,2,1:T(4,128)S(1)}, f32[80,3,3]{0,2,1:T(4,128)S(1)}, u32[]{:S(2)}, u32[]{:S(2)}) collective-permute-start(f32[80,3,3]{0,2,1:T(4,128)S(1)} %slice.511), channel_id=1, source_target_pairs={{496,1},{497,2},{498,3},{499,4},{500,5},{501,6},{502,7},{503,8},{5... | collective-permute-start | bytes 8648 | tf_op jit(solution)/shard_map/ppermute | solution.py:25
  (2 other events, 1.4 us)

commit v2 on v1

--- a/solution.py
+++ b/solution.py
@@ -27,34 +27,25 @@
 
 def gather_halo(x, hn, hs, hw, he):
     rows, cols = x.shape[-2:]
-    row_part = {-1: slice(rows - hn, rows), 0: slice(0, rows), 1: slice(0, hs)}
-    col_part = {-1: slice(cols - hw, cols), 0: slice(0, cols), 1: slice(0, he)}
-    grid = []
-    for dy in (-1, 0, 1):
-        line = []
-        for dx in (-1, 0, 1):
-            piece = x[..., row_part[dy], col_part[dx]]
-            line.append(piece if dy == 0 and dx == 0 else neighbour_shift(piece, dy, dx))
-        grid.append(jnp.concatenate(line, axis=-1))
-    return jnp.concatenate(grid, axis=-2)
+    west = neighbour_shift(x[..., :, cols - hw :], 0, -1)
+    east = neighbour_shift(x[..., :, :he], 0, 1)
+    x = jnp.concatenate([west, x, east], axis=-1)
+    north = neighbour_shift(x[..., rows - hn :, :], -1, 0)
+    south = neighbour_shift(x[..., :hs, :], 1, 0)
+    return jnp.concatenate([north, x, south], axis=-2)
 
 
 def scatter_halo(g, rows, cols, gn, gs, gw, ge):
-    total = g[..., gn : gn + rows, gw : gw + cols]
-    row_part = {-1: (slice(0, gn), slice(rows - gn, rows)),
-                0: (slice(gn, gn + rows), slice(0, rows)),
-                1: (slice(gn + rows, gn + rows + gs), slice(0, gs))}
-    col_part = {-1: (slice(0, gw), slice(cols - gw, cols)),
-                0: (slice(gw, gw + cols), slice(0, cols)),
-                1: (slice(gw + cols, gw + cols + ge), slice(0, ge))}
-    for dy in (-1, 0, 1):
-        for dx in (-1, 0, 1):
-            if dy == 0 and dx == 0:
-                continue
-            src_r, dst_r = row_part[dy]
-            src_c, dst_c = col_part[dx]
-            arrived = neighbour_shift(g[..., src_r, src_c], -dy, -dx)
-            total = total.at[..., dst_r, dst_c].add(arrived)
+    h = g[..., gn : gn + rows, :]
+    from_south = neighbour_shift(g[..., :gn, :], 1, 0)
+    from_north = neighbour_shift(g[..., gn + rows :, :], -1, 0)
+    h = h.at[..., rows - gn :, :].add(from_south)
+    h = h.at[..., :gs, :].add(from_north)
+    total = h[..., :, gw : gw + cols]
+    from_east = neighbour_shift(h[..., :, :gw], 0, 1)
+    from_west = neighbour_shift(h[..., :, gw + cols :], 0, -1)
+    total = total.at[..., :, cols - gw :].add(from_east)
+    total = total.at[..., :, :ge].add(from_west)
     return total
 
 

time: 129 us -> 105 us (0.81)
  starting transfers between devices: 68.8 us -> 39.2 us
  waiting for transfers between devices: 4.55 us -> 19 us
  other arithmetic: 22.2 us -> 15.8 us
  local copies, waits for them, and re-layouts: 17.4 us -> 14.7 us
    ppermute x8 -> x0, starting transfers between devices: 42.1 us -> none  [neighbour_shift(): return lax.ppermute(block, ('lon', 'lat'), pairs)]
    ppermute x4, waiting for transfers between devices: 0.01 us -> 10.9 us  [neighbour_shift(): return lax.ppermute(block, 'lat', pairs)]
    ppermute x4, starting transfers between devices: 13.8 us -> 23.1 us  [neighbour_shift(): return lax.ppermute(block, 'lon', pairs)]
    ppermute x4, waiting for transfers between devices: 0.01 us -> 8.11 us  [neighbour_shift(): return lax.ppermute(block, 'lon', pairs)]
    ppermute x8 -> x0, waiting for transfers between devices: 4.53 us -> none  [neighbour_shift(): return lax.ppermute(block, ('lon', 'lat'), pairs)]
    concatenate x1 -> x2, other arithmetic: 4.77 us -> 1.54 us  [the longest x1 1.32 us: gather_halo(): return jnp.concatenate([north, x, south], axis=-2)]
    ppermute x4, starting transfers between devices: 13 us -> 16.1 us  [neighbour_shift(): return lax.ppermute(block, 'lat', pairs)]
    another operation x3 -> x0, other arithmetic: 2.67 us -> none
  transfers between devices with their start and end apart: 16 -> 8, of which waited for: 2 -> 7; matrix products, arithmetic and copies ran while one was open for 5% -> 1% of each run, Pallas kernels for 0% -> 0%
where the time goes in v2:
time: 105 us; the launch traced here: 104 us
  starting transfers between devices  39.2 us (37%)
  waiting for transfers between devices  19 us (18%)
  other arithmetic  15.8 us (15%)
  local copies, waits for them, and re-layouts  14.7 us (14%)
  matrix products  13.8 us (13%)
  between operations  1.67 us (2%)
    ppermute x4, starting transfers between devices, neighbour_shift(): return lax.ppermute(block, 'lon', pairs)  23.1 us
    ppermute x4, starting transfers between devices, neighbour_shift(): return lax.ppermute(block, 'lat', pairs)  16.1 us
    ppermute x4, waiting for transfers between devices, neighbour_shift(): return lax.ppermute(block, 'lat', pairs)  10.9 us
    add x3, other arithmetic, diffuse(): result = result + weight * (near - center)  10.9 us
    dot_general x1, matrix products, on_device(): along = jnp.einsum('zrc,co->zro', state, wx, precision=hi)  10.5 us
    ppermute x4, waiting for transfers between devices, neighbour_shift(): return lax.ppermute(block, 'lon', pairs)  8.11 us
    slice x1, local copies, waits for them, and re-layouts, on_device(): weights = edge_weights(ext[channels], ext[channels + 1])  4.12 us
    unnamed x20, local copies, waits for them, and re-layouts  3.57 us
  transfers between devices with their start and end apart: 8, of which 7 were waited for; matrix products, arithmetic and copies ran while one was open for 1% of the time, Pallas kernels for 0%

profile of v2, /device:TPU:6, one launch (start us, length us, event | category | flops | bytes accessed | tf_op | source)
XLA Modules:
  0.0 104.2 jit_solution(12495980554345864616)
XLA Ops:
  2.1 1.8 %copy.18 = f32[80,32,128]{0,2,1:T(8,128)} copy(f32[80,32,128]{2,1,0:T(8,128)S(1)} %copy-done.2) | data formatting | bytes 2621440 | tf_op args[0]
  3.9 2.0 %copy.19 = f32[1,32,128]{0,2,1:T(8,128)} copy(f32[1,32,128]{2,1,0:T(8,128)S(1)} %bitcast.36) | data formatting | bytes 32768 | tf_op jit(solution)/shard_map/broadcast_in_dim | solution.py:85
  5.9 1.3 %pad_maximum_fusion.8 = f32[82,32,3]{0,2,1:T(4,128)S(1)} fusion(f32[1,32,128]{0,2,1:T(8,128)S(1)} %copy.20, f32[1,32,128]{0,2,1:T(8,128)} %copy.19, f32[80,32,128]{0,2,1:T(8,128)} %copy.18), kind=kLoop, calls=%fused_computation.90 | loop fusion | flops 15744 | bytes 1374976 | tf_op jit(solution)/shard_map/slice | solution.py:30
  7.2 4.0 %collective-permute-start = (f32[82,32,3]{0,2,1:T(4,128)S(1)}, f32[82,32,3]{0,2,1:T(4,128)S(1)}, u32[]{:S(2)}, u32[]{:S(2)}) collective-permute-start(f32[82,32,3]{0,2,1:T(4,128)S(1)} %pad_maximum_fusion.8), channel_id=1, source_target_pairs={{496,0},{0,16},{16,32},{32,48},{48,64},{64,80},{80,96},{96,112},{1... | collective-permute-start | bytes 94472 | tf_op jit(solution)/shard_map/ppermute | solution.py:15
  11.3 10.5 %collective-permute-start.1 = (f32[82,32,4]{0,2,1:T(4,128)S(1)}, f32[82,32,4]{0,2,1:T(4,128)S(1)}, u32[]{:S(2)}, u32[]{:S(2)}) collective-permute-start(f32[82,32,4]{0,2,1:T(4,128)S(1)} %pad_maximum_fusion.6), channel_id=1, source_target_pairs={{16,0},{32,16},{48,32},{64,48},{80,64},{96,80},{112,96},{128,112},... | collective-permute-start | bytes 125960 | tf_op jit(solution)/shard_map/ppermute | solution.py:15
  22.0 1.8 %collective-permute-done.1 = f32[82,32,4]{0,2,1:T(4,128)S(1)} collective-permute-done((f32[82,32,4]{0,2,1:T(4,128)S(1)}, f32[82,32,4]{0,2,1:T(4,128)S(1)}, u32[]{:S(2)}, u32[]{:S(2)}) %collective-permute-start.1) | collective-permute-done | bytes 42016 | tf_op jit(solution)/shard_map/ppermute | solution.py:15
  23.9 1.9 %collective-permute-start.2 = (f32[82,3,135]{0,2,1:T(8,128)S(1)}, f32[82,3,135]{0,2,1:T(8,128)S(1)}, u32[]{:S(2)}, u32[]{:S(2)}) collective-permute-start(f32[82,3,135]{0,2,1:T(8,128)S(1)} %pad_maximum_fusion.5), channel_id=1, source_target_pairs={{0,1},{1,2},{2,3},{3,4},{4,5},{5,6},{6,7},{7,8},{8,9},{9,10},{10,1... | collective-permute-start | bytes 398528 | tf_op jit(solution)/shard_map/ppermute | solution.py:18
  26.1 6.0 %collective-permute-start.3 = (f32[82,4,135]{0,2,1:T(8,128)S(1)}, f32[82,4,135]{0,2,1:T(8,128)S(1)}, u32[]{:S(2)}, u32[]{:S(2)}) collective-permute-start(f32[82,4,135]{0,2,1:T(8,128)S(1)} %pad_maximum_fusion.1), channel_id=1, source_target_pairs={{1,0},{2,1},{3,2},{4,3},{5,4},{6,5},{7,6},{8,7},{9,8},{10,9},{11,1... | collective-permute-start | bytes 531368 | tf_op jit(solution)/shard_map/ppermute | solution.py:18
  33.4 2.7 %collective-permute-done.3 = f32[82,4,135]{0,2,1:T(8,128)S(1)} collective-permute-done((f32[82,4,135]{0,2,1:T(8,128)S(1)}, f32[82,4,135]{0,2,1:T(8,128)S(1)}, u32[]{:S(2)}, u32[]{:S(2)}) %collective-permute-start.3) | collective-permute-done | bytes 177152 | tf_op jit(solution)/shard_map/ppermute | solution.py:18
  36.2 1.3 %pad_maximum_fusion = f32[82,39,135]{0,2,1:T(8,128)S(1)} fusion(f32[82,4,135]{0,2,1:T(8,128)S(1)} %collective-permute-done.3, f32[82,32,4]{0,2,1:T(4,128)S(1)} %collective-permute-done.1, f32[1,32,128]{0,2,1:T(8,128)S(1)} %copy.20, f32[1,32,128]{0,2,1:T(8,128)S(1)} %copy-done.1, f32[80,32,128]{0,2,1:T(8,128)S(1)} %copy-done, ...), kind=kLoop, calls=%fused_computation.2 | loop fusion | flops 2590380 | bytes 3453840 | tf_op jit(solution)/shard_map/concatenate | solution.py:35
  37.5 4.1 %slice_reduce_fusion.1 = (f32[39,135]{1,0:T(8,128)S(1)}, f32[39,135]{1,0:T(8,128)S(1)}) fusion(f32[82,39,135]{0,2,1:T(8,128)S(1)} %pad_maximum_fusion), kind=kLoop, calls=%fused_computation.1 | loop fusion | bytes 84240 | tf_op jit(solution)/shard_map/slice | solution.py:89
  42.0 3.6 %fusion.13 = f32[80,37,133]{0,2,1:T(8,128)S(1)} fusion(f32[82,39,135]{0,2,1:T(8,128)S(1)} %pad_maximum_fusion, f32[37,133]{1,0:T(8,128)S(1)} %get-tuple-element.66, f32[37,133]{1,0:T(8,128)S(1)} %get-tuple-element.64, f32[37,133]{1,0:T(8,128)S(1)} %get-tuple-element.65, f32[37,133]{1,0:T(8,128)S(1)} %get-tuple-element.63), kind=kLoop, calls=%fused_computation.22 | loop fusion | flops 4724160 | bytes 9527056 | tf_op jit(solution)/shard_map/add | solution.py:68
  46.0 3.1 %fusion.87 = (f32[80,35,131]{0,2,1:T(8,128)S(1)}, f32[80,35,131]{0,2,1:T(8,128)S(1)}, f32[80,35,131]{0,2,1:T(8,128)}, f32[80,35,131]{0,2,1:T(8,128)}, f32[80,35,131]{0,2,1:T(8,128)}) fusion(f32[80,37,133]{0,2,1:T(8,128)S(1)} %fusion.13), kind=kLoop, calls=%fused_computation.137 | loop fusion | bytes 14672000 | tf_op jit(solution)/shard_map/slice | solution.py:64
  49.1 10.5 %fusion.51 = f32[80,128]{1,0:T(8,128)S(1)} fusion(f32[80,35,131]{0,2,1:T(8,128)S(1)} %get-tuple-element.59, f32[80,35,131]{0,2,1:T(8,128)} %get-tuple-element.60, f32[80,35,131]{0,2,1:T(8,128)} %get-tuple-element.61, f32[80,35,131]{0,2,1:T(8,128)} %get-tuple-element.62, f32[80,35,131]{0,2,1:T(8,128)S(1)} %get-tuple-element.58, f32[33,129]{1,0:T(8,128)S(1)} %slice.342, ...), kind=kOutput, calls=%fused_computation.66 | convolution fusion | flops 527935040 | bytes 11716608 | tf_op jit(solution)/shard_map/zrc,co->zro/dot_general | solution.py:107
  59.7 3.3 %fusion.49 = f32[80,33,129]{0,2,1:T(8,128)S(1)} fusion(f32[80,128]{1,0:T(8,128)S(1)} %bitcast_divide_fusion, f32[33,128]{1,0:T(8,128)S(1)} %select_add_fusion.3, f32[128]{0:T(128)S(1)} %get-tuple-element.69, s32[128]{0:T(128)S(1)} %add_bitcast_fusion, f32[128]{0:T(128)S(1)} %get-tuple-element.67, s32[128]{0:T(128)S(1)} %bitcast.39), kind=kOutput, calls=%fused_computation.64 | convolution fusion | flops 523520640 | bytes 1422144 | tf_op jit(solution)/shard_map/zro,co->zrc/dot_general | solution.py:116
  63.0 3.2 %fusion.25 = f32[80,35,131]{0,2,1:T(8,128)S(1)} fusion(f32[80,33,129]{0,2,1:T(8,128)S(1)} %fusion.49, f32[35,131]{1,0:T(8,128)S(1)} %slice.332, f32[35,131]{1,0:T(8,128)S(1)} %slice.330, f32[35,131]{1,0:T(8,128)S(1)} %slice.328, f32[35,131]{1,0:T(8,128)S(1)} %slice.326), kind=kLoop, calls=%fused_computation.42 | loop fusion | flops 4401600 | bytes 2902800 | tf_op jit(solution)/shard_map/add | solution.py:68
  66.2 4.1 %fusion.5 = f32[80,37,133]{0,2,1:T(8,128)S(1)} fusion(f32[80,35,131]{0,2,1:T(8,128)S(1)} %fusion.25, f32[37,133]{1,0:T(8,128)S(1)} %get-tuple-element.66, f32[37,133]{1,0:T(8,128)S(1)} %get-tuple-element.64, f32[37,133]{1,0:T(8,128)S(1)} %get-tuple-element.65, f32[37,133]{1,0:T(8,128)S(1)} %get-tuple-element.63), kind=kLoop, calls=%fused_computation.13 | loop fusion | flops 4724160 | bytes 3120656 | tf_op jit(solution)/shard_map/add | solution.py:68
  70.4 6.2 %collective-permute-start.4 = (f32[80,2,133]{0,2,1:T(8,128)S(1)}, f32[80,2,133]{0,2,1:T(8,128)S(1)}, u32[]{:S(2)}, u32[]{:S(2)}) collective-permute-start(f32[80,2,133]{0,2,1:T(8,128)S(1)} %slice.345), channel_id=1, source_target_pairs={{1,0},{2,1},{3,2},{4,3},{5,4},{6,5},{7,6},{8,7},{9,8},{10,9},{11,1... | collective-permute-start | bytes 255368 | tf_op jit(solution)/shard_map/ppermute | solution.py:18
  76.8 1.9 %collective-permute-start.5 = (f32[80,3,133]{0,2,1:T(8,128)S(1)}, f32[80,3,133]{0,2,1:T(8,128)S(1)}, u32[]{:S(2)}, u32[]{:S(2)}) collective-permute-start(f32[80,3,133]{0,2,1:T(8,128)S(1)} %slice.347), channel_id=1, source_target_pairs={{0,1},{1,2},{2,3},{3,4},{4,5},{5,6},{6,7},{7,8},{8,9},{9,10},{10,1... | collective-permute-start | bytes 383048 | tf_op jit(solution)/shard_map/ppermute | solution.py:18
  79.2 7.1 %collective-permute-done.5 = f32[80,3,133]{0,2,1:T(8,128)S(1)} collective-permute-done((f32[80,3,133]{0,2,1:T(8,128)S(1)}, f32[80,3,133]{0,2,1:T(8,128)S(1)}, u32[]{:S(2)}, u32[]{:S(2)}) %collective-permute-start.5) | collective-permute-done | bytes 127712 | tf_op jit(solution)/shard_map/ppermute | solution.py:18
  86.4 6.7 %collective-permute-start.6 = (f32[80,32,2]{0,2,1:T(2,128)S(1)}, f32[80,32,2]{0,2,1:T(2,128)S(1)}, u32[]{:S(2)}, u32[]{:S(2)}) collective-permute-start(f32[80,32,2]{0,2,1:T(2,128)S(1)} %slice.350), channel_id=1, source_target_pairs={{16,0},{32,16},{48,32},{64,48},{80,64},{96,80},{112,96},{128,112},... | collective-permute-start | bytes 61448 | tf_op jit(solution)/shard_map/ppermute | solution.py:15
  93.9 1.9 %collective-permute-start.7 = (f32[80,32,3]{0,2,1:T(4,128)S(1)}, f32[80,32,3]{0,2,1:T(4,128)S(1)}, u32[]{:S(2)}, u32[]{:S(2)}) collective-permute-start(f32[80,32,3]{0,2,1:T(4,128)S(1)} %slice.352), channel_id=1, source_target_pairs={{496,0},{0,16},{16,32},{32,48},{48,64},{64,80},{80,96},{96,112},{1... | collective-permute-start | bytes 92168 | tf_op jit(solution)/shard_map/ppermute | solution.py:15
  95.9 6.3 %collective-permute-done.7 = f32[80,32,3]{0,2,1:T(4,128)S(1)} collective-permute-done((f32[80,32,3]{0,2,1:T(4,128)S(1)}, f32[80,32,3]{0,2,1:T(4,128)S(1)}, u32[]{:S(2)}, u32[]{:S(2)}) %collective-permute-start.7) | collective-permute-done | bytes 30752 | tf_op jit(solution)/shard_map/ppermute | solution.py:15
  102.5 1.7 %copy.21 = f32[80,32,128]{2,1,0:T(8,128)} copy(f32[80,32,128]{0,2,1:T(8,128)S(1)} %scatter-add.19) | data formatting | bytes 2621440
  (55 shorter events, 5.5 us)
Async XLA Ops:
  0.6 1.5 %copy-start.2 = (f32[80,32,128]{2,1,0:T(8,128)S(1)}, f32[80,32,128]{2,1,0:T(8,128)}, u32[]{:S(2)}) copy-start(f32[80,32,128]{2,1,0:T(8,128)} %param.17) | copy-start | bytes 3932164
  1.5 2.5 %copy-start.5 = (f32[32,128]{1,0:T(8,128)S(1)}, f32[32,128]{1,0:T(8,128)}, u32[]{:S(2)}) copy-start(f32[32,128]{1,0:T(8,128)} %param.18) | copy-start | bytes 49156
  5.9 5.3 %copy-start = (f32[80,32,128]{0,2,1:T(8,128)S(1)}, f32[80,32,128]{0,2,1:T(8,128)}, u32[]{:S(2)}) copy-start(f32[80,32,128]{0,2,1:T(8,128)} %copy.18) | copy-start | bytes 3932164
  5.9 5.3 %copy-start.1 = (f32[1,32,128]{0,2,1:T(8,128)S(1)}, f32[1,32,128]{0,2,1:T(8,128)}, u32[]{:S(2)}) copy-start(f32[1,32,128]{0,2,1:T(8,128)} %copy.19) | copy-start | bytes 49156
  7.2 14.7 %copy-start.6 = (f32[1,2,128]{2,1,0:T(2,128)S(1)}, f32[1,2,128]{2,1,0:T(2,128)}, u32[]{:S(2)}) copy-start(f32[1,2,128]{2,1,0:T(2,128)} %param.24) | copy-start | bytes 3076
  7.2 14.7 %copy-start.7 = (s32[1,128]{1,0:T(1,128)S(1)}, s32[1,128]{1,0:T(1,128)}, u32[]{:S(2)}) copy-start(s32[1,128]{1,0:T(1,128)} %param.22) | copy-start | bytes 1540
  7.2 14.8 %collective-permute-start = (f32[82,32,3]{0,2,1:T(4,128)S(1)}, f32[82,32,3]{0,2,1:T(4,128)S(1)}, u32[]{:S(2)}, u32[]{:S(2)}) collective-permute-start(f32[82,32,3]{0,2,1:T(4,128)S(1)} %pad_maximum_fusion.8), channel_id=1, source_target_pairs={{496,0},{0,16},{16,32},{32,48},{48,64},{64,80},{80,96},{96,112},{1... | collective-permute-start | bytes 94472 | tf_op jit(solution)/shard_map/ppermute | solution.py:15
  11.3 12.4 %collective-permute-start.1 = (f32[82,32,4]{0,2,1:T(4,128)S(1)}, f32[82,32,4]{0,2,1:T(4,128)S(1)}, u32[]{:S(2)}, u32[]{:S(2)}) collective-permute-start(f32[82,32,4]{0,2,1:T(4,128)S(1)} %pad_maximum_fusion.6), channel_id=1, source_target_pairs={{16,0},{32,16},{48,32},{64,48},{80,64},{96,80},{112,96},{128,112},... | collective-permute-start | bytes 125960 | tf_op jit(solution)/shard_map/ppermute | solution.py:15
  23.9 8.2 %copy-start.8 = (s32[1,128]{1,0:T(1,128)S(1)}, s32[1,128]{1,0:T(1,128)}, u32[]{:S(2)}) copy-start(s32[1,128]{1,0:T(1,128)} %param.23) | copy-start | bytes 1540
  23.9 9.5 %collective-permute-start.2 = (f32[82,3,135]{0,2,1:T(8,128)S(1)}, f32[82,3,135]{0,2,1:T(8,128)S(1)}, u32[]{:S(2)}, u32[]{:S(2)}) collective-permute-start(f32[82,3,135]{0,2,1:T(8,128)S(1)} %pad_maximum_fusion.5), channel_id=1, source_target_pairs={{0,1},{1,2},{2,3},{3,4},{4,5},{5,6},{6,7},{7,8},{8,9},{9,10},{10,1... | collective-permute-start | bytes 398528 | tf_op jit(solution)/shard_map/ppermute | solution.py:18
  26.1 10.1 %collective-permute-start.3 = (f32[82,4,135]{0,2,1:T(8,128)S(1)}, f32[82,4,135]{0,2,1:T(8,128)S(1)}, u32[]{:S(2)}, u32[]{:S(2)}) collective-permute-start(f32[82,4,135]{0,2,1:T(8,128)S(1)} %pad_maximum_fusion.1), channel_id=1, source_target_pairs={{1,0},{2,1},{3,2},{4,3},{5,4},{6,5},{7,6},{8,7},{9,8},{10,9},{11,1... | collective-permute-start | bytes 531368 | tf_op jit(solution)/shard_map/ppermute | solution.py:18
  49.1 10.5 %copy-start.3 = (f32[1,80,128]{2,1,0:T(8,128)S(1)}, f32[1,80,128]{2,1,0:T(8,128)}, u32[]{:S(2)}) copy-start(f32[1,80,128]{2,1,0:T(8,128)} %param.20) | copy-start | bytes 122884
  49.1 10.5 %copy-start.4 = (f32[1,80,128]{2,1,0:T(8,128)S(1)}, f32[1,80,128]{2,1,0:T(8,128)}, u32[]{:S(2)}) copy-start(f32[1,80,128]{2,1,0:T(8,128)} %param.21) | copy-start | bytes 122884
  70.4 8.8 %collective-permute-start.4 = (f32[80,2,133]{0,2,1:T(8,128)S(1)}, f32[80,2,133]{0,2,1:T(8,128)S(1)}, u32[]{:S(2)}, u32[]{:S(2)}) collective-permute-start(f32[80,2,133]{0,2,1:T(8,128)S(1)} %slice.345), channel_id=1, source_target_pairs={{1,0},{2,1},{3,2},{4,3},{5,4},{6,5},{7,6},{8,7},{9,8},{10,9},{11,1... | collective-permute-start | bytes 255368 | tf_op jit(solution)/shard_map/ppermute | solution.py:18
  76.8 9.5 %collective-permute-start.5 = (f32[80,3,133]{0,2,1:T(8,128)S(1)}, f32[80,3,133]{0,2,1:T(8,128)S(1)}, u32[]{:S(2)}, u32[]{:S(2)}) collective-permute-start(f32[80,3,133]{0,2,1:T(8,128)S(1)} %slice.347), channel_id=1, source_target_pairs={{0,1},{1,2},{2,3},{3,4},{4,5},{5,6},{6,7},{7,8},{8,9},{9,10},{10,1... | collective-permute-start | bytes 383048 | tf_op jit(solution)/shard_map/ppermute | solution.py:18
  86.4 9.5 %collective-permute-start.6 = (f32[80,32,2]{0,2,1:T(2,128)S(1)}, f32[80,32,2]{0,2,1:T(2,128)S(1)}, u32[]{:S(2)}, u32[]{:S(2)}) collective-permute-start(f32[80,32,2]{0,2,1:T(2,128)S(1)} %slice.350), channel_id=1, source_target_pairs={{16,0},{32,16},{48,32},{64,48},{80,64},{96,80},{112,96},{128,112},... | collective-permute-start | bytes 61448 | tf_op jit(solution)/shard_map/ppermute | solution.py:15
  93.9 8.3 %collective-permute-start.7 = (f32[80,32,3]{0,2,1:T(4,128)S(1)}, f32[80,32,3]{0,2,1:T(4,128)S(1)}, u32[]{:S(2)}, u32[]{:S(2)}) collective-permute-start(f32[80,32,3]{0,2,1:T(4,128)S(1)} %slice.352), channel_id=1, source_target_pairs={{496,0},{0,16},{16,32},{32,48},{48,64},{64,80},{80,96},{96,112},{1... | collective-permute-start | bytes 92168 | tf_op jit(solution)/shard_map/ppermute | solution.py:15

commit v3 on v2

--- a/solution.py
+++ b/solution.py
@@ -25,14 +25,20 @@
     return lax.ppermute(block, ("lon", "lat"), pairs)
 
 
-def gather_halo(x, hn, hs, hw, he):
+def gather_halo(x, split, hn, hs, hw, he):
     rows, cols = x.shape[-2:]
     west = neighbour_shift(x[..., :, cols - hw :], 0, -1)
     east = neighbour_shift(x[..., :, :he], 0, 1)
-    x = jnp.concatenate([west, x, east], axis=-1)
-    north = neighbour_shift(x[..., rows - hn :, :], -1, 0)
-    south = neighbour_shift(x[..., :hs, :], 1, 0)
-    return jnp.concatenate([north, x, south], axis=-2)
+    edge_n = jnp.concatenate([west[..., rows - hn :, :], x[..., rows - hn :, :], east[..., rows - hn :, :]], axis=-1)
+    edge_s = jnp.concatenate([west[..., :hs, :], x[..., :hs, :], east[..., :hs, :]], axis=-1)
+    north = neighbour_shift(edge_n, -1, 0)
+    south = neighbour_shift(edge_s, 1, 0)
+
+    def assemble(part):
+        middle = jnp.concatenate([west[part], x[part], east[part]], axis=-1)
+        return jnp.concatenate([north[part], middle, south[part]], axis=-2)
+
+    return assemble(slice(0, split)), assemble(slice(split, None))
 
 
 def scatter_halo(g, rows, cols, gn, gs, gw, ge):
@@ -84,12 +90,12 @@
     stacked = jnp.concatenate(
         [control, diffusivity[None], land_mask.astype(jnp.float32)[None]], axis=0
     )
-    ext = gather_halo(stacked, HN, HS, HW, HE)
-    field = ext[:channels]
-    weights = edge_weights(ext[channels], ext[channels + 1])
+    field, coeff = gather_halo(stacked, channels, HN, HS, HW, HE)
+    weights = edge_weights(coeff[0], coeff[1])
 
     state = diffuse(diffuse(field, weights), trim(weights, 1))
     state = state[:, 1 : rows + 2, 1 : cols + 2]
+    state = lax.optimization_barrier(state)
 
     frac_y = obs_frac[0, 0]
     frac_x = obs_frac[0, 1]
@@ -114,6 +120,7 @@
 
     spread = wy[None] * weighted[:, None, :]
     adjoint = jnp.einsum("zro,co->zrc", spread, wx, precision=hi)
+    adjoint = lax.optimization_barrier(adjoint)
 
     once = diffuse(pad2(adjoint, 2), trim(weights, 1))
     twice = diffuse(pad2(once, 2), weights)

time: 105 us -> 101 us (0.962)
  matrix products: 13.8 us -> 8.95 us
  other arithmetic: 15.8 us -> 20.3 us
  local copies, waits for them, and re-layouts: 14.7 us -> 13 us
  waiting for transfers between devices: 19 us -> 17.9 us
    add x3 -> x4, other arithmetic: 10.9 us -> 16.3 us  [diffuse(): result = result + weight * (near - center)]
    dot_general x1, matrix products: 10.5 us -> 5.65 us  [on_device(): along = jnp.einsum('zrc,co->zro', state, wx, precision=hi)]
    slice x1 -> x12, local copies, waits for them, and re-layouts: 4.12 us -> 1.45 us  [the longest x4 0.82 us: assemble(): middle = jnp.concatenate([west[part], x[part], east[part]], axis=-1)]
    broadcast_in_dim x1, local copies, waits for them, and re-layouts: 0.64 us -> 1.99 us  [on_device(): land_mask.astype(jnp.float32)[None]]
    ppermute x4, waiting for transfers between devices: 10.9 us -> 9.79 us  [neighbour_shift(): return lax.ppermute(block, 'lat', pairs)]
    unnamed x20 -> x22, local copies, waits for them, and re-layouts: 3.57 us -> 2.58 us
  transfers between devices with their start and end apart: 8 -> 8, of which waited for: 7 -> 6; matrix products, arithmetic and copies ran while one was open for 1% -> 3% of each run, Pallas kernels for 0% -> 0%
where the time goes in v3:
time: 101 us
  starting transfers between devices  39.2 us (39%)
  other arithmetic  20.3 us (20%)
  waiting for transfers between devices  17.9 us (18%)
  local copies, waits for them, and re-layouts  13 us (13%)
  matrix products  8.95 us (9%)
  between operations  1.73 us (2%)
    ppermute x4, starting transfers between devices, neighbour_shift(): return lax.ppermute(block, 'lon', pairs)  23.1 us
    add x4, other arithmetic, diffuse(): result = result + weight * (near - center)  16.3 us
    ppermute x4, starting transfers between devices, neighbour_shift(): return lax.ppermute(block, 'lat', pairs)  16.1 us
    ppermute x4, waiting for transfers between devices, neighbour_shift(): return lax.ppermute(block, 'lat', pairs)  9.79 us
    ppermute x4, waiting for transfers between devices, neighbour_shift(): return lax.ppermute(block, 'lon', pairs)  8.1 us
    dot_general x1, matrix products, on_device(): along = jnp.einsum('zrc,co->zro', state, wx, precision=hi)  5.65 us
    dot_general x1, matrix products, on_device(): adjoint = jnp.einsum('zro,co->zrc', spread, wx, precision=hi)  3.3 us
    slice x1, local copies, waits for them, and re-layouts, diffuse(): center = padded[..., 1:-1, 1:-1]  3.09 us
  transfers between devices with their start and end apart: 8, of which 6 were waited for; matrix products, arithmetic and copies ran while one was open for 3% of the time, Pallas kernels for 0%

profile of v3, /device:TPU:6, one launch (start us, length us, event | category | flops | bytes accessed | tf_op | source)
XLA Modules:
  0.0 101.0 jit_solution(3756836425428903648)
XLA Ops:
  0.6 0.8 convert_bitcast_fusion
  1.5 2.0 %copy.17 = f32[1,32,128]{0,2,1:T(8,128)} copy(f32[1,32,128]{2,1,0:T(8,128)S(1)} %convert_bitcast_fusion) | data formatting | bytes 32768 | tf_op jit(solution)/shard_map/broadcast_in_dim | solution.py:91
  4.3 2.0 %copy.16 = f32[1,32,128]{0,2,1:T(8,128)} copy(f32[1,32,128]{2,1,0:T(8,128)S(1)} %bitcast.49) | data formatting | bytes 32768 | tf_op jit(solution)/shard_map/broadcast_in_dim | solution.py:91
  6.2 1.3 %pad_maximum_fusion.7 = f32[82,32,3]{0,2,1:T(4,128)S(1)} fusion(f32[1,32,128]{0,2,1:T(8,128)} %copy.17, f32[1,32,128]{0,2,1:T(8,128)} %copy.16, f32[80,32,128]{0,2,1:T(8,128)S(1)} %copy.15), kind=kLoop, calls=%fused_computation.85 | loop fusion | flops 15744 | bytes 1374976 | tf_op jit(solution)/shard_map/slice | solution.py:30
  7.5 4.0 %collective-permute-start = (f32[82,32,3]{0,2,1:T(4,128)S(1)}, f32[82,32,3]{0,2,1:T(4,128)S(1)}, u32[]{:S(2)}, u32[]{:S(2)}) collective-permute-start(f32[82,32,3]{0,2,1:T(4,128)S(1)} %pad_maximum_fusion.7), channel_id=1, source_target_pairs={{496,0},{0,16},{16,32},{32,48},{48,64},{64,80},{80,96},{96,112},{1... | collective-permute-start | bytes 94472 | tf_op jit(solution)/shard_map/ppermute | solution.py:15
  11.7 10.5 %collective-permute-start.1 = (f32[82,32,4]{0,2,1:T(4,128)S(1)}, f32[82,32,4]{0,2,1:T(4,128)S(1)}, u32[]{:S(2)}, u32[]{:S(2)}) collective-permute-start(f32[82,32,4]{0,2,1:T(4,128)S(1)} %pad_maximum_fusion.6), channel_id=1, source_target_pairs={{16,0},{32,16},{48,32},{64,48},{80,64},{96,80},{112,96},{128,112},... | collective-permute-start | bytes 125960 | tf_op jit(solution)/shard_map/ppermute | solution.py:15
  22.3 1.8 %collective-permute-done.1 = f32[82,32,4]{0,2,1:T(4,128)S(1)} collective-permute-done((f32[82,32,4]{0,2,1:T(4,128)S(1)}, f32[82,32,4]{0,2,1:T(4,128)S(1)}, u32[]{:S(2)}, u32[]{:S(2)}) %collective-permute-start.1) | collective-permute-done | bytes 42016 | tf_op jit(solution)/shard_map/ppermute | solution.py:15
  24.2 1.9 %collective-permute-start.2 = (f32[82,3,135]{0,2,1:T(8,128)S(1)}, f32[82,3,135]{0,2,1:T(8,128)S(1)}, u32[]{:S(2)}, u32[]{:S(2)}) collective-permute-start(f32[82,3,135]{0,2,1:T(8,128)S(1)} %fusion.49), channel_id=1, source_target_pairs={{0,1},{1,2},{2,3},{3,4},{4,5},{5,6},{6,7},{7,8},{8,9},{9,10},{10,1... | collective-permute-start | bytes 398528 | tf_op jit(solution)/shard_map/ppermute | solution.py:18
  26.4 6.0 %collective-permute-start.3 = (f32[82,4,135]{0,2,1:T(8,128)S(1)}, f32[82,4,135]{0,2,1:T(8,128)S(1)}, u32[]{:S(2)}, u32[]{:S(2)}) collective-permute-start(f32[82,4,135]{0,2,1:T(8,128)S(1)} %fusion.46), channel_id=1, source_target_pairs={{1,0},{2,1},{3,2},{4,3},{5,4},{6,5},{7,6},{8,7},{9,8},{10,9},{11,1... | collective-permute-start | bytes 531368 | tf_op jit(solution)/shard_map/ppermute | solution.py:18
  34.3 2.2 %collective-permute-done.3 = f32[82,4,135]{0,2,1:T(8,128)S(1)} collective-permute-done((f32[82,4,135]{0,2,1:T(8,128)S(1)}, f32[82,4,135]{0,2,1:T(8,128)S(1)}, u32[]{:S(2)}, u32[]{:S(2)}) %collective-permute-start.3) | collective-permute-done | bytes 177152 | tf_op jit(solution)/shard_map/ppermute | solution.py:18
  38.7 3.6 %fusion.13 = f32[80,37,133]{0,2,1:T(8,128)S(1)} fusion(f32[80,39,135]{0,2,1:T(8,128)S(1)} %pad_maximum_fusion, f32[37,133]{1,0:T(8,128)S(1)} %get-tuple-element.62, f32[37,133]{1,0:T(8,128)S(1)} %get-tuple-element.60, f32[37,133]{1,0:T(8,128)S(1)} %get-tuple-element.61, f32[37,133]{1,0:T(8,128)S(1)} %get-tuple-element.59), kind=kLoop, calls=%fused_computation.20 | loop fusion | flops 4724160 | bytes 9527056 | tf_op jit(solution)/shard_map/add | solution.py:74
  42.4 3.1 %fusion.76 = (f32[80,35,131]{0,2,1:T(8,128)S(1)}, f32[80,35,131]{0,2,1:T(8,128)S(1)}, f32[80,35,131]{0,2,1:T(8,128)}, f32[80,35,131]{0,2,1:T(8,128)}, f32[80,35,131]{0,2,1:T(8,128)}) fusion(f32[80,37,133]{0,2,1:T(8,128)S(1)} %fusion.13), kind=kLoop, calls=%fused_computation.134 | loop fusion | bytes 14672000 | tf_op jit(solution)/shard_map/slice | solution.py:70
  45.5 5.1 %fusion.33 = f32[80,33,129]{0,2,1:T(8,128)S(1)} fusion(f32[80,35,131]{0,2,1:T(8,128)S(1)} %get-tuple-element.55, f32[80,35,131]{0,2,1:T(8,128)} %get-tuple-element.56, f32[80,35,131]{0,2,1:T(8,128)} %get-tuple-element.57, f32[80,35,131]{0,2,1:T(8,128)} %get-tuple-element.58, f32[80,35,131]{0,2,1:T(8,128)S(1)} %get-tuple-element.54, ...), kind=kLoop, calls=%fused_computation.49 | loop fusion | flops 4086720 | bytes 8241552 | tf_op jit(solution)/shard_map/add | solution.py:74
  50.6 5.6 %fusion.42 = f32[80,128]{1,0:T(8,128)S(1)} fusion(f32[80,33,129]{0,2,1:T(8,128)S(1)} %fusion.33, f32[33,128]{1,0:T(8,128)S(1)} %select_add_fusion.3, f32[128]{0:T(128)S(1)} %get-tuple-element.67, s32[128]{0:T(128)S(1)} %add_bitcast_fusion, f32[128]{0:T(128)S(1)} %get-tuple-element.65, s32[128]{0:T(128)S(1)} %bitcast.51), kind=kOutput, calls=%fused_computation.62 | convolution fusion | flops 523848320 | bytes 1422144 | tf_op jit(solution)/shard_map/zrc,co->zro/dot_general | solution.py:113
  56.3 3.3 %fusion.40 = f32[80,33,129]{0,2,1:T(8,128)S(1)} fusion(f32[80,128]{1,0:T(8,128)S(1)} %bitcast_divide_fusion, f32[33,128]{1,0:T(8,128)S(1)} %select_add_fusion.3, f32[128]{0:T(128)S(1)} %get-tuple-element.67, s32[128]{0:T(128)S(1)} %add_bitcast_fusion, f32[128]{0:T(128)S(1)} %get-tuple-element.65, s32[128]{0:T(128)S(1)} %bitcast.52), kind=kOutput, calls=%fused_computation.60 | convolution fusion | flops 523520640 | bytes 1422144 | tf_op jit(solution)/shard_map/zro,co->zrc/dot_general | solution.py:122
  59.6 3.2 %fusion.25 = f32[80,35,131]{0,2,1:T(8,128)S(1)} fusion(f32[80,33,129]{0,2,1:T(8,128)S(1)} %fusion.40, f32[35,131]{1,0:T(8,128)S(1)} %slice.388, f32[35,131]{1,0:T(8,128)S(1)} %slice.386, f32[35,131]{1,0:T(8,128)S(1)} %slice.384, f32[35,131]{1,0:T(8,128)S(1)} %slice.382), kind=kLoop, calls=%fused_computation.40 | loop fusion | flops 4401600 | bytes 2902800 | tf_op jit(solution)/shard_map/add | solution.py:74
  62.8 4.3 %fusion.5 = f32[80,37,133]{0,2,1:T(8,128)S(1)} fusion(f32[80,35,131]{0,2,1:T(8,128)S(1)} %fusion.25, f32[37,133]{1,0:T(8,128)S(1)} %get-tuple-element.62, f32[37,133]{1,0:T(8,128)S(1)} %get-tuple-element.60, f32[37,133]{1,0:T(8,128)S(1)} %get-tuple-element.61, f32[37,133]{1,0:T(8,128)S(1)} %get-tuple-element.59), kind=kLoop, calls=%fused_computation.11 | loop fusion | flops 4724160 | bytes 3120656 | tf_op jit(solution)/shard_map/add | solution.py:74
  67.2 6.2 %collective-permute-start.4 = (f32[80,2,133]{0,2,1:T(8,128)S(1)}, f32[80,2,133]{0,2,1:T(8,128)S(1)}, u32[]{:S(2)}, u32[]{:S(2)}) collective-permute-start(f32[80,2,133]{0,2,1:T(8,128)S(1)} %slice.401), channel_id=1, source_target_pairs={{1,0},{2,1},{3,2},{4,3},{5,4},{6,5},{7,6},{8,7},{9,8},{10,9},{11,1... | collective-permute-start | bytes 255368 | tf_op jit(solution)/shard_map/ppermute | solution.py:18
  73.6 1.9 %collective-permute-start.5 = (f32[80,3,133]{0,2,1:T(8,128)S(1)}, f32[80,3,133]{0,2,1:T(8,128)S(1)}, u32[]{:S(2)}, u32[]{:S(2)}) collective-permute-start(f32[80,3,133]{0,2,1:T(8,128)S(1)} %slice.403), channel_id=1, source_target_pairs={{0,1},{1,2},{2,3},{3,4},{4,5},{5,6},{6,7},{7,8},{8,9},{9,10},{10,1... | collective-permute-start | bytes 383048 | tf_op jit(solution)/shard_map/ppermute | solution.py:18
  76.0 7.1 %collective-permute-done.5 = f32[80,3,133]{0,2,1:T(8,128)S(1)} collective-permute-done((f32[80,3,133]{0,2,1:T(8,128)S(1)}, f32[80,3,133]{0,2,1:T(8,128)S(1)}, u32[]{:S(2)}, u32[]{:S(2)}) %collective-permute-start.5) | collective-permute-done | bytes 127712 | tf_op jit(solution)/shard_map/ppermute | solution.py:18
  83.2 6.7 %collective-permute-start.6 = (f32[80,32,2]{0,2,1:T(2,128)S(1)}, f32[80,32,2]{0,2,1:T(2,128)S(1)}, u32[]{:S(2)}, u32[]{:S(2)}) collective-permute-start(f32[80,32,2]{0,2,1:T(2,128)S(1)} %slice.406), channel_id=1, source_target_pairs={{16,0},{32,16},{48,32},{64,48},{80,64},{96,80},{112,96},{128,112},... | collective-permute-start | bytes 61448 | tf_op jit(solution)/shard_map/ppermute | solution.py:15
  90.7 1.9 %collective-permute-start.7 = (f32[80,32,3]{0,2,1:T(4,128)S(1)}, f32[80,32,3]{0,2,1:T(4,128)S(1)}, u32[]{:S(2)}, u32[]{:S(2)}) collective-permute-start(f32[80,32,3]{0,2,1:T(4,128)S(1)} %slice.408), channel_id=1, source_target_pairs={{496,0},{0,16},{16,32},{32,48},{48,64},{64,80},{80,96},{96,112},{1... | collective-permute-start | bytes 92168 | tf_op jit(solution)/shard_map/ppermute | solution.py:15
  92.7 6.3 %collective-permute-done.7 = f32[80,32,3]{0,2,1:T(4,128)S(1)} collective-permute-done((f32[80,32,3]{0,2,1:T(4,128)S(1)}, f32[80,32,3]{0,2,1:T(4,128)S(1)}, u32[]{:S(2)}, u32[]{:S(2)}) %collective-permute-start.7) | collective-permute-done | bytes 30752 | tf_op jit(solution)/shard_map/ppermute | solution.py:15
  99.3 1.7 %copy.23 = f32[80,32,128]{2,1,0:T(8,128)} copy(f32[80,32,128]{0,2,1:T(8,128)S(1)} %scatter-add.19) | data formatting | bytes 2621440
  (71 shorter events, 6.7 us)
Async XLA Ops:
  0.6 2.8 %copy-start.2 = (f32[80,32,128]{2,1,0:T(8,128)S(1)}, f32[80,32,128]{2,1,0:T(8,128)}, u32[]{:S(2)}) copy-start(f32[80,32,128]{2,1,0:T(8,128)} %param.17) | copy-start | bytes 3932164
  1.5 2.8 %copy-start.5 = (f32[32,128]{1,0:T(8,128)S(1)}, f32[32,128]{1,0:T(8,128)}, u32[]{:S(2)}) copy-start(f32[32,128]{1,0:T(8,128)} %param.18) | copy-start | bytes 49156
  6.2 5.3 %copy-start = (f32[1,32,128]{0,2,1:T(8,128)S(1)}, f32[1,32,128]{0,2,1:T(8,128)}, u32[]{:S(2)}) copy-start(f32[1,32,128]{0,2,1:T(8,128)} %copy.17) | copy-start | bytes 49156
  6.2 5.3 %copy-start.1 = (f32[1,32,128]{0,2,1:T(8,128)S(1)}, f32[1,32,128]{0,2,1:T(8,128)}, u32[]{:S(2)}) copy-start(f32[1,32,128]{0,2,1:T(8,128)} %copy.16) | copy-start | bytes 49156
  7.5 14.7 %copy-start.7 = (f32[1,2,128]{2,1,0:T(2,128)S(1)}, f32[1,2,128]{2,1,0:T(2,128)}, u32[]{:S(2)}) copy-start(f32[1,2,128]{2,1,0:T(2,128)} %param.24) | copy-start | bytes 3076
  7.5 14.7 %copy-start.9 = (s32[1,128]{1,0:T(1,128)S(1)}, s32[1,128]{1,0:T(1,128)}, u32[]{:S(2)}) copy-start(s32[1,128]{1,0:T(1,128)} %param.22) | copy-start | bytes 1540
  7.5 14.8 %collective-permute-start = (f32[82,32,3]{0,2,1:T(4,128)S(1)}, f32[82,32,3]{0,2,1:T(4,128)S(1)}, u32[]{:S(2)}, u32[]{:S(2)}) collective-permute-start(f32[82,32,3]{0,2,1:T(4,128)S(1)} %pad_maximum_fusion.7), channel_id=1, source_target_pairs={{496,0},{0,16},{16,32},{32,48},{48,64},{64,80},{80,96},{96,112},{1... | collective-permute-start | bytes 94472 | tf_op jit(solution)/shard_map/ppermute | solution.py:15
  11.7 12.4 %collective-permute-start.1 = (f32[82,32,4]{0,2,1:T(4,128)S(1)}, f32[82,32,4]{0,2,1:T(4,128)S(1)}, u32[]{:S(2)}, u32[]{:S(2)}) collective-permute-start(f32[82,32,4]{0,2,1:T(4,128)S(1)} %pad_maximum_fusion.6), channel_id=1, source_target_pairs={{16,0},{32,16},{48,32},{64,48},{80,64},{96,80},{112,96},{128,112},... | collective-permute-start | bytes 125960 | tf_op jit(solution)/shard_map/ppermute | solution.py:15
  24.2 9.7 %collective-permute-start.2 = (f32[82,3,135]{0,2,1:T(8,128)S(1)}, f32[82,3,135]{0,2,1:T(8,128)S(1)}, u32[]{:S(2)}, u32[]{:S(2)}) collective-permute-start(f32[82,3,135]{0,2,1:T(8,128)S(1)} %fusion.49), channel_id=1, source_target_pairs={{0,1},{1,2},{2,3},{3,4},{4,5},{5,6},{6,7},{7,8},{8,9},{9,10},{10,1... | collective-permute-start | bytes 398528 | tf_op jit(solution)/shard_map/ppermute | solution.py:18
  26.2 6.3 %copy-start.8 = (s32[1,128]{1,0:T(1,128)S(1)}, s32[1,128]{1,0:T(1,128)}, u32[]{:S(2)}) copy-start(s32[1,128]{1,0:T(1,128)} %param.23) | copy-start | bytes 1540
  26.4 10.1 %collective-permute-start.3 = (f32[82,4,135]{0,2,1:T(8,128)S(1)}, f32[82,4,135]{0,2,1:T(8,128)S(1)}, u32[]{:S(2)}, u32[]{:S(2)}) collective-permute-start(f32[82,4,135]{0,2,1:T(8,128)S(1)} %fusion.46), channel_id=1, source_target_pairs={{1,0},{2,1},{3,2},{4,3},{5,4},{6,5},{7,6},{8,7},{9,8},{10,9},{11,1... | collective-permute-start | bytes 531368 | tf_op jit(solution)/shard_map/ppermute | solution.py:18
  42.4 3.1 %copy-start.3 = (f32[33,129]{1,0:T(8,128)S(1)}, f32[33,129]{1,0:T(8,128)}, u32[]{:S(2)}) copy-start(f32[33,129]{1,0:T(8,128)} %slice.398) | copy-start | bytes 51088
  45.5 10.8 %copy-start.4 = (f32[1,80,128]{2,1,0:T(8,128)S(1)}, f32[1,80,128]{2,1,0:T(8,128)}, u32[]{:S(2)}) copy-start(f32[1,80,128]{2,1,0:T(8,128)} %param.20) | copy-start | bytes 122884
  45.5 10.8 %copy-start.6 = (f32[1,80,128]{2,1,0:T(8,128)S(1)}, f32[1,80,128]{2,1,0:T(8,128)}, u32[]{:S(2)}) copy-start(f32[1,80,128]{2,1,0:T(8,128)} %param.21) | copy-start | bytes 122884
  67.2 8.8 %collective-permute-start.4 = (f32[80,2,133]{0,2,1:T(8,128)S(1)}, f32[80,2,133]{0,2,1:T(8,128)S(1)}, u32[]{:S(2)}, u32[]{:S(2)}) collective-permute-start(f32[80,2,133]{0,2,1:T(8,128)S(1)} %slice.401), channel_id=1, source_target_pairs={{1,0},{2,1},{3,2},{4,3},{5,4},{6,5},{7,6},{8,7},{9,8},{10,9},{11,1... | collective-permute-start | bytes 255368 | tf_op jit(solution)/shard_map/ppermute | solution.py:18
  73.6 9.5 %collective-permute-start.5 = (f32[80,3,133]{0,2,1:T(8,128)S(1)}, f32[80,3,133]{0,2,1:T(8,128)S(1)}, u32[]{:S(2)}, u32[]{:S(2)}) collective-permute-start(f32[80,3,133]{0,2,1:T(8,128)S(1)} %slice.403), channel_id=1, source_target_pairs={{0,1},{1,2},{2,3},{3,4},{4,5},{5,6},{6,7},{7,8},{8,9},{9,10},{10,1... | collective-permute-start | bytes 383048 | tf_op jit(solution)/shard_map/ppermute | solution.py:18
  83.2 9.5 %collective-permute-start.6 = (f32[80,32,2]{0,2,1:T(2,128)S(1)}, f32[80,32,2]{0,2,1:T(2,128)S(1)}, u32[]{:S(2)}, u32[]{:S(2)}) collective-permute-start(f32[80,32,2]{0,2,1:T(2,128)S(1)} %slice.406), channel_id=1, source_target_pairs={{16,0},{32,16},{48,32},{64,48},{80,64},{96,80},{112,96},{128,112},... | collective-permute-start | bytes 61448 | tf_op jit(solution)/shard_map/ppermute | solution.py:15
  90.7 8.3 %collective-permute-start.7 = (f32[80,32,3]{0,2,1:T(4,128)S(1)}, f32[80,32,3]{0,2,1:T(4,128)S(1)}, u32[]{:S(2)}, u32[]{:S(2)}) collective-permute-start(f32[80,32,3]{0,2,1:T(4,128)S(1)} %slice.408), channel_id=1, source_target_pairs={{496,0},{0,16},{16,32},{32,48},{48,64},{64,80},{80,96},{96,112},{1... | collective-permute-start | bytes 92168 | tf_op jit(solution)/shard_map/ppermute | solution.py:15

commit v4 on v3

--- a/solution.py
+++ b/solution.py
@@ -25,20 +25,30 @@
     return lax.ppermute(block, ("lon", "lat"), pairs)
 
 
-def gather_halo(x, split, hn, hs, hw, he):
-    rows, cols = x.shape[-2:]
-    west = neighbour_shift(x[..., :, cols - hw :], 0, -1)
-    east = neighbour_shift(x[..., :, :he], 0, 1)
-    edge_n = jnp.concatenate([west[..., rows - hn :, :], x[..., rows - hn :, :], east[..., rows - hn :, :]], axis=-1)
-    edge_s = jnp.concatenate([west[..., :hs, :], x[..., :hs, :], east[..., :hs, :]], axis=-1)
+def gather_halo(parts, hn, hs, hw, he):
+    rows, cols = parts[0].shape[-2:]
+    sizes = [p.shape[0] for p in parts]
+
+    def joined(window):
+        return jnp.concatenate([p[window] for p in parts], axis=0)
+
+    west = neighbour_shift(joined((Ellipsis, slice(None), slice(cols - hw, None))), 0, -1)
+    east = neighbour_shift(joined((Ellipsis, slice(None), slice(0, he))), 0, 1)
+    edge_n = jnp.concatenate(
+        [west[..., rows - hn :, :], joined((Ellipsis, slice(rows - hn, None), slice(None))),
+         east[..., rows - hn :, :]], axis=-1)
+    edge_s = jnp.concatenate(
+        [west[..., :hs, :], joined((Ellipsis, slice(0, hs), slice(None))), east[..., :hs, :]], axis=-1)
     north = neighbour_shift(edge_n, -1, 0)
     south = neighbour_shift(edge_s, 1, 0)
 
-    def assemble(part):
-        middle = jnp.concatenate([west[part], x[part], east[part]], axis=-1)
-        return jnp.concatenate([north[part], middle, south[part]], axis=-2)
-
-    return assemble(slice(0, split)), assemble(slice(split, None))
+    out, at = [], 0
+    for part, size in zip(parts, sizes):
+        span = slice(at, at + size)
+        middle = jnp.concatenate([west[span], part, east[span]], axis=-1)
+        out.append(jnp.concatenate([north[span], middle, south[span]], axis=-2))
+        at += size
+    return out
 
 
 def scatter_halo(g, rows, cols, gn, gs, gw, ge):
@@ -87,10 +97,8 @@
     control, diffusivity, land_mask, innovations, obs_sigma, obs_row, obs_col, obs_frac, obs_counts
 ):
     channels, rows, cols = control.shape
-    stacked = jnp.concatenate(
-        [control, diffusivity[None], land_mask.astype(jnp.float32)[None]], axis=0
-    )
-    field, coeff = gather_halo(stacked, channels, HN, HS, HW, HE)
+    coeff = jnp.stack([diffusivity, land_mask.astype(jnp.float32)])
+    field, coeff = gather_halo([control, coeff], HN, HS, HW, HE)
     weights = edge_weights(coeff[0], coeff[1])
 
     state = diffuse(diffuse(field, weights), trim(weights, 1))

time: 101 us -> 99.8 us (0.988)
  local copies, waits for them, and re-layouts: 13 us -> 11.7 us
    broadcast_in_dim x2 -> x0, local copies, waits for them, and re-layouts: 3.95 us -> none  [the longest x1 1.99 us: on_device(): land_mask.astype(jnp.float32)[None]]
    unnamed x22 -> x20, local copies, waits for them, and re-layouts: 2.58 us -> 4.22 us
    another operation x0 -> x5, other arithmetic: none -> 1.54 us  [on_device(): coeff = jnp.stack([diffusivity, land_mask.astype(jnp.float32)])]
    slice x2 -> x0, other arithmetic: 1.4 us -> none  [the longest x1 1.25 us: gather_halo(): west = neighbour_shift(x[..., :, cols - hw:], 0, -1)]
where the time goes in v4:
time: 99.8 us; the launch traced here: 99.3 us
  starting transfers between devices  39 us (39%)
  other arithmetic  20.4 us (20%)
  waiting for transfers between devices  17.5 us (18%)
  local copies, waits for them, and re-layouts  11.7 us (12%)
  matrix products  8.95 us (9%)
  between operations  1.82 us (2%)
    ppermute x4, starting transfers between devices, neighbour_shift(): return lax.ppermute(block, 'lon', pairs)  22.9 us
    add x4, other arithmetic, diffuse(): result = result + weight * (near - center)  16.3 us
    ppermute x4, starting transfers between devices, neighbour_shift(): return lax.ppermute(block, 'lat', pairs)  16.1 us
    ppermute x4, waiting for transfers between devices, neighbour_shift(): return lax.ppermute(block, 'lat', pairs)  9.79 us
    ppermute x4, waiting for transfers between devices, neighbour_shift(): return lax.ppermute(block, 'lon', pairs)  7.7 us
    dot_general x1, matrix products, on_device(): along = jnp.einsum('zrc,co->zro', state, wx, precision=hi)  5.65 us
    unnamed x20, local copies, waits for them, and re-layouts  4.22 us
    dot_general x1, matrix products, on_device(): adjoint = jnp.einsum('zro,co->zrc', spread, wx, precision=hi)  3.3 us
  transfers between devices with their start and end apart: 8, of which 6 were waited for; matrix products, arithmetic and copies ran while one was open for 3% of the time, Pallas kernels for 0%

profile of v4, /device:TPU:6, one launch (start us, length us, event | category | flops | bytes accessed | tf_op | source)
XLA Modules:
  0.0 99.3 jit_solution(4926530791006626382)
XLA Ops:
  0.7 0.7 convert_bitcast_fusion
  1.4 0.8 fusion.70
  2.5 1.8 %copy.51 = f32[80,32,128]{0,2,1:T(8,128)S(1)} copy(f32[80,32,128]{2,1,0:T(8,128)} %param.17) | data formatting | bytes 2621440 | tf_op args[0]
  4.5 3.8 %collective-permute-start = (f32[82,32,3]{0,2,1:T(4,128)S(1)}, f32[82,32,3]{0,2,1:T(4,128)S(1)}, u32[]{:S(2)}, u32[]{:S(2)}) collective-permute-start(f32[82,32,3]{0,2,1:T(4,128)S(1)} %pad_maximum_fusion.4), channel_id=1, source_target_pairs={{496,0},{0,16},{16,32},{32,48},{48,64},{64,80},{80,96},{96,112},{1... | collective-permute-start | bytes 94472 | tf_op jit(solution)/shard_map/ppermute | solution.py:15
  8.8 10.5 %collective-permute-start.1 = (f32[82,32,4]{0,2,1:T(4,128)S(1)}, f32[82,32,4]{0,2,1:T(4,128)S(1)}, u32[]{:S(2)}, u32[]{:S(2)}) collective-permute-start(f32[82,32,4]{0,2,1:T(4,128)S(1)} %pad_maximum_fusion.5), channel_id=1, source_target_pairs={{16,0},{32,16},{48,32},{64,48},{80,64},{96,80},{112,96},{128,112},... | collective-permute-start | bytes 125960 | tf_op jit(solution)/shard_map/ppermute | solution.py:15
  19.8 1.4 %collective-permute-done.1 = f32[82,32,4]{0,2,1:T(4,128)S(1)} collective-permute-done((f32[82,32,4]{0,2,1:T(4,128)S(1)}, f32[82,32,4]{0,2,1:T(4,128)S(1)}, u32[]{:S(2)}, u32[]{:S(2)}) %collective-permute-start.1) | collective-permute-done | bytes 42016 | tf_op jit(solution)/shard_map/ppermute | solution.py:15
  21.2 0.8 pad_maximum_fusion.2
  22.0 1.9 %collective-permute-start.2 = (f32[82,3,135]{0,2,1:T(8,128)}, f32[82,3,135]{0,2,1:T(8,128)S(1)}, u32[]{:S(2)}, u32[]{:S(2)}) collective-permute-start(f32[82,3,135]{0,2,1:T(8,128)} %pad_maximum_fusion.2), channel_id=1, source_target_pairs={{0,1},{1,2},{2,3},{3,4},{4,5},{5,6},{6,7},{7,8},{8,9},{9,10},{10,1... | collective-permute-start | bytes 398528 | tf_op jit(solution)/shard_map/ppermute | solution.py:18
  24.1 6.0 %collective-permute-start.3 = (f32[82,4,135]{0,2,1:T(8,128)S(1)}, f32[82,4,135]{0,2,1:T(8,128)S(1)}, u32[]{:S(2)}, u32[]{:S(2)}) collective-permute-start(f32[82,4,135]{0,2,1:T(8,128)S(1)} %pad_maximum_fusion.1), channel_id=1, source_target_pairs={{1,0},{2,1},{3,2},{4,3},{5,4},{6,5},{7,6},{8,7},{9,8},{10,9},{11,1... | collective-permute-start | bytes 531368 | tf_op jit(solution)/shard_map/ppermute | solution.py:18
  32.0 2.1 %collective-permute-done.3 = f32[82,4,135]{0,2,1:T(8,128)S(1)} collective-permute-done((f32[82,4,135]{0,2,1:T(8,128)S(1)}, f32[82,4,135]{0,2,1:T(8,128)S(1)}, u32[]{:S(2)}, u32[]{:S(2)}) %collective-permute-start.3) | collective-permute-done | bytes 177152 | tf_op jit(solution)/shard_map/ppermute | solution.py:18
  37.0 3.6 %fusion.13 = f32[80,37,133]{0,2,1:T(8,128)S(1)} fusion(f32[80,39,135]{0,2,1:T(8,128)S(1)} %pad_maximum_fusion, f32[37,133]{1,0:T(8,128)S(1)} %get-tuple-element.68, f32[37,133]{1,0:T(8,128)S(1)} %get-tuple-element.66, f32[37,133]{1,0:T(8,128)S(1)} %get-tuple-element.67, f32[37,133]{1,0:T(8,128)S(1)} %get-tuple-element.65), kind=kLoop, calls=%fused_computation.20 | loop fusion | flops 4724160 | bytes 9527056 | tf_op jit(solution)/shard_map/add | solution.py:84
  40.6 3.1 %fusion.75 = (f32[80,35,131]{0,2,1:T(8,128)S(1)}, f32[80,35,131]{0,2,1:T(8,128)S(1)}, f32[80,35,131]{0,2,1:T(8,128)}, f32[80,35,131]{0,2,1:T(8,128)}, f32[80,35,131]{0,2,1:T(8,128)}) fusion(f32[80,37,133]{0,2,1:T(8,128)S(1)} %fusion.13), kind=kLoop, calls=%fused_computation.138 | loop fusion | bytes 14672000 | tf_op jit(solution)/shard_map/slice | solution.py:80
  43.8 5.1 %fusion.33 = f32[80,33,129]{0,2,1:T(8,128)S(1)} fusion(f32[80,35,131]{0,2,1:T(8,128)S(1)} %get-tuple-element.61, f32[80,35,131]{0,2,1:T(8,128)} %get-tuple-element.62, f32[80,35,131]{0,2,1:T(8,128)} %get-tuple-element.63, f32[80,35,131]{0,2,1:T(8,128)} %get-tuple-element.64, f32[80,35,131]{0,2,1:T(8,128)S(1)} %get-tuple-element.60, ...), kind=kLoop, calls=%fused_computation.49 | loop fusion | flops 4086720 | bytes 8241552 | tf_op jit(solution)/shard_map/add | solution.py:84
  48.9 5.6 %fusion.42 = f32[80,128]{1,0:T(8,128)S(1)} fusion(f32[80,33,129]{0,2,1:T(8,128)S(1)} %fusion.33, f32[33,128]{1,0:T(8,128)S(1)} %select_add_fusion.3, f32[128]{0:T(128)S(1)} %get-tuple-element.73, s32[128]{0:T(128)S(1)} %add_bitcast_fusion, f32[128]{0:T(128)S(1)} %get-tuple-element.71, s32[128]{0:T(128)S(1)} %bitcast.54), kind=kOutput, calls=%fused_computation.62 | convolution fusion | flops 523848320 | bytes 1422144 | tf_op jit(solution)/shard_map/zrc,co->zro/dot_general | solution.py:121
  54.6 3.3 %fusion.40 = f32[80,33,129]{0,2,1:T(8,128)S(1)} fusion(f32[80,128]{1,0:T(8,128)S(1)} %bitcast_divide_fusion, f32[33,128]{1,0:T(8,128)S(1)} %select_add_fusion.3, f32[128]{0:T(128)S(1)} %get-tuple-element.73, s32[128]{0:T(128)S(1)} %add_bitcast_fusion, f32[128]{0:T(128)S(1)} %get-tuple-element.71, s32[128]{0:T(128)S(1)} %bitcast.55), kind=kOutput, calls=%fused_computation.60 | convolution fusion | flops 523520640 | bytes 1422144 | tf_op jit(solution)/shard_map/zro,co->zrc/dot_general | solution.py:130
  57.9 3.2 %fusion.25 = f32[80,35,131]{0,2,1:T(8,128)S(1)} fusion(f32[80,33,129]{0,2,1:T(8,128)S(1)} %fusion.40, f32[35,131]{1,0:T(8,128)S(1)} %slice.412, f32[35,131]{1,0:T(8,128)S(1)} %slice.410, f32[35,131]{1,0:T(8,128)S(1)} %slice.408, f32[35,131]{1,0:T(8,128)S(1)} %slice.406), kind=kLoop, calls=%fused_computation.40 | loop fusion | flops 4401600 | bytes 2902800 | tf_op jit(solution)/shard_map/add | solution.py:84
  61.1 4.3 %fusion.5 = f32[80,37,133]{0,2,1:T(8,128)S(1)} fusion(f32[80,35,131]{0,2,1:T(8,128)S(1)} %fusion.25, f32[37,133]{1,0:T(8,128)S(1)} %get-tuple-element.68, f32[37,133]{1,0:T(8,128)S(1)} %get-tuple-element.66, f32[37,133]{1,0:T(8,128)S(1)} %get-tuple-element.67, f32[37,133]{1,0:T(8,128)S(1)} %get-tuple-element.65), kind=kLoop, calls=%fused_computation.11 | loop fusion | flops 4724160 | bytes 3120656 | tf_op jit(solution)/shard_map/add | solution.py:84
  65.5 6.2 %collective-permute-start.4 = (f32[80,2,133]{0,2,1:T(8,128)S(1)}, f32[80,2,133]{0,2,1:T(8,128)S(1)}, u32[]{:S(2)}, u32[]{:S(2)}) collective-permute-start(f32[80,2,133]{0,2,1:T(8,128)S(1)} %slice.425), channel_id=1, source_target_pairs={{1,0},{2,1},{3,2},{4,3},{5,4},{6,5},{7,6},{8,7},{9,8},{10,9},{11,1... | collective-permute-start | bytes 255368 | tf_op jit(solution)/shard_map/ppermute | solution.py:18
  71.9 1.9 %collective-permute-start.5 = (f32[80,3,133]{0,2,1:T(8,128)S(1)}, f32[80,3,133]{0,2,1:T(8,128)S(1)}, u32[]{:S(2)}, u32[]{:S(2)}) collective-permute-start(f32[80,3,133]{0,2,1:T(8,128)S(1)} %slice.427), channel_id=1, source_target_pairs={{0,1},{1,2},{2,3},{3,4},{4,5},{5,6},{6,7},{7,8},{8,9},{9,10},{10,1... | collective-permute-start | bytes 383048 | tf_op jit(solution)/shard_map/ppermute | solution.py:18
  74.3 7.1 %collective-permute-done.5 = f32[80,3,133]{0,2,1:T(8,128)S(1)} collective-permute-done((f32[80,3,133]{0,2,1:T(8,128)S(1)}, f32[80,3,133]{0,2,1:T(8,128)S(1)}, u32[]{:S(2)}, u32[]{:S(2)}) %collective-permute-start.5) | collective-permute-done | bytes 127712 | tf_op jit(solution)/shard_map/ppermute | solution.py:18
  81.5 6.7 %collective-permute-start.6 = (f32[80,32,2]{0,2,1:T(2,128)S(1)}, f32[80,32,2]{0,2,1:T(2,128)S(1)}, u32[]{:S(2)}, u32[]{:S(2)}) collective-permute-start(f32[80,32,2]{0,2,1:T(2,128)S(1)} %slice.430), channel_id=1, source_target_pairs={{16,0},{32,16},{48,32},{64,48},{80,64},{96,80},{112,96},{128,112},... | collective-permute-start | bytes 61448 | tf_op jit(solution)/shard_map/ppermute | solution.py:15
  89.0 1.9 %collective-permute-start.7 = (f32[80,32,3]{0,2,1:T(4,128)S(1)}, f32[80,32,3]{0,2,1:T(4,128)S(1)}, u32[]{:S(2)}, u32[]{:S(2)}) collective-permute-start(f32[80,32,3]{0,2,1:T(4,128)S(1)} %slice.432), channel_id=1, source_target_pairs={{496,0},{0,16},{16,32},{32,48},{48,64},{64,80},{80,96},{96,112},{1... | collective-permute-start | bytes 92168 | tf_op jit(solution)/shard_map/ppermute | solution.py:15
  91.0 6.3 %collective-permute-done.7 = f32[80,32,3]{0,2,1:T(4,128)S(1)} collective-permute-done((f32[80,32,3]{0,2,1:T(4,128)S(1)}, f32[80,32,3]{0,2,1:T(4,128)S(1)}, u32[]{:S(2)}, u32[]{:S(2)}) %collective-permute-start.7) | collective-permute-done | bytes 30752 | tf_op jit(solution)/shard_map/ppermute | solution.py:15
  97.6 1.7 %copy.64 = f32[80,32,128]{2,1,0:T(8,128)} copy(f32[80,32,128]{0,2,1:T(8,128)S(1)} %scatter-add.19) | data formatting | bytes 2621440
  (77 shorter events, 7.3 us)
Async XLA Ops:
  0.6 7.7 %copy-start = (f32[32,128]{1,0:T(8,128)S(1)}, f32[32,128]{1,0:T(8,128)}, u32[]{:S(2)}) copy-start(f32[32,128]{1,0:T(8,128)} %param.18) | copy-start | bytes 49156
  0.6 18.7 %copy-start.5 = (f32[1,2,128]{2,1,0:T(2,128)S(1)}, f32[1,2,128]{2,1,0:T(2,128)}, u32[]{:S(2)}) copy-start(f32[1,2,128]{2,1,0:T(2,128)} %param.24) | copy-start | bytes 3076
  0.7 18.7 %copy-start.7 = (s32[1,128]{1,0:T(1,128)S(1)}, s32[1,128]{1,0:T(1,128)}, u32[]{:S(2)}) copy-start(s32[1,128]{1,0:T(1,128)} %param.22) | copy-start | bytes 1540
  4.3 25.8 %copy-start.6 = (s32[1,128]{1,0:T(1,128)S(1)}, s32[1,128]{1,0:T(1,128)}, u32[]{:S(2)}) copy-start(s32[1,128]{1,0:T(1,128)} %param.23) | copy-start | bytes 1540
  4.5 15.3 %collective-permute-start = (f32[82,32,3]{0,2,1:T(4,128)S(1)}, f32[82,32,3]{0,2,1:T(4,128)S(1)}, u32[]{:S(2)}, u32[]{:S(2)}) collective-permute-start(f32[82,32,3]{0,2,1:T(4,128)S(1)} %pad_maximum_fusion.4), channel_id=1, source_target_pairs={{496,0},{0,16},{16,32},{32,48},{48,64},{64,80},{80,96},{96,112},{1... | collective-permute-start | bytes 94472 | tf_op jit(solution)/shard_map/ppermute | solution.py:15
  8.8 12.4 %collective-permute-start.1 = (f32[82,32,4]{0,2,1:T(4,128)S(1)}, f32[82,32,4]{0,2,1:T(4,128)S(1)}, u32[]{:S(2)}, u32[]{:S(2)}) collective-permute-start(f32[82,32,4]{0,2,1:T(4,128)S(1)} %pad_maximum_fusion.5), channel_id=1, source_target_pairs={{16,0},{32,16},{48,32},{64,48},{80,64},{96,80},{112,96},{128,112},... | collective-permute-start | bytes 125960 | tf_op jit(solution)/shard_map/ppermute | solution.py:15
  22.0 9.7 %collective-permute-start.2 = (f32[82,3,135]{0,2,1:T(8,128)}, f32[82,3,135]{0,2,1:T(8,128)S(1)}, u32[]{:S(2)}, u32[]{:S(2)}) collective-permute-start(f32[82,3,135]{0,2,1:T(8,128)} %pad_maximum_fusion.2), channel_id=1, source_target_pairs={{0,1},{1,2},{2,3},{3,4},{4,5},{5,6},{6,7},{7,8},{8,9},{9,10},{10,1... | collective-permute-start | bytes 398528 | tf_op jit(solution)/shard_map/ppermute | solution.py:18
  24.1 10.1 %collective-permute-start.3 = (f32[82,4,135]{0,2,1:T(8,128)S(1)}, f32[82,4,135]{0,2,1:T(8,128)S(1)}, u32[]{:S(2)}, u32[]{:S(2)}) collective-permute-start(f32[82,4,135]{0,2,1:T(8,128)S(1)} %pad_maximum_fusion.1), channel_id=1, source_target_pairs={{1,0},{2,1},{3,2},{4,3},{5,4},{6,5},{7,6},{8,7},{9,8},{10,9},{11,1... | collective-permute-start | bytes 531368 | tf_op jit(solution)/shard_map/ppermute | solution.py:18
  40.6 3.1 %copy-start.1 = (f32[33,129]{1,0:T(8,128)S(1)}, f32[33,129]{1,0:T(8,128)}, u32[]{:S(2)}) copy-start(f32[33,129]{1,0:T(8,128)} %slice.420) | copy-start | bytes 51088
  40.6 3.1 %copy-start.2 = (f32[33,129]{1,0:T(8,128)S(1)}, f32[33,129]{1,0:T(8,128)}, u32[]{:S(2)}) copy-start(f32[33,129]{1,0:T(8,128)} %slice.422) | copy-start | bytes 51088
  43.7 10.8 %copy-start.3 = (f32[1,80,128]{2,1,0:T(8,128)S(1)}, f32[1,80,128]{2,1,0:T(8,128)}, u32[]{:S(2)}) copy-start(f32[1,80,128]{2,1,0:T(8,128)} %param.20) | copy-start | bytes 122884
  43.7 10.8 %copy-start.4 = (f32[1,80,128]{2,1,0:T(8,128)S(1)}, f32[1,80,128]{2,1,0:T(8,128)}, u32[]{:S(2)}) copy-start(f32[1,80,128]{2,1,0:T(8,128)} %param.21) | copy-start | bytes 122884
  65.5 8.8 %collective-permute-start.4 = (f32[80,2,133]{0,2,1:T(8,128)S(1)}, f32[80,2,133]{0,2,1:T(8,128)S(1)}, u32[]{:S(2)}, u32[]{:S(2)}) collective-permute-start(f32[80,2,133]{0,2,1:T(8,128)S(1)} %slice.425), channel_id=1, source_target_pairs={{1,0},{2,1},{3,2},{4,3},{5,4},{6,5},{7,6},{8,7},{9,8},{10,9},{11,1... | collective-permute-start | bytes 255368 | tf_op jit(solution)/shard_map/ppermute | solution.py:18
  71.9 9.5 %collective-permute-start.5 = (f32[80,3,133]{0,2,1:T(8,128)S(1)}, f32[80,3,133]{0,2,1:T(8,128)S(1)}, u32[]{:S(2)}, u32[]{:S(2)}) collective-permute-start(f32[80,3,133]{0,2,1:T(8,128)S(1)} %slice.427), channel_id=1, source_target_pairs={{0,1},{1,2},{2,3},{3,4},{4,5},{5,6},{6,7},{7,8},{8,9},{9,10},{10,1... | collective-permute-start | bytes 383048 | tf_op jit(solution)/shard_map/ppermute | solution.py:18
  81.5 9.5 %collective-permute-start.6 = (f32[80,32,2]{0,2,1:T(2,128)S(1)}, f32[80,32,2]{0,2,1:T(2,128)S(1)}, u32[]{:S(2)}, u32[]{:S(2)}) collective-permute-start(f32[80,32,2]{0,2,1:T(2,128)S(1)} %slice.430), channel_id=1, source_target_pairs={{16,0},{32,16},{48,32},{64,48},{80,64},{96,80},{112,96},{128,112},... | collective-permute-start | bytes 61448 | tf_op jit(solution)/shard_map/ppermute | solution.py:15
  89.0 8.3 %collective-permute-start.7 = (f32[80,32,3]{0,2,1:T(4,128)S(1)}, f32[80,32,3]{0,2,1:T(4,128)S(1)}, u32[]{:S(2)}, u32[]{:S(2)}) collective-permute-start(f32[80,32,3]{0,2,1:T(4,128)S(1)} %slice.432), channel_id=1, source_target_pairs={{496,0},{0,16},{16,32},{32,48},{48,64},{64,80},{80,96},{96,112},{1... | collective-permute-start | bytes 92168 | tf_op jit(solution)/shard_map/ppermute | solution.py:15

commit v5 on v4

--- a/solution.py
+++ b/solution.py
@@ -101,8 +101,10 @@
     field, coeff = gather_halo([control, coeff], HN, HS, HW, HE)
     weights = edge_weights(coeff[0], coeff[1])
 
-    state = diffuse(diffuse(field, weights), trim(weights, 1))
-    state = state[:, 1 : rows + 2, 1 : cols + 2]
+    once = diffuse(field, weights)
+    state = diffuse(
+        once[:, 1 : rows + 4, 1 : cols + 4], [w[2 : rows + 3, 2 : cols + 3] for w in weights]
+    )
     state = lax.optimization_barrier(state)
 
     frac_y = obs_frac[0, 0]

time: 99.8 us -> 93 us (0.932)
  local copies, waits for them, and re-layouts: 11.7 us -> 7.38 us
  other arithmetic: 20.4 us -> 17.8 us
    slice x5 -> x4, local copies, waits for them, and re-layouts: 4.66 us -> 0.32 us  [on_device(): w[2:rows + 3, 2:cols + 3]]
    add x4, other arithmetic: 16.3 us -> 13.8 us  [diffuse(): result = result + weight * (near - center)]
    unnamed x20 -> x16, local copies, waits for them, and re-layouts: 4.22 us -> 4.21 us
where the time goes in v5:
time: 93 us; the launch traced here: 92.5 us
  starting transfers between devices  39 us (42%)
  other arithmetic  17.8 us (19%)
  waiting for transfers between devices  17.5 us (19%)
  matrix products  8.95 us (10%)
  local copies, waits for them, and re-layouts  7.38 us (8%)
  between operations  1.81 us (2%)
    ppermute x4, starting transfers between devices, neighbour_shift(): return lax.ppermute(block, 'lon', pairs)  22.9 us
    ppermute x4, starting transfers between devices, neighbour_shift(): return lax.ppermute(block, 'lat', pairs)  16.1 us
    add x4, other arithmetic, diffuse(): result = result + weight * (near - center)  13.8 us
    ppermute x4, waiting for transfers between devices, neighbour_shift(): return lax.ppermute(block, 'lat', pairs)  9.79 us
    ppermute x4, waiting for transfers between devices, neighbour_shift(): return lax.ppermute(block, 'lon', pairs)  7.7 us
    dot_general x1, matrix products, on_device(): along = jnp.einsum('zrc,co->zro', state, wx, precision=hi)  5.65 us
    unnamed x16, local copies, waits for them, and re-layouts  4.21 us
    dot_general x1, matrix products, on_device(): adjoint = jnp.einsum('zro,co->zrc', spread, wx, precision=hi)  3.3 us
  transfers between devices with their start and end apart: 8, of which 6 were waited for; matrix products, arithmetic and copies ran while one was open for 3% of the time, Pallas kernels for 0%

profile of v5, /device:TPU:6, one launch (start us, length us, event | category | flops | bytes accessed | tf_op | source)
XLA Modules:
  0.0 92.5 jit_solution(16798892253525496259)
XLA Ops:
  0.7 0.7 convert_bitcast_fusion
  1.4 0.8 fusion.70
  2.5 1.8 %copy.51 = f32[80,32,128]{0,2,1:T(8,128)S(1)} copy(f32[80,32,128]{2,1,0:T(8,128)} %param.17) | data formatting | bytes 2621440 | tf_op args[0]
  4.5 3.8 %collective-permute-start = (f32[82,32,3]{0,2,1:T(4,128)S(1)}, f32[82,32,3]{0,2,1:T(4,128)S(1)}, u32[]{:S(2)}, u32[]{:S(2)}) collective-permute-start(f32[82,32,3]{0,2,1:T(4,128)S(1)} %pad_maximum_fusion.4), channel_id=1, source_target_pairs={{496,0},{0,16},{16,32},{32,48},{48,64},{64,80},{80,96},{96,112},{1... | collective-permute-start | bytes 94472 | tf_op jit(solution)/shard_map/ppermute | solution.py:15
  8.8 10.5 %collective-permute-start.1 = (f32[82,32,4]{0,2,1:T(4,128)S(1)}, f32[82,32,4]{0,2,1:T(4,128)S(1)}, u32[]{:S(2)}, u32[]{:S(2)}) collective-permute-start(f32[82,32,4]{0,2,1:T(4,128)S(1)} %pad_maximum_fusion.5), channel_id=1, source_target_pairs={{16,0},{32,16},{48,32},{64,48},{80,64},{96,80},{112,96},{128,112},... | collective-permute-start | bytes 125960 | tf_op jit(solution)/shard_map/ppermute | solution.py:15
  19.8 1.4 %collective-permute-done.1 = f32[82,32,4]{0,2,1:T(4,128)S(1)} collective-permute-done((f32[82,32,4]{0,2,1:T(4,128)S(1)}, f32[82,32,4]{0,2,1:T(4,128)S(1)}, u32[]{:S(2)}, u32[]{:S(2)}) %collective-permute-start.1) | collective-permute-done | bytes 42016 | tf_op jit(solution)/shard_map/ppermute | solution.py:15
  21.2 0.8 pad_maximum_fusion.2
  22.0 1.9 %collective-permute-start.2 = (f32[82,3,135]{0,2,1:T(8,128)}, f32[82,3,135]{0,2,1:T(8,128)S(1)}, u32[]{:S(2)}, u32[]{:S(2)}) collective-permute-start(f32[82,3,135]{0,2,1:T(8,128)} %pad_maximum_fusion.2), channel_id=1, source_target_pairs={{0,1},{1,2},{2,3},{3,4},{4,5},{5,6},{6,7},{7,8},{8,9},{9,10},{10,1... | collective-permute-start | bytes 398528 | tf_op jit(solution)/shard_map/ppermute | solution.py:18
  24.1 6.0 %collective-permute-start.3 = (f32[82,4,135]{0,2,1:T(8,128)S(1)}, f32[82,4,135]{0,2,1:T(8,128)S(1)}, u32[]{:S(2)}, u32[]{:S(2)}) collective-permute-start(f32[82,4,135]{0,2,1:T(8,128)S(1)} %pad_maximum_fusion.1), channel_id=1, source_target_pairs={{1,0},{2,1},{3,2},{4,3},{5,4},{6,5},{7,6},{8,7},{9,8},{10,9},{11,1... | collective-permute-start | bytes 531368 | tf_op jit(solution)/shard_map/ppermute | solution.py:18
  32.0 2.1 %collective-permute-done.3 = f32[82,4,135]{0,2,1:T(8,128)S(1)} collective-permute-done((f32[82,4,135]{0,2,1:T(8,128)S(1)}, f32[82,4,135]{0,2,1:T(8,128)S(1)}, u32[]{:S(2)}, u32[]{:S(2)}) %collective-permute-start.3) | collective-permute-done | bytes 177152 | tf_op jit(solution)/shard_map/ppermute | solution.py:18
  35.7 3.6 %fusion.13 = f32[80,37,133]{0,2,1:T(8,128)S(1)} fusion(f32[80,39,135]{0,2,1:T(8,128)S(1)} %pad_maximum_fusion, f32[37,133]{1,0:T(8,128)S(1)} %get-tuple-element.63, f32[37,133]{1,0:T(8,128)S(1)} %get-tuple-element.61, f32[37,133]{1,0:T(8,128)S(1)} %get-tuple-element.62, f32[37,133]{1,0:T(8,128)S(1)} %get-tuple-element.60), kind=kLoop, calls=%fused_computation.20 | loop fusion | flops 4724160 | bytes 9527056 | tf_op jit(solution)/shard_map/add | solution.py:84
  39.4 2.8 %fusion.33 = f32[80,33,129]{0,2,1:T(8,128)S(1)} fusion(f32[80,37,133]{0,2,1:T(8,128)S(1)} %fusion.13, f32[33,129]{1,0:T(8,128)S(1)} %slice.426, f32[33,129]{1,0:T(8,128)S(1)} %slice.424, f32[33,129]{1,0:T(8,128)S(1)} %slice.422, f32[33,129]{1,0:T(8,128)S(1)} %slice.420), kind=kLoop, calls=%fused_computation.49 | loop fusion | flops 4086720 | bytes 8241552 | tf_op jit(solution)/shard_map/add | solution.py:84
  42.2 5.6 %fusion.42 = f32[80,128]{1,0:T(8,128)S(1)} fusion(f32[80,33,129]{0,2,1:T(8,128)S(1)} %fusion.33, f32[33,128]{1,0:T(8,128)S(1)} %select_add_fusion.3, f32[128]{0:T(128)S(1)} %get-tuple-element.68, s32[128]{0:T(128)S(1)} %add_bitcast_fusion, f32[128]{0:T(128)S(1)} %get-tuple-element.66, s32[128]{0:T(128)S(1)} %bitcast.54), kind=kOutput, calls=%fused_computation.62 | convolution fusion | flops 523848320 | bytes 1422144 | tf_op jit(solution)/shard_map/zrc,co->zro/dot_general | solution.py:123
  47.9 3.3 %fusion.40 = f32[80,33,129]{0,2,1:T(8,128)S(1)} fusion(f32[80,128]{1,0:T(8,128)S(1)} %bitcast_divide_fusion, f32[33,128]{1,0:T(8,128)S(1)} %select_add_fusion.3, f32[128]{0:T(128)S(1)} %get-tuple-element.68, s32[128]{0:T(128)S(1)} %add_bitcast_fusion, f32[128]{0:T(128)S(1)} %get-tuple-element.66, s32[128]{0:T(128)S(1)} %bitcast.55), kind=kOutput, calls=%fused_computation.60 | convolution fusion | flops 523520640 | bytes 1422144 | tf_op jit(solution)/shard_map/zro,co->zrc/dot_general | solution.py:132
  51.3 3.2 %fusion.25 = f32[80,35,131]{0,2,1:T(8,128)S(1)} fusion(f32[80,33,129]{0,2,1:T(8,128)S(1)} %fusion.40, f32[35,131]{1,0:T(8,128)S(1)} %slice.431, f32[35,131]{1,0:T(8,128)S(1)} %slice.430, f32[35,131]{1,0:T(8,128)S(1)} %slice.429, f32[35,131]{1,0:T(8,128)S(1)} %slice.428), kind=kLoop, calls=%fused_computation.40 | loop fusion | flops 4401600 | bytes 2902800 | tf_op jit(solution)/shard_map/add | solution.py:84
  54.5 4.1 %fusion.5 = f32[80,37,133]{0,2,1:T(8,128)S(1)} fusion(f32[80,35,131]{0,2,1:T(8,128)S(1)} %fusion.25, f32[37,133]{1,0:T(8,128)S(1)} %get-tuple-element.63, f32[37,133]{1,0:T(8,128)S(1)} %get-tuple-element.61, f32[37,133]{1,0:T(8,128)S(1)} %get-tuple-element.62, f32[37,133]{1,0:T(8,128)S(1)} %get-tuple-element.60), kind=kLoop, calls=%fused_computation.11 | loop fusion | flops 4724160 | bytes 3120656 | tf_op jit(solution)/shard_map/add | solution.py:84
  58.6 6.2 %collective-permute-start.4 = (f32[80,2,133]{0,2,1:T(8,128)S(1)}, f32[80,2,133]{0,2,1:T(8,128)S(1)}, u32[]{:S(2)}, u32[]{:S(2)}) collective-permute-start(f32[80,2,133]{0,2,1:T(8,128)S(1)} %slice.434), channel_id=1, source_target_pairs={{1,0},{2,1},{3,2},{4,3},{5,4},{6,5},{7,6},{8,7},{9,8},{10,9},{11,1... | collective-permute-start | bytes 255368 | tf_op jit(solution)/shard_map/ppermute | solution.py:18
  65.0 1.9 %collective-permute-start.5 = (f32[80,3,133]{0,2,1:T(8,128)S(1)}, f32[80,3,133]{0,2,1:T(8,128)S(1)}, u32[]{:S(2)}, u32[]{:S(2)}) collective-permute-start(f32[80,3,133]{0,2,1:T(8,128)S(1)} %slice.436), channel_id=1, source_target_pairs={{0,1},{1,2},{2,3},{3,4},{4,5},{5,6},{6,7},{7,8},{8,9},{9,10},{10,1... | collective-permute-start | bytes 383048 | tf_op jit(solution)/shard_map/ppermute | solution.py:18
  67.4 7.1 %collective-permute-done.5 = f32[80,3,133]{0,2,1:T(8,128)S(1)} collective-permute-done((f32[80,3,133]{0,2,1:T(8,128)S(1)}, f32[80,3,133]{0,2,1:T(8,128)S(1)}, u32[]{:S(2)}, u32[]{:S(2)}) %collective-permute-start.5) | collective-permute-done | bytes 127712 | tf_op jit(solution)/shard_map/ppermute | solution.py:18
  74.6 6.7 %collective-permute-start.6 = (f32[80,32,2]{0,2,1:T(2,128)S(1)}, f32[80,32,2]{0,2,1:T(2,128)S(1)}, u32[]{:S(2)}, u32[]{:S(2)}) collective-permute-start(f32[80,32,2]{0,2,1:T(2,128)S(1)} %slice.439), channel_id=1, source_target_pairs={{16,0},{32,16},{48,32},{64,48},{80,64},{96,80},{112,96},{128,112},... | collective-permute-start | bytes 61448 | tf_op jit(solution)/shard_map/ppermute | solution.py:15
  81.3 0.6 fusion.57
  82.2 1.9 %collective-permute-start.7 = (f32[80,32,3]{0,2,1:T(4,128)S(1)}, f32[80,32,3]{0,2,1:T(4,128)S(1)}, u32[]{:S(2)}, u32[]{:S(2)}) collective-permute-start(f32[80,32,3]{0,2,1:T(4,128)S(1)} %slice.441), channel_id=1, source_target_pairs={{496,0},{0,16},{16,32},{32,48},{48,64},{64,80},{80,96},{96,112},{1... | collective-permute-start | bytes 92168 | tf_op jit(solution)/shard_map/ppermute | solution.py:15
  84.2 6.3 %collective-permute-done.7 = f32[80,32,3]{0,2,1:T(4,128)S(1)} collective-permute-done((f32[80,32,3]{0,2,1:T(4,128)S(1)}, f32[80,32,3]{0,2,1:T(4,128)S(1)}, u32[]{:S(2)}, u32[]{:S(2)}) %collective-permute-start.7) | collective-permute-done | bytes 30752 | tf_op jit(solution)/shard_map/ppermute | solution.py:15
  90.8 1.7 %copy.64 = f32[80,32,128]{2,1,0:T(8,128)} copy(f32[80,32,128]{0,2,1:T(8,128)S(1)} %scatter-add.19) | data formatting | bytes 2621440
  (72 shorter events, 5.5 us)
Async XLA Ops:
  0.6 7.7 %copy-start = (f32[32,128]{1,0:T(8,128)S(1)}, f32[32,128]{1,0:T(8,128)}, u32[]{:S(2)}) copy-start(f32[32,128]{1,0:T(8,128)} %param.18) | copy-start | bytes 49156
  0.6 18.7 %copy-start.3 = (f32[1,2,128]{2,1,0:T(2,128)S(1)}, f32[1,2,128]{2,1,0:T(2,128)}, u32[]{:S(2)}) copy-start(f32[1,2,128]{2,1,0:T(2,128)} %param.24) | copy-start | bytes 3076
  0.7 18.7 %copy-start.5 = (s32[1,128]{1,0:T(1,128)S(1)}, s32[1,128]{1,0:T(1,128)}, u32[]{:S(2)}) copy-start(s32[1,128]{1,0:T(1,128)} %param.22) | copy-start | bytes 1540
  4.3 25.8 %copy-start.4 = (s32[1,128]{1,0:T(1,128)S(1)}, s32[1,128]{1,0:T(1,128)}, u32[]{:S(2)}) copy-start(s32[1,128]{1,0:T(1,128)} %param.23) | copy-start | bytes 1540
  4.5 15.3 %collective-permute-start = (f32[82,32,3]{0,2,1:T(4,128)S(1)}, f32[82,32,3]{0,2,1:T(4,128)S(1)}, u32[]{:S(2)}, u32[]{:S(2)}) collective-permute-start(f32[82,32,3]{0,2,1:T(4,128)S(1)} %pad_maximum_fusion.4), channel_id=1, source_target_pairs={{496,0},{0,16},{16,32},{32,48},{48,64},{64,80},{80,96},{96,112},{1... | collective-permute-start | bytes 94472 | tf_op jit(solution)/shard_map/ppermute | solution.py:15
  8.8 12.4 %collective-permute-start.1 = (f32[82,32,4]{0,2,1:T(4,128)S(1)}, f32[82,32,4]{0,2,1:T(4,128)S(1)}, u32[]{:S(2)}, u32[]{:S(2)}) collective-permute-start(f32[82,32,4]{0,2,1:T(4,128)S(1)} %pad_maximum_fusion.5), channel_id=1, source_target_pairs={{16,0},{32,16},{48,32},{64,48},{80,64},{96,80},{112,96},{128,112},... | collective-permute-start | bytes 125960 | tf_op jit(solution)/shard_map/ppermute | solution.py:15
  22.0 9.7 %collective-permute-start.2 = (f32[82,3,135]{0,2,1:T(8,128)}, f32[82,3,135]{0,2,1:T(8,128)S(1)}, u32[]{:S(2)}, u32[]{:S(2)}) collective-permute-start(f32[82,3,135]{0,2,1:T(8,128)} %pad_maximum_fusion.2), channel_id=1, source_target_pairs={{0,1},{1,2},{2,3},{3,4},{4,5},{5,6},{6,7},{7,8},{8,9},{9,10},{10,1... | collective-permute-start | bytes 398528 | tf_op jit(solution)/shard_map/ppermute | solution.py:18
  24.1 10.1 %collective-permute-start.3 = (f32[82,4,135]{0,2,1:T(8,128)S(1)}, f32[82,4,135]{0,2,1:T(8,128)S(1)}, u32[]{:S(2)}, u32[]{:S(2)}) collective-permute-start(f32[82,4,135]{0,2,1:T(8,128)S(1)} %pad_maximum_fusion.1), channel_id=1, source_target_pairs={{1,0},{2,1},{3,2},{4,3},{5,4},{6,5},{7,6},{8,7},{9,8},{10,9},{11,1... | collective-permute-start | bytes 531368 | tf_op jit(solution)/shard_map/ppermute | solution.py:18
  39.4 8.5 %copy-start.1 = (f32[1,80,128]{2,1,0:T(8,128)S(1)}, f32[1,80,128]{2,1,0:T(8,128)}, u32[]{:S(2)}) copy-start(f32[1,80,128]{2,1,0:T(8,128)} %param.20) | copy-start | bytes 122884
  39.4 8.5 %copy-start.2 = (f32[1,80,128]{2,1,0:T(8,128)S(1)}, f32[1,80,128]{2,1,0:T(8,128)}, u32[]{:S(2)}) copy-start(f32[1,80,128]{2,1,0:T(8,128)} %param.21) | copy-start | bytes 122884
  58.6 8.8 %collective-permute-start.4 = (f32[80,2,133]{0,2,1:T(8,128)S(1)}, f32[80,2,133]{0,2,1:T(8,128)S(1)}, u32[]{:S(2)}, u32[]{:S(2)}) collective-permute-start(f32[80,2,133]{0,2,1:T(8,128)S(1)} %slice.434), channel_id=1, source_target_pairs={{1,0},{2,1},{3,2},{4,3},{5,4},{6,5},{7,6},{8,7},{9,8},{10,9},{11,1... | collective-permute-start | bytes 255368 | tf_op jit(solution)/shard_map/ppermute | solution.py:18
  65.0 9.5 %collective-permute-start.5 = (f32[80,3,133]{0,2,1:T(8,128)S(1)}, f32[80,3,133]{0,2,1:T(8,128)S(1)}, u32[]{:S(2)}, u32[]{:S(2)}) collective-permute-start(f32[80,3,133]{0,2,1:T(8,128)S(1)} %slice.436), channel_id=1, source_target_pairs={{0,1},{1,2},{2,3},{3,4},{4,5},{5,6},{6,7},{7,8},{8,9},{9,10},{10,1... | collective-permute-start | bytes 383048 | tf_op jit(solution)/shard_map/ppermute | solution.py:18
  74.6 9.5 %collective-permute-start.6 = (f32[80,32,2]{0,2,1:T(2,128)S(1)}, f32[80,32,2]{0,2,1:T(2,128)S(1)}, u32[]{:S(2)}, u32[]{:S(2)}) collective-permute-start(f32[80,32,2]{0,2,1:T(2,128)S(1)} %slice.439), channel_id=1, source_target_pairs={{16,0},{32,16},{48,32},{64,48},{80,64},{96,80},{112,96},{128,112},... | collective-permute-start | bytes 61448 | tf_op jit(solution)/shard_map/ppermute | solution.py:15
  82.2 8.3 %collective-permute-start.7 = (f32[80,32,3]{0,2,1:T(4,128)S(1)}, f32[80,32,3]{0,2,1:T(4,128)S(1)}, u32[]{:S(2)}, u32[]{:S(2)}) collective-permute-start(f32[80,32,3]{0,2,1:T(4,128)S(1)} %slice.441), channel_id=1, source_target_pairs={{496,0},{0,16},{16,32},{32,48},{48,64},{64,80},{80,96},{96,112},{1... | collective-permute-start | bytes 92168 | tf_op jit(solution)/shard_map/ppermute | solution.py:15

commit v6 on v5

--- a/solution.py
+++ b/solution.py
@@ -73,15 +73,14 @@
     for oy, ox in ((0, 1), (0, -1), (1, 0), (-1, 0)):
         near = (slice(1 + oy, kappa.shape[0] - 1 + oy), slice(1 + ox, kappa.shape[1] - 1 + ox))
         out.append(0.5 * (kappa_mid + kappa[near]) * mask_mid * mask[near])
-    return out
+    return [1.0 - (((out[0] + out[1]) + out[2]) + out[3])] + out
 
 
 def diffuse(padded, weights):
-    center = padded[..., 1:-1, 1:-1]
-    result = center
-    for (oy, ox), weight in zip(((0, 1), (0, -1), (1, 0), (-1, 0)), weights):
+    result = weights[0] * padded[..., 1:-1, 1:-1]
+    for (oy, ox), weight in zip(((0, 1), (0, -1), (1, 0), (-1, 0)), weights[1:]):
         near = padded[..., 1 + oy : padded.shape[-2] - 1 + oy, 1 + ox : padded.shape[-1] - 1 + ox]
-        result = result + weight * (near - center)
+        result = result + weight * near
     return result
 
 

time: 93 us -> 95.8 us (1.030)
  other arithmetic: 17.8 us -> 20.4 us
    add x4, other arithmetic: 13.8 us -> 16.4 us  [diffuse(): result = result + weight * near]
where the time goes in v6:
time: 95.8 us; the launch traced here: 95.2 us
  starting transfers between devices  39 us (41%)
  other arithmetic  20.4 us (21%)
  waiting for transfers between devices  17.5 us (18%)
  matrix products  8.95 us (9%)
  local copies, waits for them, and re-layouts  7.54 us (8%)
  between operations  1.81 us (2%)
    ppermute x4, starting transfers between devices, neighbour_shift(): return lax.ppermute(block, 'lon', pairs)  22.9 us
    add x4, other arithmetic, diffuse(): result = result + weight * near  16.4 us
    ppermute x4, starting transfers between devices, neighbour_shift(): return lax.ppermute(block, 'lat', pairs)  16.1 us
    ppermute x4, waiting for transfers between devices, neighbour_shift(): return lax.ppermute(block, 'lat', pairs)  9.79 us
    ppermute x4, waiting for transfers between devices, neighbour_shift(): return lax.ppermute(block, 'lon', pairs)  7.7 us
    dot_general x1, matrix products, on_device(): along = jnp.einsum('zrc,co->zro', state, wx, precision=hi)  5.65 us
    unnamed x16, local copies, waits for them, and re-layouts  4.21 us
    dot_general x1, matrix products, on_device(): adjoint = jnp.einsum('zro,co->zrc', spread, wx, precision=hi)  3.3 us
  transfers between devices with their start and end apart: 8, of which 6 were waited for; matrix products, arithmetic and copies ran while one was open for 3% of the time, Pallas kernels for 0%

profile of v6, /device:TPU:6, one launch (start us, length us, event | category | flops | bytes accessed | tf_op | source)
XLA Modules:
  0.0 95.2 jit_solution(11846925909402681821)
XLA Ops:
  0.7 0.7 convert_bitcast_fusion
  1.4 0.8 fusion.56
  2.5 1.8 %copy.51 = f32[80,32,128]{0,2,1:T(8,128)S(1)} copy(f32[80,32,128]{2,1,0:T(8,128)} %param.17) | data formatting | bytes 2621440 | tf_op args[0]
  4.5 3.8 %collective-permute-start = (f32[82,32,3]{0,2,1:T(4,128)S(1)}, f32[82,32,3]{0,2,1:T(4,128)S(1)}, u32[]{:S(2)}, u32[]{:S(2)}) collective-permute-start(f32[82,32,3]{0,2,1:T(4,128)S(1)} %pad_maximum_fusion.4), channel_id=1, source_target_pairs={{496,0},{0,16},{16,32},{32,48},{48,64},{64,80},{80,96},{96,112},{1... | collective-permute-start | bytes 94472 | tf_op jit(solution)/shard_map/ppermute | solution.py:15
  8.8 10.5 %collective-permute-start.1 = (f32[82,32,4]{0,2,1:T(4,128)S(1)}, f32[82,32,4]{0,2,1:T(4,128)S(1)}, u32[]{:S(2)}, u32[]{:S(2)}) collective-permute-start(f32[82,32,4]{0,2,1:T(4,128)S(1)} %pad_maximum_fusion.5), channel_id=1, source_target_pairs={{16,0},{32,16},{48,32},{64,48},{80,64},{96,80},{112,96},{128,112},... | collective-permute-start | bytes 125960 | tf_op jit(solution)/shard_map/ppermute | solution.py:15
  19.8 1.4 %collective-permute-done.1 = f32[82,32,4]{0,2,1:T(4,128)S(1)} collective-permute-done((f32[82,32,4]{0,2,1:T(4,128)S(1)}, f32[82,32,4]{0,2,1:T(4,128)S(1)}, u32[]{:S(2)}, u32[]{:S(2)}) %collective-permute-start.1) | collective-permute-done | bytes 42016 | tf_op jit(solution)/shard_map/ppermute | solution.py:15
  21.2 0.8 pad_maximum_fusion.2
  22.0 1.9 %collective-permute-start.2 = (f32[82,3,135]{0,2,1:T(8,128)}, f32[82,3,135]{0,2,1:T(8,128)S(1)}, u32[]{:S(2)}, u32[]{:S(2)}) collective-permute-start(f32[82,3,135]{0,2,1:T(8,128)} %pad_maximum_fusion.2), channel_id=1, source_target_pairs={{0,1},{1,2},{2,3},{3,4},{4,5},{5,6},{6,7},{7,8},{8,9},{9,10},{10,1... | collective-permute-start | bytes 398528 | tf_op jit(solution)/shard_map/ppermute | solution.py:18
  24.1 6.0 %collective-permute-start.3 = (f32[82,4,135]{0,2,1:T(8,128)S(1)}, f32[82,4,135]{0,2,1:T(8,128)S(1)}, u32[]{:S(2)}, u32[]{:S(2)}) collective-permute-start(f32[82,4,135]{0,2,1:T(8,128)S(1)} %pad_maximum_fusion.1), channel_id=1, source_target_pairs={{1,0},{2,1},{3,2},{4,3},{5,4},{6,5},{7,6},{8,7},{9,8},{10,9},{11,1... | collective-permute-start | bytes 531368 | tf_op jit(solution)/shard_map/ppermute | solution.py:18
  32.0 2.1 %collective-permute-done.3 = f32[82,4,135]{0,2,1:T(8,128)S(1)} collective-permute-done((f32[82,4,135]{0,2,1:T(8,128)S(1)}, f32[82,4,135]{0,2,1:T(8,128)S(1)}, u32[]{:S(2)}, u32[]{:S(2)}) %collective-permute-start.3) | collective-permute-done | bytes 177152 | tf_op jit(solution)/shard_map/ppermute | solution.py:18
  35.9 4.4 %fusion.9 = f32[80,37,133]{0,2,1:T(8,128)S(1)} fusion(f32[80,39,135]{0,2,1:T(8,128)S(1)} %pad_maximum_fusion, f32[37,133]{1,0:T(8,128)S(1)} %get-tuple-element.64, f32[37,133]{1,0:T(8,128)S(1)} %get-tuple-element.63, f32[37,133]{1,0:T(8,128)S(1)} %get-tuple-element.62, f32[37,133]{1,0:T(8,128)S(1)} %get-tuple-element.61, f32[37,133]{1,0:T(8,128)S(1)} %get-tuple-element.60), kind=kLoop, calls=%fused_computation.16 | loop fusion | flops 3543120 | bytes 9546740 | tf_op jit(solution)/shard_map/add | solution.py:83
  40.3 3.4 %fusion.22 = f32[80,33,129]{0,2,1:T(8,128)S(1)} fusion(f32[80,37,133]{0,2,1:T(8,128)S(1)} %fusion.9, f32[33,129]{1,0:T(8,128)S(1)} %slice.436, f32[33,129]{1,0:T(8,128)S(1)} %slice.434, f32[33,129]{1,0:T(8,128)S(1)} %slice.432, f32[33,129]{1,0:T(8,128)S(1)} %slice.430, f32[33,129]{1,0:T(8,128)S(1)} %slice.419), kind=kLoop, calls=%fused_computation.39 | loop fusion | flops 3065040 | bytes 8258580 | tf_op jit(solution)/shard_map/add | solution.py:83
  43.7 5.6 %fusion.28 = f32[80,128]{1,0:T(8,128)S(1)} fusion(f32[80,33,129]{0,2,1:T(8,128)S(1)} %fusion.22, f32[33,128]{1,0:T(8,128)S(1)} %select_add_fusion.3, f32[128]{0:T(128)S(1)} %get-tuple-element.69, s32[128]{0:T(128)S(1)} %add_bitcast_fusion, f32[128]{0:T(128)S(1)} %get-tuple-element.67, s32[128]{0:T(128)S(1)} %bitcast.54), kind=kOutput, calls=%fused_computation.50 | convolution fusion | flops 523848320 | bytes 1422144 | tf_op jit(solution)/shard_map/zrc,co->zro/dot_general | solution.py:122
  49.4 3.3 %fusion.26 = f32[80,33,129]{0,2,1:T(8,128)S(1)} fusion(f32[80,128]{1,0:T(8,128)S(1)} %bitcast_divide_fusion, f32[33,128]{1,0:T(8,128)S(1)} %select_add_fusion.3, f32[128]{0:T(128)S(1)} %get-tuple-element.69, s32[128]{0:T(128)S(1)} %add_bitcast_fusion, f32[128]{0:T(128)S(1)} %get-tuple-element.67, s32[128]{0:T(128)S(1)} %bitcast.55), kind=kOutput, calls=%fused_computation.48 | convolution fusion | flops 523520640 | bytes 1422144 | tf_op jit(solution)/shard_map/zro,co->zrc/dot_general | solution.py:131
  52.7 3.8 %fusion.17 = f32[80,35,131]{0,2,1:T(8,128)S(1)} fusion(f32[80,33,129]{0,2,1:T(8,128)S(1)} %fusion.26, f32[35,131]{1,0:T(8,128)S(1)} %slice.441, f32[35,131]{1,0:T(8,128)S(1)} %slice.440, f32[35,131]{1,0:T(8,128)S(1)} %slice.439, f32[35,131]{1,0:T(8,128)S(1)} %slice.438, f32[35,131]{1,0:T(8,128)S(1)} %slice.418), kind=kLoop, calls=%fused_computation.33 | loop fusion | flops 3301200 | bytes 2921140 | tf_op jit(solution)/shard_map/add | solution.py:83
  56.6 4.8 %fusion.4 = f32[80,37,133]{0,2,1:T(8,128)S(1)} fusion(f32[80,35,131]{0,2,1:T(8,128)S(1)} %fusion.17, f32[37,133]{1,0:T(8,128)S(1)} %get-tuple-element.64, f32[37,133]{1,0:T(8,128)S(1)} %get-tuple-element.63, f32[37,133]{1,0:T(8,128)S(1)} %get-tuple-element.62, f32[37,133]{1,0:T(8,128)S(1)} %get-tuple-element.61, f32[37,133]{1,0:T(8,128)S(1)} %get-tuple-element.60), kind=kLoop, calls=%fused_computation.10 | loop fusion | flops 3543120 | bytes 3140340 | tf_op jit(solution)/shard_map/add | solution.py:83
  61.4 6.2 %collective-permute-start.4 = (f32[80,2,133]{0,2,1:T(8,128)S(1)}, f32[80,2,133]{0,2,1:T(8,128)S(1)}, u32[]{:S(2)}, u32[]{:S(2)}) collective-permute-start(f32[80,2,133]{0,2,1:T(8,128)S(1)} %slice.444), channel_id=1, source_target_pairs={{1,0},{2,1},{3,2},{4,3},{5,4},{6,5},{7,6},{8,7},{9,8},{10,9},{11,1... | collective-permute-start | bytes 255368 | tf_op jit(solution)/shard_map/ppermute | solution.py:18
  67.8 1.9 %collective-permute-start.5 = (f32[80,3,133]{0,2,1:T(8,128)S(1)}, f32[80,3,133]{0,2,1:T(8,128)S(1)}, u32[]{:S(2)}, u32[]{:S(2)}) collective-permute-start(f32[80,3,133]{0,2,1:T(8,128)S(1)} %slice.446), channel_id=1, source_target_pairs={{0,1},{1,2},{2,3},{3,4},{4,5},{5,6},{6,7},{7,8},{8,9},{9,10},{10,1... | collective-permute-start | bytes 383048 | tf_op jit(solution)/shard_map/ppermute | solution.py:18
  70.2 7.1 %collective-permute-done.5 = f32[80,3,133]{0,2,1:T(8,128)S(1)} collective-permute-done((f32[80,3,133]{0,2,1:T(8,128)S(1)}, f32[80,3,133]{0,2,1:T(8,128)S(1)}, u32[]{:S(2)}, u32[]{:S(2)}) %collective-permute-start.5) | collective-permute-done | bytes 127712 | tf_op jit(solution)/shard_map/ppermute | solution.py:18
  77.4 6.7 %collective-permute-start.6 = (f32[80,32,2]{0,2,1:T(2,128)S(1)}, f32[80,32,2]{0,2,1:T(2,128)S(1)}, u32[]{:S(2)}, u32[]{:S(2)}) collective-permute-start(f32[80,32,2]{0,2,1:T(2,128)S(1)} %slice.449), channel_id=1, source_target_pairs={{16,0},{32,16},{48,32},{64,48},{80,64},{96,80},{112,96},{128,112},... | collective-permute-start | bytes 61448 | tf_op jit(solution)/shard_map/ppermute | solution.py:15
  84.0 0.6 fusion.43
  84.9 1.9 %collective-permute-start.7 = (f32[80,32,3]{0,2,1:T(4,128)S(1)}, f32[80,32,3]{0,2,1:T(4,128)S(1)}, u32[]{:S(2)}, u32[]{:S(2)}) collective-permute-start(f32[80,32,3]{0,2,1:T(4,128)S(1)} %slice.451), channel_id=1, source_target_pairs={{496,0},{0,16},{16,32},{32,48},{48,64},{64,80},{80,96},{96,112},{1... | collective-permute-start | bytes 92168 | tf_op jit(solution)/shard_map/ppermute | solution.py:15
  86.9 6.3 %collective-permute-done.7 = f32[80,32,3]{0,2,1:T(4,128)S(1)} collective-permute-done((f32[80,32,3]{0,2,1:T(4,128)S(1)}, f32[80,32,3]{0,2,1:T(4,128)S(1)}, u32[]{:S(2)}, u32[]{:S(2)}) %collective-permute-start.7) | collective-permute-done | bytes 30752 | tf_op jit(solution)/shard_map/ppermute | solution.py:15
  93.5 1.7 %copy.64 = f32[80,32,128]{2,1,0:T(8,128)} copy(f32[80,32,128]{0,2,1:T(8,128)S(1)} %scatter-add.19) | data formatting | bytes 2621440
  (74 shorter events, 5.6 us)
Async XLA Ops:
  0.6 7.7 %copy-start = (f32[32,128]{1,0:T(8,128)S(1)}, f32[32,128]{1,0:T(8,128)}, u32[]{:S(2)}) copy-start(f32[32,128]{1,0:T(8,128)} %param.18) | copy-start | bytes 49156
  0.6 18.7 %copy-start.3 = (f32[1,2,128]{2,1,0:T(2,128)S(1)}, f32[1,2,128]{2,1,0:T(2,128)}, u32[]{:S(2)}) copy-start(f32[1,2,128]{2,1,0:T(2,128)} %param.24) | copy-start | bytes 3076
  0.7 18.7 %copy-start.5 = (s32[1,128]{1,0:T(1,128)S(1)}, s32[1,128]{1,0:T(1,128)}, u32[]{:S(2)}) copy-start(s32[1,128]{1,0:T(1,128)} %param.22) | copy-start | bytes 1540
  4.3 25.8 %copy-start.4 = (s32[1,128]{1,0:T(1,128)S(1)}, s32[1,128]{1,0:T(1,128)}, u32[]{:S(2)}) copy-start(s32[1,128]{1,0:T(1,128)} %param.23) | copy-start | bytes 1540
  4.5 15.3 %collective-permute-start = (f32[82,32,3]{0,2,1:T(4,128)S(1)}, f32[82,32,3]{0,2,1:T(4,128)S(1)}, u32[]{:S(2)}, u32[]{:S(2)}) collective-permute-start(f32[82,32,3]{0,2,1:T(4,128)S(1)} %pad_maximum_fusion.4), channel_id=1, source_target_pairs={{496,0},{0,16},{16,32},{32,48},{48,64},{64,80},{80,96},{96,112},{1... | collective-permute-start | bytes 94472 | tf_op jit(solution)/shard_map/ppermute | solution.py:15
  8.8 12.4 %collective-permute-start.1 = (f32[82,32,4]{0,2,1:T(4,128)S(1)}, f32[82,32,4]{0,2,1:T(4,128)S(1)}, u32[]{:S(2)}, u32[]{:S(2)}) collective-permute-start(f32[82,32,4]{0,2,1:T(4,128)S(1)} %pad_maximum_fusion.5), channel_id=1, source_target_pairs={{16,0},{32,16},{48,32},{64,48},{80,64},{96,80},{112,96},{128,112},... | collective-permute-start | bytes 125960 | tf_op jit(solution)/shard_map/ppermute | solution.py:15
  22.0 9.7 %collective-permute-start.2 = (f32[82,3,135]{0,2,1:T(8,128)}, f32[82,3,135]{0,2,1:T(8,128)S(1)}, u32[]{:S(2)}, u32[]{:S(2)}) collective-permute-start(f32[82,3,135]{0,2,1:T(8,128)} %pad_maximum_fusion.2), channel_id=1, source_target_pairs={{0,1},{1,2},{2,3},{3,4},{4,5},{5,6},{6,7},{7,8},{8,9},{9,10},{10,1... | collective-permute-start | bytes 398528 | tf_op jit(solution)/shard_map/ppermute | solution.py:18
  24.1 10.1 %collective-permute-start.3 = (f32[82,4,135]{0,2,1:T(8,128)S(1)}, f32[82,4,135]{0,2,1:T(8,128)S(1)}, u32[]{:S(2)}, u32[]{:S(2)}) collective-permute-start(f32[82,4,135]{0,2,1:T(8,128)S(1)} %pad_maximum_fusion.1), channel_id=1, source_target_pairs={{1,0},{2,1},{3,2},{4,3},{5,4},{6,5},{7,6},{8,7},{9,8},{10,9},{11,1... | collective-permute-start | bytes 531368 | tf_op jit(solution)/shard_map/ppermute | solution.py:18
  40.3 9.1 %copy-start.1 = (f32[1,80,128]{2,1,0:T(8,128)S(1)}, f32[1,80,128]{2,1,0:T(8,128)}, u32[]{:S(2)}) copy-start(f32[1,80,128]{2,1,0:T(8,128)} %param.20) | copy-start | bytes 122884
  40.3 9.1 %copy-start.2 = (f32[1,80,128]{2,1,0:T(8,128)S(1)}, f32[1,80,128]{2,1,0:T(8,128)}, u32[]{:S(2)}) copy-start(f32[1,80,128]{2,1,0:T(8,128)} %param.21) | copy-start | bytes 122884
  61.4 8.8 %collective-permute-start.4 = (f32[80,2,133]{0,2,1:T(8,128)S(1)}, f32[80,2,133]{0,2,1:T(8,128)S(1)}, u32[]{:S(2)}, u32[]{:S(2)}) collective-permute-start(f32[80,2,133]{0,2,1:T(8,128)S(1)} %slice.444), channel_id=1, source_target_pairs={{1,0},{2,1},{3,2},{4,3},{5,4},{6,5},{7,6},{8,7},{9,8},{10,9},{11,1... | collective-permute-start | bytes 255368 | tf_op jit(solution)/shard_map/ppermute | solution.py:18
  67.8 9.5 %collective-permute-start.5 = (f32[80,3,133]{0,2,1:T(8,128)S(1)}, f32[80,3,133]{0,2,1:T(8,128)S(1)}, u32[]{:S(2)}, u32[]{:S(2)}) collective-permute-start(f32[80,3,133]{0,2,1:T(8,128)S(1)} %slice.446), channel_id=1, source_target_pairs={{0,1},{1,2},{2,3},{3,4},{4,5},{5,6},{6,7},{7,8},{8,9},{9,10},{10,1... | collective-permute-start | bytes 383048 | tf_op jit(solution)/shard_map/ppermute | solution.py:18
  77.4 9.5 %collective-permute-start.6 = (f32[80,32,2]{0,2,1:T(2,128)S(1)}, f32[80,32,2]{0,2,1:T(2,128)S(1)}, u32[]{:S(2)}, u32[]{:S(2)}) collective-permute-start(f32[80,32,2]{0,2,1:T(2,128)S(1)} %slice.449), channel_id=1, source_target_pairs={{16,0},{32,16},{48,32},{64,48},{80,64},{96,80},{112,96},{128,112},... | collective-permute-start | bytes 61448 | tf_op jit(solution)/shard_map/ppermute | solution.py:15
  84.9 8.3 %collective-permute-start.7 = (f32[80,32,3]{0,2,1:T(4,128)S(1)}, f32[80,32,3]{0,2,1:T(4,128)S(1)}, u32[]{:S(2)}, u32[]{:S(2)}) collective-permute-start(f32[80,32,3]{0,2,1:T(4,128)S(1)} %slice.451), channel_id=1, source_target_pairs={{496,0},{0,16},{16,32},{32,48},{48,64},{64,80},{80,96},{96,112},{1... | collective-permute-start | bytes 92168 | tf_op jit(solution)/shard_map/ppermute | solution.py:15

commit v7 on v5

--- a/solution.py
+++ b/solution.py
@@ -132,9 +132,26 @@
     adjoint = jnp.einsum("zro,co->zrc", spread, wx, precision=hi)
     adjoint = lax.optimization_barrier(adjoint)
 
-    once = diffuse(pad2(adjoint, 2), trim(weights, 1))
-    twice = diffuse(pad2(once, 2), weights)
-    gradient = scatter_halo(twice, rows, cols, GN, GS, GW, GE)
+    spread_a = pad2(adjoint, 2)
+    inner = trim(weights, 1)
+    once_n = diffuse(spread_a[:, 0:4], [w[0:2] for w in inner])
+    twice_n = diffuse(jnp.pad(once_n, ((0, 0), (2, 0), (2, 2))), [w[0:2] for w in weights])
+    once_s = diffuse(spread_a[:, rows : rows + 5], [w[rows : rows + 3] for w in inner])
+    twice_s = diffuse(
+        jnp.pad(once_s, ((0, 0), (0, 2), (2, 2))), [w[rows + 2 : rows + 5] for w in weights]
+    )
+    from_south = neighbour_shift(twice_n, 1, 0)
+    from_north = neighbour_shift(twice_s, -1, 0)
+
+    once = diffuse(spread_a, inner)
+    middle = diffuse(pad2(once, 2)[:, 2 : rows + 4], [w[2 : rows + 2] for w in weights])
+    middle = middle.at[:, rows - GN :, :].add(from_south)
+    middle = middle.at[:, :GS, :].add(from_north)
+    gradient = middle[:, :, GW : GW + cols]
+    from_east = neighbour_shift(middle[:, :, :GW], 0, 1)
+    from_west = neighbour_shift(middle[:, :, GW + cols :], 0, -1)
+    gradient = gradient.at[:, :, cols - GW :].add(from_east)
+    gradient = gradient.at[:, :, :GE].add(from_west)
     return gradient, departure[None]
 
 

time: 93 us -> 90.6 us (0.974)
  waiting for transfers between devices: 17.5 us -> 7.65 us
  local copies, waits for them, and re-layouts: 7.38 us -> 14.3 us
  other arithmetic: 17.8 us -> 21.6 us
  matrix products: 8.95 us -> 6.08 us
    ppermute x4, waiting for transfers between devices: 9.79 us -> 0.01 us  [neighbour_shift(): return lax.ppermute(block, 'lat', pairs)]
    dot_general x1, matrix products: 5.65 us -> 2.79 us  [on_device(): along = jnp.einsum('zrc,co->zro', state, wx, precision=hi)]
    slice x4, local copies, waits for them, and re-layouts: 0.82 us -> 3.46 us  [gather_halo(): middle = jnp.concatenate([west[span], part, east[span]], axis=-1)]
    slice x6 -> x5, local copies, waits for them, and re-layouts: 0.36 us -> 2.49 us  [joined(): return jnp.concatenate([p[window] for p in parts], axis=0)]
    add x4 -> x8, other arithmetic: 13.8 us -> 15.5 us  [diffuse(): result = result + weight * (near - center)]
    slice x4, local copies, waits for them, and re-layouts: 0.62 us -> 1.86 us  [gather_halo(): out.append(jnp.concatenate([north[span], middle, south[span]], axis=-2))]
    concatenate x2, other arithmetic: 0.41 us -> 1.5 us  [gather_halo(): out.append(jnp.concatenate([north[span], middle, south[span]], axis=-2))]
    unnamed x16 -> x25, local copies, waits for them, and re-layouts: 4.21 us -> 4.03 us
  transfers between devices with their start and end apart: 8 -> 8, of which waited for: 6 -> 2; matrix products, arithmetic and copies ran while one was open for 3% -> 19% of each run, Pallas kernels for 0% -> 0%
where the time goes in v7:
time: 90.6 us; the launch traced here: 90.1 us
  starting transfers between devices  38.6 us (43%)
  other arithmetic  21.6 us (24%)
  local copies, waits for them, and re-layouts  14.3 us (16%)
  waiting for transfers between devices  7.65 us (8%)
  matrix products  6.08 us (7%)
  between operations  1.9 us (2%)
    ppermute x4, starting transfers between devices, neighbour_shift(): return lax.ppermute(block, 'lon', pairs)  22.6 us
    ppermute x4, starting transfers between devices, neighbour_shift(): return lax.ppermute(block, 'lat', pairs)  15.9 us
    add x8, other arithmetic, diffuse(): result = result + weight * (near - center)  15.5 us
    ppermute x4, waiting for transfers between devices, neighbour_shift(): return lax.ppermute(block, 'lon', pairs)  7.64 us
    unnamed x25, local copies, waits for them, and re-layouts  4.03 us
    slice x4, local copies, waits for them, and re-layouts, gather_halo(): middle = jnp.concatenate([west[span], part, east[span]], axis=-1)  3.46 us
    dot_general x1, matrix products, on_device(): adjoint = jnp.einsum('zro,co->zrc', spread, wx, precision=hi)  3.29 us
    dot_general x1, matrix products, on_device(): along = jnp.einsum('zrc,co->zro', state, wx, precision=hi)  2.79 us
  transfers between devices with their start and end apart: 8, of which 2 were waited for; matrix products, arithmetic and copies ran while one was open for 19% of the time, Pallas kernels for 0%

profile of v7, /device:TPU:6, one launch (start us, length us, event | category | flops | bytes accessed | tf_op | source)
XLA Modules:
  0.0 90.1 jit_solution(14181778797719242263)
XLA Ops:
  0.7 0.8 convert_bitcast_fusion
  2.6 1.7 %slice.445 = f32[80,32,3]{2,1,0:T(8,128)S(1)} slice(f32[80,32,128]{2,1,0:T(8,128)} %param.17), slice={[0:80], [0:32], [125:128]} | slice | bytes 61440 | tf_op jit(solution)/shard_map/slice | solution.py:33
  5.2 3.8 %collective-permute-start = (f32[82,32,3]{0,1,2:T(8,128)S(1)}, f32[82,32,3]{0,1,2:T(8,128)S(1)}, u32[]{:S(2)}, u32[]{:S(2)}) collective-permute-start(f32[82,32,3]{0,1,2:T(8,128)S(1)} %pad_maximum_fusion.5), channel_id=1, source_target_pairs={{496,0},{0,16},{16,32},{32,48},{48,64},{64,80},{80,96},{96,112},{1... | collective-permute-start | bytes 94472 | tf_op jit(solution)/shard_map/ppermute | solution.py:15
  10.3 10.5 %collective-permute-start.1 = (f32[82,32,4]{0,1,2:T(8,128)S(1)}, f32[82,32,4]{0,1,2:T(8,128)S(1)}, u32[]{:S(2)}, u32[]{:S(2)}) collective-permute-start(f32[82,32,4]{0,1,2:T(8,128)S(1)} %pad_maximum_fusion.4), channel_id=1, source_target_pairs={{16,0},{32,16},{48,32},{64,48},{80,64},{96,80},{112,96},{128,112},... | collective-permute-start | bytes 125960 | tf_op jit(solution)/shard_map/ppermute | solution.py:15
  21.4 1.3 %collective-permute-done.1 = f32[82,32,4]{0,1,2:T(8,128)S(1)} collective-permute-done((f32[82,32,4]{0,1,2:T(8,128)S(1)}, f32[82,32,4]{0,1,2:T(8,128)S(1)}, u32[]{:S(2)}, u32[]{:S(2)}) %collective-permute-start.1) | collective-permute-done | bytes 42016 | tf_op jit(solution)/shard_map/ppermute | solution.py:15
  23.2 1.9 %collective-permute-start.2 = (f32[82,3,135]{2,1,0:T(4,128)S(1)}, f32[82,3,135]{2,1,0:T(4,128)}, u32[]{:S(2)}, u32[]{:S(2)}) collective-permute-start(f32[82,3,135]{2,1,0:T(4,128)S(1)} %pad_maximum_fusion.2), channel_id=1, source_target_pairs={{0,1},{1,2},{2,3},{3,4},{4,5},{5,6},{6,7},{7,8},{8,9},{9,10},{10,1... | collective-permute-start | bytes 398528 | tf_op jit(solution)/shard_map/ppermute | solution.py:18
  25.3 1.1 %fusion.42 = f32[82,4,135]{2,1,0:T(4,128)} fusion(f32[1,32,128]{2,1,0:T(8,128)S(1)} %convert_bitcast_fusion, f32[1,32,128]{2,1,0:T(8,128)S(1)} %bitcast.47, f32[82,4,4]{2,1,0:T(4,128)S(1)} %copy.67, f32[80,4,128]{2,1,0:T(4,128)S(1)} %slice.457, f32[82,4,3]{2,1,0:T(4,128)S(1)} %copy.66), kind=kLoop, calls=%fused_computation.73 | loop fusion | flops 177120 | bytes 382912 | tf_op jit(solution)/shard_map/concatenate | solution.py:40
  26.4 6.0 %collective-permute-start.3 = (f32[82,4,135]{2,1,0:T(4,128)}, f32[82,4,135]{2,1,0:T(4,128)S(1)}, u32[]{:S(2)}, u32[]{:S(2)}) collective-permute-start(f32[82,4,135]{2,1,0:T(4,128)} %fusion.42), channel_id=1, source_target_pairs={{1,0},{2,1},{3,2},{4,3},{5,4},{6,5},{7,6},{8,7},{9,8},{10,9},{11,1... | collective-permute-start | bytes 531368 | tf_op jit(solution)/shard_map/ppermute | solution.py:18
  34.0 1.2 %copy.64 = f32[80,32,3]{2,1,0:T(8,128)S(1)} copy(f32[80,32,3]{0,1,2:T(8,128)S(1)} %bitcast.50) | data formatting | bytes 61440 | tf_op jit(solution)/shard_map/slice | solution.py:48
  35.7 2.1 %copy.65 = f32[80,32,4]{2,1,0:T(8,128)} copy(f32[80,32,4]{0,1,2:T(8,128)S(1)} %bitcast.49) | data formatting | bytes 81920 | tf_op jit(solution)/shard_map/slice | solution.py:48
  38.5 1.0 %slice.561 = f32[80,3,135]{2,1,0:T(4,128)S(1)} slice(f32[82,3,135]{2,1,0:T(4,128)} %collective-permute-done.2), slice={[0:80], [0:3], [0:135]} | slice | bytes 259200 | tf_op jit(solution)/shard_map/slice | solution.py:49
  41.3 1.4 %pad_maximum_fusion = f32[80,39,135]{2,1,0:T(8,128)S(1)} fusion(f32[80,4,135]{2,1,0:T(4,128)S(1)} %slice.566, f32[80,32,4]{2,1,0:T(8,128)S(1)} %copy-done.1, f32[80,32,128]{2,1,0:T(8,128)S(1)} %copy-done, f32[80,32,3]{2,1,0:T(8,128)S(1)} %copy.64, f32[80,3,135]{2,1,0:T(4,128)S(1)} %slice.561), kind=kLoop, calls=%fused_computation.24 | loop fusion | flops 1684800 | bytes 3369600 | tf_op jit(solution)/shard_map/concatenate | solution.py:49
  42.7 3.8 %fusion.9 = f32[80,37,133]{2,1,0:T(8,128)S(1)} fusion(f32[80,39,135]{2,1,0:T(8,128)S(1)} %pad_maximum_fusion, f32[37,133]{1,0:T(8,128)S(1)} %get-tuple-element.59, f32[37,133]{1,0:T(8,128)S(1)} %get-tuple-element.57, f32[37,133]{1,0:T(8,128)S(1)} %get-tuple-element.58, f32[37,133]{1,0:T(8,128)S(1)} %get-tuple-element.56), kind=kLoop, calls=%fused_computation.14 | loop fusion | flops 4724160 | bytes 9527056 | tf_op jit(solution)/shard_map/add | solution.py:84
  46.4 4.4 %fusion.1 = f32[80,33,129]{2,1,0:T(8,128)S(1)} fusion(f32[80,37,133]{2,1,0:T(8,128)S(1)} %fusion.9, f32[33,129]{1,0:T(8,128)S(1)} %slice.595, f32[33,129]{1,0:T(8,128)S(1)} %slice.593, f32[33,129]{1,0:T(8,128)S(1)} %slice.591, f32[33,129]{1,0:T(8,128)S(1)} %slice.589), kind=kLoop, calls=%fused_computation.2 | loop fusion | flops 4086720 | bytes 8241552 | tf_op jit(solution)/shard_map/add | solution.py:84
  50.9 2.8 %fusion.35 = f32[80,128]{1,0:T(8,128)S(1)} fusion(f32[80,33,129]{2,1,0:T(8,128)S(1)} %fusion.1, f32[33,128]{1,0:T(8,128)S(1)} %select_add_fusion.3, f32[128]{0:T(128)S(1)} %get-tuple-element.64, s32[128]{0:T(128)S(1)} %copy-done.8, f32[128]{0:T(128)S(1)} %get-tuple-element.62, s32[128]{0:T(128)S(1)} %bitcast.51), kind=kOutput, calls=%fused_computation.58 | convolution fusion | flops 523848320 | bytes 1422144 | tf_op jit(solution)/shard_map/zrc,co->zro/dot_general | solution.py:123
  53.8 3.3 %fusion.33 = f32[80,33,129]{0,2,1:T(8,128)S(1)} fusion(f32[80,128]{1,0:T(8,128)S(1)} %bitcast_divide_fusion, f32[33,128]{1,0:T(8,128)S(1)} %select_add_fusion.3, f32[128]{0:T(128)S(1)} %get-tuple-element.64, s32[128]{0:T(128)S(1)} %copy-done.8, f32[128]{0:T(128)S(1)} %get-tuple-element.62, s32[128]{0:T(128)S(1)} %bitcast.52), kind=kOutput, calls=%fused_computation.56 | convolution fusion | flops 523520640 | bytes 1422144 | tf_op jit(solution)/shard_map/zro,co->zrc/dot_general | solution.py:132
  57.6 1.9 %collective-permute-start.5 = (f32[80,3,133]{0,2,1:T(8,128)S(1)}, f32[80,3,133]{0,2,1:T(8,128)S(1)}, u32[]{:S(2)}, u32[]{:S(2)}) collective-permute-start(f32[80,3,133]{0,2,1:T(8,128)S(1)} %fusion.48), channel_id=1, source_target_pairs={{0,1},{1,2},{2,3},{3,4},{4,5},{5,6},{6,7},{7,8},{8,9},{9,10},{10,1... | collective-permute-start | bytes 383048 | tf_op jit(solution)/shard_map/ppermute | solution.py:18
  60.0 6.0 %collective-permute-start.4 = (f32[80,2,133]{0,2,1:T(8,128)S(1)}, f32[80,2,133]{0,2,1:T(8,128)S(1)}, u32[]{:S(2)}, u32[]{:S(2)}) collective-permute-start(f32[80,2,133]{0,2,1:T(8,128)S(1)} %fusion.76), channel_id=1, source_target_pairs={{1,0},{2,1},{3,2},{4,3},{5,4},{6,5},{7,6},{8,7},{9,8},{10,9},{11,1... | collective-permute-start | bytes 255368 | tf_op jit(solution)/shard_map/ppermute | solution.py:18
  66.1 3.2 %multiply_add_fusion = f32[80,35,131]{0,2,1:T(8,128)S(1)} fusion(f32[80,33,129]{0,2,1:T(8,128)S(1)} %fusion.33, f32[35,131]{1,0:T(8,128)S(1)} %slice.600, f32[35,131]{1,0:T(8,128)S(1)} %slice.599, f32[35,131]{1,0:T(8,128)S(1)} %slice.598, f32[35,131]{1,0:T(8,128)S(1)} %slice.597), kind=kLoop, calls=%fused_computation.32 | loop fusion | flops 4401600 | bytes 2902800 | tf_op jit(solution)/shard_map/add | solution.py:84
  69.3 3.1 %fusion.23 = f32[80,32,133]{0,2,1:T(8,128)S(1)} fusion(f32[80,35,131]{0,2,1:T(8,128)S(1)} %multiply_add_fusion, f32[32,133]{1,0:T(8,128)S(1)} %slice.604, f32[32,133]{1,0:T(8,128)S(1)} %slice.603, f32[32,133]{1,0:T(8,128)S(1)} %slice.602, f32[32,133]{1,0:T(8,128)S(1)} %slice.601), kind=kLoop, calls=%fused_computation.48 | loop fusion | flops 4085760 | bytes 2897216 | tf_op jit(solution)/shard_map/add | solution.py:84
  72.5 6.4 %collective-permute-start.6 = (f32[80,32,2]{0,2,1:T(2,128)S(1)}, f32[80,32,2]{0,2,1:T(2,128)S(1)}, u32[]{:S(2)}, u32[]{:S(2)}) collective-permute-start(f32[80,32,2]{0,2,1:T(2,128)S(1)} %slice.625), channel_id=1, source_target_pairs={{16,0},{32,16},{48,32},{64,48},{80,64},{96,80},{112,96},{128,112},... | collective-permute-start | bytes 61448 | tf_op jit(solution)/shard_map/ppermute | solution.py:15
  79.8 1.9 %collective-permute-start.7 = (f32[80,32,3]{0,2,1:T(4,128)S(1)}, f32[80,32,3]{0,2,1:T(4,128)S(1)}, u32[]{:S(2)}, u32[]{:S(2)}) collective-permute-start(f32[80,32,3]{0,2,1:T(4,128)S(1)} %slice.627), channel_id=1, source_target_pairs={{496,0},{0,16},{16,32},{32,48},{48,64},{64,80},{80,96},{96,112},{1... | collective-permute-start | bytes 92168 | tf_op jit(solution)/shard_map/ppermute | solution.py:15
  81.8 6.3 %collective-permute-done.7 = f32[80,32,3]{0,2,1:T(4,128)S(1)} collective-permute-done((f32[80,32,3]{0,2,1:T(4,128)S(1)}, f32[80,32,3]{0,2,1:T(4,128)S(1)}, u32[]{:S(2)}, u32[]{:S(2)}) %collective-permute-start.7) | collective-permute-done | bytes 30752 | tf_op jit(solution)/shard_map/ppermute | solution.py:15
  88.3 1.7 %copy.71 = f32[80,32,128]{2,1,0:T(8,128)} copy(f32[80,32,128]{0,2,1:T(8,128)S(1)} %scatter-add.19) | data formatting | bytes 2621440
  (104 shorter events, 10.4 us)
Async XLA Ops:
  0.6 8.4 %copy-start.2 = (f32[32,128]{1,0:T(8,128)S(1)}, f32[32,128]{1,0:T(8,128)}, u32[]{:S(2)}) copy-start(f32[32,128]{1,0:T(8,128)} %param.18) | copy-start | bytes 49156
  0.6 8.8 %copy-start = (f32[80,32,128]{2,1,0:T(8,128)S(1)}, f32[80,32,128]{2,1,0:T(8,128)}, u32[]{:S(2)}) copy-start(f32[80,32,128]{2,1,0:T(8,128)} %param.17) | copy-start | bytes 3932164
  2.6 18.3 %copy-start.5 = (f32[1,2,128]{2,1,0:T(2,128)S(1)}, f32[1,2,128]{2,1,0:T(2,128)}, u32[]{:S(2)}) copy-start(f32[1,2,128]{2,1,0:T(2,128)} %param.24) | copy-start | bytes 3076
  2.6 18.3 %copy-start.9 = (s32[1,128]{1,0:T(1,128)S(1)}, s32[1,128]{1,0:T(1,128)}, u32[]{:S(2)}) copy-start(s32[1,128]{1,0:T(1,128)} %param.22) | copy-start | bytes 1540
  5.2 15.8 %collective-permute-start = (f32[82,32,3]{0,1,2:T(8,128)S(1)}, f32[82,32,3]{0,1,2:T(8,128)S(1)}, u32[]{:S(2)}, u32[]{:S(2)}) collective-permute-start(f32[82,32,3]{0,1,2:T(8,128)S(1)} %pad_maximum_fusion.5), channel_id=1, source_target_pairs={{496,0},{0,16},{16,32},{32,48},{48,64},{64,80},{80,96},{96,112},{1... | collective-permute-start | bytes 94472 | tf_op jit(solution)/shard_map/ppermute | solution.py:15
  9.1 23.4 %copy-start.6 = (s32[1,128]{1,0:T(1,128)S(1)}, s32[1,128]{1,0:T(1,128)}, u32[]{:S(2)}) copy-start(s32[1,128]{1,0:T(1,128)} %param.23) | copy-start | bytes 1540
  10.3 12.4 %collective-permute-start.1 = (f32[82,32,4]{0,1,2:T(8,128)S(1)}, f32[82,32,4]{0,1,2:T(8,128)S(1)}, u32[]{:S(2)}, u32[]{:S(2)}) collective-permute-start(f32[82,32,4]{0,1,2:T(8,128)S(1)} %pad_maximum_fusion.4), channel_id=1, source_target_pairs={{16,0},{32,16},{48,32},{64,48},{80,64},{96,80},{112,96},{128,112},... | collective-permute-start | bytes 125960 | tf_op jit(solution)/shard_map/ppermute | solution.py:15
  23.2 14.5 %collective-permute-start.2 = (f32[82,3,135]{2,1,0:T(4,128)S(1)}, f32[82,3,135]{2,1,0:T(4,128)}, u32[]{:S(2)}, u32[]{:S(2)}) collective-permute-start(f32[82,3,135]{2,1,0:T(4,128)S(1)} %pad_maximum_fusion.2), channel_id=1, source_target_pairs={{0,1},{1,2},{2,3},{3,4},{4,5},{5,6},{6,7},{7,8},{8,9},{9,10},{10,1... | collective-permute-start | bytes 398528 | tf_op jit(solution)/shard_map/ppermute | solution.py:18
  26.4 13.2 %collective-permute-start.3 = (f32[82,4,135]{2,1,0:T(4,128)}, f32[82,4,135]{2,1,0:T(4,128)S(1)}, u32[]{:S(2)}, u32[]{:S(2)}) collective-permute-start(f32[82,4,135]{2,1,0:T(4,128)} %fusion.42), channel_id=1, source_target_pairs={{1,0},{2,1},{3,2},{4,3},{5,4},{6,5},{7,6},{8,7},{9,8},{10,9},{11,1... | collective-permute-start | bytes 531368 | tf_op jit(solution)/shard_map/ppermute | solution.py:18
  37.7 3.5 %copy-start.1 = (f32[80,32,4]{2,1,0:T(8,128)S(1)}, f32[80,32,4]{2,1,0:T(8,128)}, u32[]{:S(2)}) copy-start(f32[80,32,4]{2,1,0:T(8,128)} %copy.65) | copy-start | bytes 122884
  46.4 4.5 %copy-start.7 = (s32[1,128]{1,0:T(1,128)S(1)}, s32[1,128]{1,0:T(1,128)}, u32[]{:S(2)}) copy-start(s32[1,128]{1,0:T(1,128)} %param.23) | copy-start | bytes 1540
  46.4 4.5 %copy-start.8 = (s32[128]{0:T(128)S(1)}, s32[128]{0:T(128)}, u32[]{:S(2)}) copy-start(s32[128]{0:T(128)} %add_bitcast_fusion) | copy-start | bytes 1540
  50.9 2.8 %copy-start.3 = (f32[1,80,128]{2,1,0:T(8,128)S(1)}, f32[1,80,128]{2,1,0:T(8,128)}, u32[]{:S(2)}) copy-start(f32[1,80,128]{2,1,0:T(8,128)} %param.20) | copy-start | bytes 122884
  50.9 2.8 %copy-start.4 = (f32[1,80,128]{2,1,0:T(8,128)S(1)}, f32[1,80,128]{2,1,0:T(8,128)}, u32[]{:S(2)}) copy-start(f32[1,80,128]{2,1,0:T(8,128)} %param.21) | copy-start | bytes 122884
  57.6 14.8 %collective-permute-start.5 = (f32[80,3,133]{0,2,1:T(8,128)S(1)}, f32[80,3,133]{0,2,1:T(8,128)S(1)}, u32[]{:S(2)}, u32[]{:S(2)}) collective-permute-start(f32[80,3,133]{0,2,1:T(8,128)S(1)} %fusion.48), channel_id=1, source_target_pairs={{0,1},{1,2},{2,3},{3,4},{4,5},{5,6},{6,7},{7,8},{8,9},{9,10},{10,1... | collective-permute-start | bytes 383048 | tf_op jit(solution)/shard_map/ppermute | solution.py:18
  60.0 12.4 %collective-permute-start.4 = (f32[80,2,133]{0,2,1:T(8,128)S(1)}, f32[80,2,133]{0,2,1:T(8,128)S(1)}, u32[]{:S(2)}, u32[]{:S(2)}) collective-permute-start(f32[80,2,133]{0,2,1:T(8,128)S(1)} %fusion.76), channel_id=1, source_target_pairs={{1,0},{2,1},{3,2},{4,3},{5,4},{6,5},{7,6},{8,7},{9,8},{10,9},{11,1... | collective-permute-start | bytes 255368 | tf_op jit(solution)/shard_map/ppermute | solution.py:18
  72.5 9.2 %collective-permute-start.6 = (f32[80,32,2]{0,2,1:T(2,128)S(1)}, f32[80,32,2]{0,2,1:T(2,128)S(1)}, u32[]{:S(2)}, u32[]{:S(2)}) collective-permute-start(f32[80,32,2]{0,2,1:T(2,128)S(1)} %slice.625), channel_id=1, source_target_pairs={{16,0},{32,16},{48,32},{64,48},{80,64},{96,80},{112,96},{128,112},... | collective-permute-start | bytes 61448 | tf_op jit(solution)/shard_map/ppermute | solution.py:15
  79.8 8.3 %collective-permute-start.7 = (f32[80,32,3]{0,2,1:T(4,128)S(1)}, f32[80,32,3]{0,2,1:T(4,128)S(1)}, u32[]{:S(2)}, u32[]{:S(2)}) collective-permute-start(f32[80,32,3]{0,2,1:T(4,128)S(1)} %slice.627), channel_id=1, source_target_pairs={{496,0},{0,16},{16,32},{32,48},{48,64},{64,80},{80,96},{96,112},{1... | collective-permute-start | bytes 92168 | tf_op jit(solution)/shard_map/ppermute | solution.py:15

commit v8 on v7

--- a/solution.py
+++ b/solution.py
@@ -1,6 +1,7 @@
 import jax
 import jax.numpy as jnp
 from jax import lax
+from jax.experimental.layout import Layout, with_layout_constraint
 from jax.sharding import PartitionSpec as P
 
 HN, HS, HW, HE = 3, 4, 3, 4
@@ -99,6 +100,7 @@
     channels, rows, cols = control.shape
     coeff = jnp.stack([diffusivity, land_mask.astype(jnp.float32)])
     field, coeff = gather_halo([control, coeff], HN, HS, HW, HE)
+    field = with_layout_constraint(field, Layout(major_to_minor=(1, 2, 0)))
     weights = edge_weights(coeff[0], coeff[1])
 
     once = diffuse(field, weights)

time: 90.6 us -> 85.6 us (0.945)
  local copies, waits for them, and re-layouts: 14.3 us -> 7.83 us
  other arithmetic: 21.6 us -> 17.8 us
  matrix products: 6.08 us -> 8.94 us
  waiting for transfers between devices: 7.65 us -> 9.92 us
    dot_general x1, matrix products: 2.79 us -> 5.65 us  [on_device(): along = jnp.einsum('zrc,co->zro', state, wx, precision=hi)]
    slice x4, local copies, waits for them, and re-layouts: 3.46 us -> 0.82 us  [gather_halo(): middle = jnp.concatenate([west[span], part, east[span]], axis=-1)]
    ppermute x4, waiting for transfers between devices: 0.01 us -> 2.22 us  [neighbour_shift(): return lax.ppermute(block, 'lat', pairs)]
    slice x5 -> x6, local copies, waits for them, and re-layouts: 2.49 us -> 0.36 us  [joined(): return jnp.concatenate([p[window] for p in parts], axis=0)]
    add x8, other arithmetic: 15.5 us -> 13.7 us  [diffuse(): result = result + weight * (near - center)]
    slice x4, local copies, waits for them, and re-layouts: 1.86 us -> 0.62 us  [gather_halo(): out.append(jnp.concatenate([north[span], middle, south[span]], axis=-2))]
    concatenate x2, other arithmetic: 1.5 us -> 0.4 us  [gather_halo(): out.append(jnp.concatenate([north[span], middle, south[span]], axis=-2))]
    concatenate x1, other arithmetic: 1.06 us -> 0.14 us  [gather_halo(): jnp.concatenate([west[..., :hs, :], joined((Ellipsis, slice(0, hs), slice...]
  transfers between devices with their start and end apart: 8 -> 8, of which waited for: 2 -> 4; matrix products, arithmetic and copies ran while one was open for 19% -> 11% of each run, Pallas kernels for 0% -> 0%
where the time goes in v8:
time: 85.6 us; the launch traced here: 85.1 us
  starting transfers between devices  38.7 us (45%)
  other arithmetic  17.8 us (21%)
  waiting for transfers between devices  9.92 us (12%)
  matrix products  8.94 us (10%)
  local copies, waits for them, and re-layouts  7.83 us (9%)
  between operations  1.9 us (2%)
    ppermute x4, starting transfers between devices, neighbour_shift(): return lax.ppermute(block, 'lon', pairs)  22.6 us
    ppermute x4, starting transfers between devices, neighbour_shift(): return lax.ppermute(block, 'lat', pairs)  16.1 us
    add x8, other arithmetic, diffuse(): result = result + weight * (near - center)  13.7 us
    ppermute x4, waiting for transfers between devices, neighbour_shift(): return lax.ppermute(block, 'lon', pairs)  7.7 us
    dot_general x1, matrix products, on_device(): along = jnp.einsum('zrc,co->zro', state, wx, precision=hi)  5.65 us
    unnamed x16, local copies, waits for them, and re-layouts  4.21 us
    dot_general x1, matrix products, on_device(): adjoint = jnp.einsum('zro,co->zrc', spread, wx, precision=hi)  3.29 us
    ppermute x4, waiting for transfers between devices, neighbour_shift(): return lax.ppermute(block, 'lat', pairs)  2.22 us
  transfers between devices with their start and end apart: 8, of which 4 were waited for; matrix products, arithmetic and copies ran while one was open for 11% of the time, Pallas kernels for 0%

profile of v8, /device:TPU:6, one launch (start us, length us, event | category | flops | bytes accessed | tf_op | source)
XLA Modules:
  0.0 85.1 jit_solution(15451805663357282929)
XLA Ops:
  0.7 0.7 convert_bitcast_fusion
  1.4 0.8 fusion.95
  2.5 1.8 %copy.51 = f32[80,32,128]{0,2,1:T(8,128)S(1)} copy(f32[80,32,128]{2,1,0:T(8,128)} %param.17) | data formatting | bytes 2621440 | tf_op args[0]
  4.5 3.8 %collective-permute-start = (f32[82,32,3]{0,2,1:T(4,128)S(1)}, f32[82,32,3]{0,2,1:T(4,128)S(1)}, u32[]{:S(2)}, u32[]{:S(2)}) collective-permute-start(f32[82,32,3]{0,2,1:T(4,128)S(1)} %pad_maximum_fusion.4), channel_id=1, source_target_pairs={{496,0},{0,16},{16,32},{32,48},{48,64},{64,80},{80,96},{96,112},{1... | collective-permute-start | bytes 94472 | tf_op jit(solution)/shard_map/ppermute | solution.py:16
  8.8 10.5 %collective-permute-start.1 = (f32[82,32,4]{0,2,1:T(4,128)S(1)}, f32[82,32,4]{0,2,1:T(4,128)S(1)}, u32[]{:S(2)}, u32[]{:S(2)}) collective-permute-start(f32[82,32,4]{0,2,1:T(4,128)S(1)} %pad_maximum_fusion.5), channel_id=1, source_target_pairs={{16,0},{32,16},{48,32},{64,48},{80,64},{96,80},{112,96},{128,112},... | collective-permute-start | bytes 125960 | tf_op jit(solution)/shard_map/ppermute | solution.py:16
  19.8 1.4 %collective-permute-done.1 = f32[82,32,4]{0,2,1:T(4,128)S(1)} collective-permute-done((f32[82,32,4]{0,2,1:T(4,128)S(1)}, f32[82,32,4]{0,2,1:T(4,128)S(1)}, u32[]{:S(2)}, u32[]{:S(2)}) %collective-permute-start.1) | collective-permute-done | bytes 42016 | tf_op jit(solution)/shard_map/ppermute | solution.py:16
  21.2 0.8 pad_maximum_fusion.2
  22.0 1.9 %collective-permute-start.2 = (f32[82,3,135]{0,2,1:T(8,128)}, f32[82,3,135]{0,2,1:T(8,128)S(1)}, u32[]{:S(2)}, u32[]{:S(2)}) collective-permute-start(f32[82,3,135]{0,2,1:T(8,128)} %pad_maximum_fusion.2), channel_id=1, source_target_pairs={{0,1},{1,2},{2,3},{3,4},{4,5},{5,6},{6,7},{7,8},{8,9},{9,10},{10,1... | collective-permute-start | bytes 398528 | tf_op jit(solution)/shard_map/ppermute | solution.py:19
  24.1 6.0 %collective-permute-start.3 = (f32[82,4,135]{0,2,1:T(8,128)S(1)}, f32[82,4,135]{0,2,1:T(8,128)S(1)}, u32[]{:S(2)}, u32[]{:S(2)}) collective-permute-start(f32[82,4,135]{0,2,1:T(8,128)S(1)} %pad_maximum_fusion.1), channel_id=1, source_target_pairs={{1,0},{2,1},{3,2},{4,3},{5,4},{6,5},{7,6},{8,7},{9,8},{10,9},{11,1... | collective-permute-start | bytes 531368 | tf_op jit(solution)/shard_map/ppermute | solution.py:19
  31.3 0.3 copy.61
  32.0 2.1 %collective-permute-done.3 = f32[82,4,135]{0,2,1:T(8,128)S(1)} collective-permute-done((f32[82,4,135]{0,2,1:T(8,128)S(1)}, f32[82,4,135]{0,2,1:T(8,128)S(1)}, u32[]{:S(2)}, u32[]{:S(2)}) %collective-permute-start.3) | collective-permute-done | bytes 177152 | tf_op jit(solution)/shard_map/ppermute | solution.py:19
  36.4 3.6 %fusion.1 = f32[80,37,133]{0,2,1:T(8,128)S(1)} fusion(f32[80,39,135]{0,2,1:T(8,128)S(1)} %pad_maximum_fusion, f32[37,133]{1,0:T(8,128)S(1)} %get-tuple-element.63, f32[37,133]{1,0:T(8,128)S(1)} %get-tuple-element.61, f32[37,133]{1,0:T(8,128)S(1)} %get-tuple-element.62, f32[37,133]{1,0:T(8,128)S(1)} %get-tuple-element.60), kind=kLoop, calls=%fused_computation.8 | loop fusion | flops 4724160 | bytes 9527056 | tf_op jit(solution)/shard_map/add | solution.py:85
  40.1 2.8 %fusion.9 = f32[80,33,129]{0,2,1:T(8,128)S(1)} fusion(f32[80,37,133]{0,2,1:T(8,128)S(1)} %fusion.1, f32[33,129]{1,0:T(8,128)S(1)} %slice.599, f32[33,129]{1,0:T(8,128)S(1)} %slice.597, f32[33,129]{1,0:T(8,128)S(1)} %slice.595, f32[33,129]{1,0:T(8,128)S(1)} %slice.593), kind=kLoop, calls=%fused_computation.31 | loop fusion | flops 4086720 | bytes 8241552 | tf_op jit(solution)/shard_map/add | solution.py:85
  42.9 5.6 %fusion.30 = f32[80,128]{1,0:T(8,128)S(1)} fusion(f32[80,33,129]{0,2,1:T(8,128)S(1)} %fusion.9, f32[33,128]{1,0:T(8,128)S(1)} %select_add_fusion.3, f32[128]{0:T(128)S(1)} %get-tuple-element.68, s32[128]{0:T(128)S(1)} %add_bitcast_fusion, f32[128]{0:T(128)S(1)} %get-tuple-element.66, s32[128]{0:T(128)S(1)} %bitcast.54), kind=kOutput, calls=%fused_computation.56 | convolution fusion | flops 523848320 | bytes 1422144 | tf_op jit(solution)/shard_map/zrc,co->zro/dot_general | solution.py:125
  48.6 3.3 %fusion.28 = f32[80,33,129]{0,2,1:T(8,128)S(1)} fusion(f32[80,128]{1,0:T(8,128)S(1)} %bitcast_divide_fusion, f32[33,128]{1,0:T(8,128)S(1)} %select_add_fusion.3, f32[128]{0:T(128)S(1)} %get-tuple-element.68, s32[128]{0:T(128)S(1)} %add_bitcast_fusion, f32[128]{0:T(128)S(1)} %get-tuple-element.66, s32[128]{0:T(128)S(1)} %bitcast.55), kind=kOutput, calls=%fused_computation.54 | convolution fusion | flops 523520640 | bytes 1422144 | tf_op jit(solution)/shard_map/zro,co->zrc/dot_general | solution.py:134
  52.5 4.2 %collective-permute-start.5 = (f32[80,3,133]{0,2,1:T(8,128)S(1)}, f32[80,3,133]{0,2,1:T(8,128)S(1)}, u32[]{:S(2)}, u32[]{:S(2)}) collective-permute-start(f32[80,3,133]{0,2,1:T(8,128)S(1)} %fusion.38), channel_id=1, source_target_pairs={{0,1},{1,2},{2,3},{3,4},{4,5},{5,6},{6,7},{7,8},{8,9},{9,10},{10,1... | collective-permute-start | bytes 383048 | tf_op jit(solution)/shard_map/ppermute | solution.py:19
  57.1 4.0 %collective-permute-start.4 = (f32[80,2,133]{0,2,1:T(8,128)S(1)}, f32[80,2,133]{0,2,1:T(8,128)S(1)}, u32[]{:S(2)}, u32[]{:S(2)}) collective-permute-start(f32[80,2,133]{0,2,1:T(8,128)S(1)} %fusion.66), channel_id=1, source_target_pairs={{1,0},{2,1},{3,2},{4,3},{5,4},{6,5},{7,6},{8,7},{9,8},{10,9},{11,1... | collective-permute-start | bytes 255368 | tf_op jit(solution)/shard_map/ppermute | solution.py:19
  61.1 3.2 %multiply_add_fusion = f32[80,35,131]{0,2,1:T(8,128)S(1)} fusion(f32[80,33,129]{0,2,1:T(8,128)S(1)} %fusion.28, f32[35,131]{1,0:T(8,128)S(1)} %slice.604, f32[35,131]{1,0:T(8,128)S(1)} %slice.603, f32[35,131]{1,0:T(8,128)S(1)} %slice.602, f32[35,131]{1,0:T(8,128)S(1)} %slice.601), kind=kLoop, calls=%fused_computation.18 | loop fusion | flops 4401600 | bytes 2902800 | tf_op jit(solution)/shard_map/add | solution.py:85
  64.3 3.0 %fusion.21 = f32[80,32,133]{0,2,1:T(8,128)S(1)} fusion(f32[80,35,131]{0,2,1:T(8,128)S(1)} %multiply_add_fusion, f32[32,133]{1,0:T(8,128)S(1)} %slice.608, f32[32,133]{1,0:T(8,128)S(1)} %slice.607, f32[32,133]{1,0:T(8,128)S(1)} %slice.606, f32[32,133]{1,0:T(8,128)S(1)} %slice.605), kind=kLoop, calls=%fused_computation.46 | loop fusion | flops 4085760 | bytes 2897216 | tf_op jit(solution)/shard_map/add | solution.py:85
  67.5 6.4 %collective-permute-start.6 = (f32[80,32,2]{0,2,1:T(2,128)S(1)}, f32[80,32,2]{0,2,1:T(2,128)S(1)}, u32[]{:S(2)}, u32[]{:S(2)}) collective-permute-start(f32[80,32,2]{0,2,1:T(2,128)S(1)} %slice.629), channel_id=1, source_target_pairs={{16,0},{32,16},{48,32},{64,48},{80,64},{96,80},{112,96},{128,112},... | collective-permute-start | bytes 61448 | tf_op jit(solution)/shard_map/ppermute | solution.py:16
  73.9 0.6 fusion.82
  74.8 1.9 %collective-permute-start.7 = (f32[80,32,3]{0,2,1:T(4,128)S(1)}, f32[80,32,3]{0,2,1:T(4,128)S(1)}, u32[]{:S(2)}, u32[]{:S(2)}) collective-permute-start(f32[80,32,3]{0,2,1:T(4,128)S(1)} %slice.631), channel_id=1, source_target_pairs={{496,0},{0,16},{16,32},{32,48},{48,64},{64,80},{80,96},{96,112},{1... | collective-permute-start | bytes 92168 | tf_op jit(solution)/shard_map/ppermute | solution.py:16
  76.8 6.3 %collective-permute-done.7 = f32[80,32,3]{0,2,1:T(4,128)S(1)} collective-permute-done((f32[80,32,3]{0,2,1:T(4,128)S(1)}, f32[80,32,3]{0,2,1:T(4,128)S(1)}, u32[]{:S(2)}, u32[]{:S(2)}) %collective-permute-start.7) | collective-permute-done | bytes 30752 | tf_op jit(solution)/shard_map/ppermute | solution.py:16
  83.4 1.7 %copy.64 = f32[80,32,128]{2,1,0:T(8,128)} copy(f32[80,32,128]{0,2,1:T(8,128)S(1)} %scatter-add.19) | data formatting | bytes 2621440
  (93 shorter events, 6.1 us)
Async XLA Ops:
  0.6 7.7 %copy-start = (f32[32,128]{1,0:T(8,128)S(1)}, f32[32,128]{1,0:T(8,128)}, u32[]{:S(2)}) copy-start(f32[32,128]{1,0:T(8,128)} %param.18) | copy-start | bytes 49156
  0.6 18.7 %copy-start.3 = (f32[1,2,128]{2,1,0:T(2,128)S(1)}, f32[1,2,128]{2,1,0:T(2,128)}, u32[]{:S(2)}) copy-start(f32[1,2,128]{2,1,0:T(2,128)} %param.24) | copy-start | bytes 3076
  0.7 18.7 %copy-start.5 = (s32[1,128]{1,0:T(1,128)S(1)}, s32[1,128]{1,0:T(1,128)}, u32[]{:S(2)}) copy-start(s32[1,128]{1,0:T(1,128)} %param.22) | copy-start | bytes 1540
  4.3 25.8 %copy-start.4 = (s32[1,128]{1,0:T(1,128)S(1)}, s32[1,128]{1,0:T(1,128)}, u32[]{:S(2)}) copy-start(s32[1,128]{1,0:T(1,128)} %param.23) | copy-start | bytes 1540
  4.5 15.3 %collective-permute-start = (f32[82,32,3]{0,2,1:T(4,128)S(1)}, f32[82,32,3]{0,2,1:T(4,128)S(1)}, u32[]{:S(2)}, u32[]{:S(2)}) collective-permute-start(f32[82,32,3]{0,2,1:T(4,128)S(1)} %pad_maximum_fusion.4), channel_id=1, source_target_pairs={{496,0},{0,16},{16,32},{32,48},{48,64},{64,80},{80,96},{96,112},{1... | collective-permute-start | bytes 94472 | tf_op jit(solution)/shard_map/ppermute | solution.py:16
  8.8 12.4 %collective-permute-start.1 = (f32[82,32,4]{0,2,1:T(4,128)S(1)}, f32[82,32,4]{0,2,1:T(4,128)S(1)}, u32[]{:S(2)}, u32[]{:S(2)}) collective-permute-start(f32[82,32,4]{0,2,1:T(4,128)S(1)} %pad_maximum_fusion.5), channel_id=1, source_target_pairs={{16,0},{32,16},{48,32},{64,48},{80,64},{96,80},{112,96},{128,112},... | collective-permute-start | bytes 125960 | tf_op jit(solution)/shard_map/ppermute | solution.py:16
  22.0 9.7 %collective-permute-start.2 = (f32[82,3,135]{0,2,1:T(8,128)}, f32[82,3,135]{0,2,1:T(8,128)S(1)}, u32[]{:S(2)}, u32[]{:S(2)}) collective-permute-start(f32[82,3,135]{0,2,1:T(8,128)} %pad_maximum_fusion.2), channel_id=1, source_target_pairs={{0,1},{1,2},{2,3},{3,4},{4,5},{5,6},{6,7},{7,8},{8,9},{9,10},{10,1... | collective-permute-start | bytes 398528 | tf_op jit(solution)/shard_map/ppermute | solution.py:19
  24.1 10.1 %collective-permute-start.3 = (f32[82,4,135]{0,2,1:T(8,128)S(1)}, f32[82,4,135]{0,2,1:T(8,128)S(1)}, u32[]{:S(2)}, u32[]{:S(2)}) collective-permute-start(f32[82,4,135]{0,2,1:T(8,128)S(1)} %pad_maximum_fusion.1), channel_id=1, source_target_pairs={{1,0},{2,1},{3,2},{4,3},{5,4},{6,5},{7,6},{8,7},{9,8},{10,9},{11,1... | collective-permute-start | bytes 531368 | tf_op jit(solution)/shard_map/ppermute | solution.py:19
  42.9 5.7 %copy-start.1 = (f32[1,80,128]{2,1,0:T(8,128)S(1)}, f32[1,80,128]{2,1,0:T(8,128)}, u32[]{:S(2)}) copy-start(f32[1,80,128]{2,1,0:T(8,128)} %param.20) | copy-start | bytes 122884
  42.9 5.7 %copy-start.2 = (f32[1,80,128]{2,1,0:T(8,128)S(1)}, f32[1,80,128]{2,1,0:T(8,128)}, u32[]{:S(2)}) copy-start(f32[1,80,128]{2,1,0:T(8,128)} %param.21) | copy-start | bytes 122884
  52.5 14.9 %collective-permute-start.5 = (f32[80,3,133]{0,2,1:T(8,128)S(1)}, f32[80,3,133]{0,2,1:T(8,128)S(1)}, u32[]{:S(2)}, u32[]{:S(2)}) collective-permute-start(f32[80,3,133]{0,2,1:T(8,128)S(1)} %fusion.38), channel_id=1, source_target_pairs={{0,1},{1,2},{2,3},{3,4},{4,5},{5,6},{6,7},{7,8},{8,9},{9,10},{10,1... | collective-permute-start | bytes 383048 | tf_op jit(solution)/shard_map/ppermute | solution.py:19
  57.1 10.2 %collective-permute-start.4 = (f32[80,2,133]{0,2,1:T(8,128)S(1)}, f32[80,2,133]{0,2,1:T(8,128)S(1)}, u32[]{:S(2)}, u32[]{:S(2)}) collective-permute-start(f32[80,2,133]{0,2,1:T(8,128)S(1)} %fusion.66), channel_id=1, source_target_pairs={{1,0},{2,1},{3,2},{4,3},{5,4},{6,5},{7,6},{8,7},{9,8},{10,9},{11,1... | collective-permute-start | bytes 255368 | tf_op jit(solution)/shard_map/ppermute | solution.py:19
  67.5 9.2 %collective-permute-start.6 = (f32[80,32,2]{0,2,1:T(2,128)S(1)}, f32[80,32,2]{0,2,1:T(2,128)S(1)}, u32[]{:S(2)}, u32[]{:S(2)}) collective-permute-start(f32[80,32,2]{0,2,1:T(2,128)S(1)} %slice.629), channel_id=1, source_target_pairs={{16,0},{32,16},{48,32},{64,48},{80,64},{96,80},{112,96},{128,112},... | collective-permute-start | bytes 61448 | tf_op jit(solution)/shard_map/ppermute | solution.py:16
  74.8 8.3 %collective-permute-start.7 = (f32[80,32,3]{0,2,1:T(4,128)S(1)}, f32[80,32,3]{0,2,1:T(4,128)S(1)}, u32[]{:S(2)}, u32[]{:S(2)}) collective-permute-start(f32[80,32,3]{0,2,1:T(4,128)S(1)} %slice.631), channel_id=1, source_target_pairs={{496,0},{0,16},{16,32},{32,48},{48,64},{64,80},{80,96},{96,112},{1... | collective-permute-start | bytes 92168 | tf_op jit(solution)/shard_map/ppermute | solution.py:16

commit v9 on v8

--- a/solution.py
+++ b/solution.py
@@ -145,13 +145,29 @@
     from_south = neighbour_shift(twice_n, 1, 0)
     from_north = neighbour_shift(twice_s, -1, 0)
 
+    once_w = diffuse(spread_a[:, 0 : rows + 4, 0:4], [w[0 : rows + 2, 0:2] for w in inner])
+    twice_w = diffuse(
+        jnp.pad(once_w, ((0, 0), (0, 0), (2, 0))), [w[2 : rows + 2, 0:2] for w in weights]
+    )
+    once_e = diffuse(
+        spread_a[:, 0 : rows + 4, cols : cols + 5], [w[0 : rows + 2, cols : cols + 3] for w in inner]
+    )
+    twice_e = diffuse(
+        jnp.pad(once_e, ((0, 0), (0, 0), (0, 2))), [w[2 : rows + 2, cols + 2 : cols + 5] for w in weights]
+    )
+    twice_w = twice_w.at[:, rows - GN :, :].add(from_south[:, :, :GW])
+    twice_w = twice_w.at[:, :GS, :].add(from_north[:, :, :GW])
+    twice_e = twice_e.at[:, rows - GN :, :].add(from_south[:, :, GW + cols :])
+    twice_e = twice_e.at[:, :GS, :].add(from_north[:, :, GW + cols :])
     once = diffuse(spread_a, inner)
-    middle = diffuse(pad2(once, 2)[:, 2 : rows + 4], [w[2 : rows + 2] for w in weights])
-    middle = middle.at[:, rows - GN :, :].add(from_south)
-    middle = middle.at[:, :GS, :].add(from_north)
-    gradient = middle[:, :, GW : GW + cols]
-    from_east = neighbour_shift(middle[:, :, :GW], 0, 1)
-    from_west = neighbour_shift(middle[:, :, GW + cols :], 0, -1)
+    once, twice_w, twice_e = lax.optimization_barrier((once, twice_w, twice_e))
+    from_east = neighbour_shift(twice_w, 0, 1)
+    from_west = neighbour_shift(twice_e, 0, -1)
+    gradient = diffuse(
+        pad2(once, 2)[:, 2 : rows + 4, 2 : cols + 4], [w[2 : rows + 2, 2 : cols + 2] for w in weights]
+    )
+    gradient = gradient.at[:, rows - GN :, :].add(from_south[:, :, GW : GW + cols])
+    gradient = gradient.at[:, :GS, :].add(from_north[:, :, GW : GW + cols])
     gradient = gradient.at[:, :, cols - GW :].add(from_east)
     gradient = gradient.at[:, :, :GE].add(from_west)
     return gradient, departure[None]

time: 85.6 us -> 83.7 us (0.978)
  starting transfers between devices: 38.7 us -> 29.5 us
  waiting for transfers between devices: 9.92 us -> 16.1 us
  local copies, waits for them, and re-layouts: 7.83 us -> 8.76 us
    ppermute x4, starting transfers between devices: 16.1 us -> 9.33 us  [neighbour_shift(): return lax.ppermute(block, 'lat', pairs)]
    ppermute x4, waiting for transfers between devices: 2.22 us -> 8.84 us  [neighbour_shift(): return lax.ppermute(block, 'lat', pairs)]
    ppermute x4, starting transfers between devices: 22.6 us -> 20.2 us  [neighbour_shift(): return lax.ppermute(block, 'lon', pairs)]
    slice x7 -> x20, local copies, waits for them, and re-layouts: 0.3 us -> 1.22 us  [the longest x4 0.3 us: on_device(): w[0:rows + 2, 0:2]]
    add x8 -> x12, other arithmetic: 13.7 us -> 14.6 us  [diffuse(): result = result + weight * (near - center)]
  transfers between devices with their start and end apart: 8 -> 8, of which waited for: 4 -> 4; matrix products, arithmetic and copies ran while one was open for 11% -> 12% of each run, Pallas kernels for 0% -> 0%
where the time goes in v9:
time: 83.7 us; the launch traced here: 83.2 us
  starting transfers between devices  29.5 us (35%)
  other arithmetic  18 us (22%)
  waiting for transfers between devices  16.1 us (19%)
  matrix products  8.93 us (11%)
  local copies, waits for them, and re-layouts  8.76 us (10%)
  between operations  1.89 us (2%)
    ppermute x4, starting transfers between devices, neighbour_shift(): return lax.ppermute(block, 'lon', pairs)  20.2 us
    add x12, other arithmetic, diffuse(): result = result + weight * (near - center)  14.6 us
    ppermute x4, starting transfers between devices, neighbour_shift(): return lax.ppermute(block, 'lat', pairs)  9.33 us
    ppermute x4, waiting for transfers between devices, neighbour_shift(): return lax.ppermute(block, 'lat', pairs)  8.84 us
    ppermute x4, waiting for transfers between devices, neighbour_shift(): return lax.ppermute(block, 'lon', pairs)  7.24 us
    dot_general x1, matrix products, on_device(): along = jnp.einsum('zrc,co->zro', state, wx, precision=hi)  5.65 us
    unnamed x16, local copies, waits for them, and re-layouts  4.21 us
    dot_general x1, matrix products, on_device(): adjoint = jnp.einsum('zro,co->zrc', spread, wx, precision=hi)  3.28 us
  transfers between devices with their start and end apart: 8, of which 4 were waited for; matrix products, arithmetic and copies ran while one was open for 12% of the time, Pallas kernels for 0%

profile of v9, /device:TPU:6, one launch (start us, length us, event | category | flops | bytes accessed | tf_op | source)
XLA Modules:
  0.0 83.2 jit_solution(15496271255234601467)
XLA Ops:
  0.7 0.7 convert_bitcast_fusion
  1.4 0.7 fusion.100
  2.4 1.8 %copy.51 = f32[80,32,128]{0,2,1:T(8,128)S(1)} copy(f32[80,32,128]{2,1,0:T(8,128)} %param.25) | data formatting | bytes 2621440 | tf_op args[0]
  4.4 12.4 %collective-permute-start.1 = (f32[82,32,4]{0,2,1:T(4,128)S(1)}, f32[82,32,4]{0,2,1:T(4,128)S(1)}, u32[]{:S(2)}, u32[]{:S(2)}) collective-permute-start(f32[82,32,4]{0,2,1:T(4,128)S(1)} %pad_maximum_fusion.5), channel_id=1, source_target_pairs={{16,0},{32,16},{48,32},{64,48},{80,64},{96,80},{112,96},{128,112},... | collective-permute-start | bytes 125960 | tf_op jit(solution)/shard_map/ppermute | solution.py:16
  17.4 1.9 %collective-permute-start = (f32[82,32,3]{0,2,1:T(4,128)S(1)}, f32[82,32,3]{0,2,1:T(4,128)S(1)}, u32[]{:S(2)}, u32[]{:S(2)}) collective-permute-start(f32[82,32,3]{0,2,1:T(4,128)S(1)} %pad_maximum_fusion.4), channel_id=1, source_target_pairs={{496,0},{0,16},{16,32},{32,48},{48,64},{64,80},{80,96},{96,112},{1... | collective-permute-start | bytes 94472 | tf_op jit(solution)/shard_map/ppermute | solution.py:16
  19.7 5.9 %collective-permute-done = f32[82,32,3]{0,2,1:T(4,128)S(1)} collective-permute-done((f32[82,32,3]{0,2,1:T(4,128)S(1)}, f32[82,32,3]{0,2,1:T(4,128)S(1)}, u32[]{:S(2)}, u32[]{:S(2)}) %collective-permute-start) | collective-permute-done | bytes 31520 | tf_op jit(solution)/shard_map/ppermute | solution.py:16
  25.8 3.1 %collective-permute-start.3 = (f32[82,4,135]{0,2,1:T(8,128)S(1)}, f32[82,4,135]{0,2,1:T(8,128)S(1)}, u32[]{:S(2)}, u32[]{:S(2)}) collective-permute-start(f32[82,4,135]{0,2,1:T(8,128)S(1)} %pad_maximum_fusion.1), channel_id=1, source_target_pairs={{1,0},{2,1},{3,2},{4,3},{5,4},{6,5},{7,6},{8,7},{9,8},{10,9},{11,1... | collective-permute-start | bytes 531368 | tf_op jit(solution)/shard_map/ppermute | solution.py:19
  29.0 1.9 %collective-permute-start.2 = (f32[82,3,135]{0,2,1:T(8,128)S(1)}, f32[82,3,135]{0,2,1:T(8,128)S(1)}, u32[]{:S(2)}, u32[]{:S(2)}) collective-permute-start(f32[82,3,135]{0,2,1:T(8,128)S(1)} %pad_maximum_fusion.2), channel_id=1, source_target_pairs={{0,1},{1,2},{2,3},{3,4},{4,5},{5,6},{6,7},{7,8},{8,9},{9,10},{10,1... | collective-permute-start | bytes 398528 | tf_op jit(solution)/shard_map/ppermute | solution.py:19
  31.7 0.3 copy.60
  32.5 6.1 %collective-permute-done.2 = f32[82,3,135]{0,2,1:T(8,128)S(1)} collective-permute-done((f32[82,3,135]{0,2,1:T(8,128)S(1)}, f32[82,3,135]{0,2,1:T(8,128)S(1)}, u32[]{:S(2)}, u32[]{:S(2)}) %collective-permute-start.2) | collective-permute-done | bytes 132872 | tf_op jit(solution)/shard_map/ppermute | solution.py:19
  42.3 3.6 %fusion.1 = f32[80,37,133]{0,2,1:T(8,128)S(1)} fusion(f32[80,39,135]{0,2,1:T(8,128)S(1)} %pad_maximum_fusion, f32[37,133]{1,0:T(8,128)S(1)} %get-tuple-element.117, f32[37,133]{1,0:T(8,128)S(1)} %get-tuple-element.115, f32[37,133]{1,0:T(8,128)S(1)} %get-tuple-element.116, f32[37,133]{1,0:T(8,128)S(1)} %get-tuple-element.114), kind=kLoop, calls=%fused_computation.3 | loop fusion | flops 4724160 | bytes 9527056 | tf_op jit(solution)/shard_map/add | solution.py:85
  46.0 2.8 %fusion.9 = f32[80,33,129]{0,2,1:T(8,128)S(1)} fusion(f32[80,37,133]{0,2,1:T(8,128)S(1)} %fusion.1, f32[33,129]{1,0:T(8,128)S(1)} %slice.877, f32[33,129]{1,0:T(8,128)S(1)} %slice.875, f32[33,129]{1,0:T(8,128)S(1)} %slice.873, f32[33,129]{1,0:T(8,128)S(1)} %slice.871), kind=kLoop, calls=%fused_computation.34 | loop fusion | flops 4086720 | bytes 8241552 | tf_op jit(solution)/shard_map/add | solution.py:85
  48.9 5.6 %fusion.18 = f32[80,128]{1,0:T(8,128)S(1)} fusion(f32[80,33,129]{0,2,1:T(8,128)S(1)} %fusion.9, f32[33,128]{1,0:T(8,128)S(1)} %select_add_fusion.3, f32[128]{0:T(128)S(1)} %get-tuple-element.122, s32[128]{0:T(128)S(1)} %add_bitcast_fusion, f32[128]{0:T(128)S(1)} %get-tuple-element.120, s32[128]{0:T(128)S(1)} %bitcast.54), kind=kOutput, calls=%fused_computation.48 | convolution fusion | flops 523848320 | bytes 1422144 | tf_op jit(solution)/shard_map/zrc,co->zro/dot_general | solution.py:125
  54.5 0.6 fusion.85
  55.2 3.3 %fusion.16 = f32[80,33,129]{0,2,1:T(8,128)S(1)} fusion(f32[80,128]{1,0:T(8,128)S(1)} %bitcast_divide_fusion, f32[33,128]{1,0:T(8,128)S(1)} %select_add_fusion.3, f32[128]{0:T(128)S(1)} %get-tuple-element.122, s32[128]{0:T(128)S(1)} %add_bitcast_fusion, f32[128]{0:T(128)S(1)} %get-tuple-element.120, s32[128]{0:T(128)S(1)} %bitcast.55), kind=kOutput, calls=%fused_computation.46 | convolution fusion | flops 523520640 | bytes 1422144 | tf_op jit(solution)/shard_map/zro,co->zrc/dot_general | solution.py:134
  58.9 1.9 %collective-permute-start.4 = (f32[80,2,133]{0,2,1:T(8,128)S(1)}, f32[80,2,133]{0,2,1:T(8,128)S(1)}, u32[]{:S(2)}, u32[]{:S(2)}) collective-permute-start(f32[80,2,133]{0,2,1:T(8,128)S(1)} %fusion.54), channel_id=1, source_target_pairs={{1,0},{2,1},{3,2},{4,3},{5,4},{6,5},{7,6},{8,7},{9,8},{10,9},{11,1... | collective-permute-start | bytes 255368 | tf_op jit(solution)/shard_map/ppermute | solution.py:19
  61.4 2.4 %collective-permute-start.5 = (f32[80,3,133]{0,2,1:T(8,128)S(1)}, f32[80,3,133]{0,2,1:T(8,128)S(1)}, u32[]{:S(2)}, u32[]{:S(2)}) collective-permute-start(f32[80,3,133]{0,2,1:T(8,128)S(1)} %fusion.26), channel_id=1, source_target_pairs={{0,1},{1,2},{2,3},{3,4},{4,5},{5,6},{6,7},{7,8},{8,9},{9,10},{10,1... | collective-permute-start | bytes 383048 | tf_op jit(solution)/shard_map/ppermute | solution.py:19
  63.8 3.4 %multiply_add_fusion = f32[80,35,131]{0,2,1:T(8,128)S(1)} fusion(f32[80,33,129]{0,2,1:T(8,128)S(1)} %fusion.16, f32[35,131]{1,0:T(8,128)S(1)} %slice.882, f32[35,131]{1,0:T(8,128)S(1)} %slice.881, f32[35,131]{1,0:T(8,128)S(1)} %slice.880, f32[35,131]{1,0:T(8,128)S(1)} %slice.879), kind=kLoop, calls=%fused_computation.13 | loop fusion | flops 4401600 | bytes 2902800 | tf_op jit(solution)/shard_map/add | solution.py:85
  68.2 2.8 %collective-permute-done.5 = f32[80,3,133]{0,2,1:T(8,128)S(1)} collective-permute-done((f32[80,3,133]{0,2,1:T(8,128)S(1)}, f32[80,3,133]{0,2,1:T(8,128)S(1)}, u32[]{:S(2)}, u32[]{:S(2)}) %collective-permute-start.5) | collective-permute-done | bytes 127712 | tf_op jit(solution)/shard_map/ppermute | solution.py:19
  71.0 1.9 %collective-permute-start.6 = (f32[80,32,2]{0,2,1:T(2,128)S(1)}, f32[80,32,2]{0,2,1:T(2,128)S(1)}, u32[]{:S(2)}, u32[]{:S(2)}) collective-permute-start(f32[80,32,2]{0,2,1:T(2,128)S(1)} %fusion.115), channel_id=1, source_target_pairs={{16,0},{32,16},{48,32},{64,48},{80,64},{96,80},{112,96},{128,112},... | collective-permute-start | bytes 61448 | tf_op jit(solution)/shard_map/ppermute | solution.py:16
  72.9 3.9 %collective-permute-start.7 = (f32[80,32,3]{0,2,1:T(4,128)S(1)}, f32[80,32,3]{0,2,1:T(4,128)S(1)}, u32[]{:S(2)}, u32[]{:S(2)}) collective-permute-start(f32[80,32,3]{0,2,1:T(4,128)S(1)} %fusion.112), channel_id=1, source_target_pairs={{496,0},{0,16},{16,32},{32,48},{48,64},{64,80},{80,96},{96,112},{1... | collective-permute-start | bytes 92168 | tf_op jit(solution)/shard_map/ppermute | solution.py:16
  76.8 2.8 %multiply_add_fusion.1 = f32[80,32,128]{0,2,1:T(8,128)S(1)} fusion(f32[80,35,131]{0,2,1:T(8,128)S(1)} %multiply_add_fusion, f32[32,128]{1,0:T(8,128)S(1)} %slice.928, f32[32,128]{1,0:T(8,128)S(1)} %slice.927, f32[32,128]{1,0:T(8,128)S(1)} %slice.926, f32[32,128]{1,0:T(8,128)S(1)} %slice.925), kind=kLoop, calls=%fused_computation.44 | loop fusion | flops 3932160 | bytes 7929856 | tf_op jit(solution)/shard_map/add | solution.py:85
  79.8 1.3 %collective-permute-done.7 = f32[80,32,3]{0,2,1:T(4,128)S(1)} collective-permute-done((f32[80,32,3]{0,2,1:T(4,128)S(1)}, f32[80,32,3]{0,2,1:T(4,128)S(1)}, u32[]{:S(2)}, u32[]{:S(2)}) %collective-permute-start.7) | collective-permute-done | bytes 30752 | tf_op jit(solution)/shard_map/ppermute | solution.py:16
  81.4 1.7 %copy.64 = f32[80,32,128]{2,1,0:T(8,128)} copy(f32[80,32,128]{0,2,1:T(8,128)S(1)} %scatter-add.39) | data formatting | bytes 2621440
  (114 shorter events, 8.1 us)
Async XLA Ops:
  0.6 16.2 %copy-start = (f32[32,128]{1,0:T(8,128)S(1)}, f32[32,128]{1,0:T(8,128)}, u32[]{:S(2)}) copy-start(f32[32,128]{1,0:T(8,128)} %param.26) | copy-start | bytes 49156
  0.6 18.7 %copy-start.3 = (f32[1,2,128]{2,1,0:T(2,128)S(1)}, f32[1,2,128]{2,1,0:T(2,128)}, u32[]{:S(2)}) copy-start(f32[1,2,128]{2,1,0:T(2,128)} %param.32) | copy-start | bytes 3076
  0.7 18.7 %copy-start.5 = (s32[1,128]{1,0:T(1,128)S(1)}, s32[1,128]{1,0:T(1,128)}, u32[]{:S(2)}) copy-start(s32[1,128]{1,0:T(1,128)} %param.30) | copy-start | bytes 1540
  4.3 26.7 %copy-start.4 = (s32[1,128]{1,0:T(1,128)S(1)}, s32[1,128]{1,0:T(1,128)}, u32[]{:S(2)}) copy-start(s32[1,128]{1,0:T(1,128)} %param.31) | copy-start | bytes 1540
  4.4 21.2 %collective-permute-start.1 = (f32[82,32,4]{0,2,1:T(4,128)S(1)}, f32[82,32,4]{0,2,1:T(4,128)S(1)}, u32[]{:S(2)}, u32[]{:S(2)}) collective-permute-start(f32[82,32,4]{0,2,1:T(4,128)S(1)} %pad_maximum_fusion.5), channel_id=1, source_target_pairs={{16,0},{32,16},{48,32},{64,48},{80,64},{96,80},{112,96},{128,112},... | collective-permute-start | bytes 125960 | tf_op jit(solution)/shard_map/ppermute | solution.py:16
  17.4 8.3 %collective-permute-start = (f32[82,32,3]{0,2,1:T(4,128)S(1)}, f32[82,32,3]{0,2,1:T(4,128)S(1)}, u32[]{:S(2)}, u32[]{:S(2)}) collective-permute-start(f32[82,32,3]{0,2,1:T(4,128)S(1)} %pad_maximum_fusion.4), channel_id=1, source_target_pairs={{496,0},{0,16},{16,32},{32,48},{48,64},{64,80},{80,96},{96,112},{1... | collective-permute-start | bytes 94472 | tf_op jit(solution)/shard_map/ppermute | solution.py:16
  25.8 13.1 %collective-permute-start.3 = (f32[82,4,135]{0,2,1:T(8,128)S(1)}, f32[82,4,135]{0,2,1:T(8,128)S(1)}, u32[]{:S(2)}, u32[]{:S(2)}) collective-permute-start(f32[82,4,135]{0,2,1:T(8,128)S(1)} %pad_maximum_fusion.1), channel_id=1, source_target_pairs={{1,0},{2,1},{3,2},{4,3},{5,4},{6,5},{7,6},{8,7},{9,8},{10,9},{11,1... | collective-permute-start | bytes 531368 | tf_op jit(solution)/shard_map/ppermute | solution.py:19
  29.0 9.5 %collective-permute-start.2 = (f32[82,3,135]{0,2,1:T(8,128)S(1)}, f32[82,3,135]{0,2,1:T(8,128)S(1)}, u32[]{:S(2)}, u32[]{:S(2)}) collective-permute-start(f32[82,3,135]{0,2,1:T(8,128)S(1)} %pad_maximum_fusion.2), channel_id=1, source_target_pairs={{0,1},{1,2},{2,3},{3,4},{4,5},{5,6},{6,7},{7,8},{8,9},{9,10},{10,1... | collective-permute-start | bytes 398528 | tf_op jit(solution)/shard_map/ppermute | solution.py:19
  48.8 5.7 %copy-start.1 = (f32[1,80,128]{2,1,0:T(8,128)S(1)}, f32[1,80,128]{2,1,0:T(8,128)}, u32[]{:S(2)}) copy-start(f32[1,80,128]{2,1,0:T(8,128)} %param.28) | copy-start | bytes 122884
  48.8 6.3 %copy-start.2 = (f32[1,80,128]{2,1,0:T(8,128)S(1)}, f32[1,80,128]{2,1,0:T(8,128)}, u32[]{:S(2)}) copy-start(f32[1,80,128]{2,1,0:T(8,128)} %param.29) | copy-start | bytes 122884
  58.9 9.2 %collective-permute-start.4 = (f32[80,2,133]{0,2,1:T(8,128)S(1)}, f32[80,2,133]{0,2,1:T(8,128)S(1)}, u32[]{:S(2)}, u32[]{:S(2)}) collective-permute-start(f32[80,2,133]{0,2,1:T(8,128)S(1)} %fusion.54), channel_id=1, source_target_pairs={{1,0},{2,1},{3,2},{4,3},{5,4},{6,5},{7,6},{8,7},{9,8},{10,9},{11,1... | collective-permute-start | bytes 255368 | tf_op jit(solution)/shard_map/ppermute | solution.py:19
  61.4 9.5 %collective-permute-start.5 = (f32[80,3,133]{0,2,1:T(8,128)S(1)}, f32[80,3,133]{0,2,1:T(8,128)S(1)}, u32[]{:S(2)}, u32[]{:S(2)}) collective-permute-start(f32[80,3,133]{0,2,1:T(8,128)S(1)} %fusion.26), channel_id=1, source_target_pairs={{0,1},{1,2},{2,3},{3,4},{4,5},{5,6},{6,7},{7,8},{8,9},{9,10},{10,1... | collective-permute-start | bytes 383048 | tf_op jit(solution)/shard_map/ppermute | solution.py:19
  71.0 8.8 %collective-permute-start.6 = (f32[80,32,2]{0,2,1:T(2,128)S(1)}, f32[80,32,2]{0,2,1:T(2,128)S(1)}, u32[]{:S(2)}, u32[]{:S(2)}) collective-permute-start(f32[80,32,2]{0,2,1:T(2,128)S(1)} %fusion.115), channel_id=1, source_target_pairs={{16,0},{32,16},{48,32},{64,48},{80,64},{96,80},{112,96},{128,112},... | collective-permute-start | bytes 61448 | tf_op jit(solution)/shard_map/ppermute | solution.py:16
  72.9 8.3 %collective-permute-start.7 = (f32[80,32,3]{0,2,1:T(4,128)S(1)}, f32[80,32,3]{0,2,1:T(4,128)S(1)}, u32[]{:S(2)}, u32[]{:S(2)}) collective-permute-start(f32[80,32,3]{0,2,1:T(4,128)S(1)} %fusion.112), channel_id=1, source_target_pairs={{496,0},{0,16},{16,32},{32,48},{48,64},{64,80},{80,96},{96,112},{1... | collective-permute-start | bytes 92168 | tf_op jit(solution)/shard_map/ppermute | solution.py:16

commit v10 on v9

--- a/solution.py
+++ b/solution.py
@@ -122,8 +122,8 @@
         col_ids == base_c + 1, frac_x[None], 0.0
     )
     hi = lax.Precision.HIGHEST
-    along = jnp.einsum("zrc,co->zro", state, wx, precision=hi)
-    sample = jnp.sum(along * wy[None], axis=1)
+    along = jnp.einsum("rcz,co->roz", jnp.transpose(state, (1, 2, 0)), wx, precision=hi)
+    sample = jnp.sum(along * wy[:, :, None], axis=0).T
 
     slots = jnp.arange(obs_row.shape[1], dtype=jnp.int32)
     valid = (slots < obs_counts[0, 0]).astype(jnp.float32)

time: 83.7 us -> 83.8 us (level)
  no operation moved by 1% of the time
where the time goes in v10:
time: 83.8 us; the launch traced here: 83.3 us
  starting transfers between devices  29.5 us (35%)
  other arithmetic  18 us (21%)
  waiting for transfers between devices  16.1 us (19%)
  matrix products  9.06 us (11%)
  local copies, waits for them, and re-layouts  8.76 us (10%)
  between operations  1.89 us (2%)
    ppermute x4, starting transfers between devices, neighbour_shift(): return lax.ppermute(block, 'lon', pairs)  20.2 us
    add x12, other arithmetic, diffuse(): result = result + weight * (near - center)  14.6 us
    ppermute x4, starting transfers between devices, neighbour_shift(): return lax.ppermute(block, 'lat', pairs)  9.33 us
    ppermute x4, waiting for transfers between devices, neighbour_shift(): return lax.ppermute(block, 'lat', pairs)  8.84 us
    ppermute x4, waiting for transfers between devices, neighbour_shift(): return lax.ppermute(block, 'lon', pairs)  7.24 us
    dot_general x1, matrix products, on_device(): jnp.einsum('rcz,co->roz', jnp.transpose(state, (1, 2, 0)), wx, precision=hi)  5.78 us
    unnamed x16, local copies, waits for them, and re-layouts  4.21 us
    dot_general x1, matrix products, on_device(): adjoint = jnp.einsum('zro,co->zrc', spread, wx, precision=hi)  3.28 us
  transfers between devices with their start and end apart: 8, of which 4 were waited for; matrix products, arithmetic and copies ran while one was open for 12% of the time, Pallas kernels for 0%

profile of v10, /device:TPU:6, one launch (start us, length us, event | category | flops | bytes accessed | tf_op | source)
XLA Modules:
  0.0 83.3 jit_solution(15541799452892050742)
XLA Ops:
  0.7 0.7 convert_bitcast_fusion
  1.4 0.7 fusion.109
  2.4 1.8 %copy.51 = f32[80,32,128]{0,2,1:T(8,128)S(1)} copy(f32[80,32,128]{2,1,0:T(8,128)} %param.25) | data formatting | bytes 2621440 | tf_op args[0]
  4.4 12.4 %collective-permute-start.1 = (f32[82,32,4]{0,2,1:T(4,128)S(1)}, f32[82,32,4]{0,2,1:T(4,128)S(1)}, u32[]{:S(2)}, u32[]{:S(2)}) collective-permute-start(f32[82,32,4]{0,2,1:T(4,128)S(1)} %pad_maximum_fusion.5), channel_id=1, source_target_pairs={{16,0},{32,16},{48,32},{64,48},{80,64},{96,80},{112,96},{128,112},... | collective-permute-start | bytes 125960 | tf_op jit(solution)/shard_map/ppermute | solution.py:16
  17.4 1.9 %collective-permute-start = (f32[82,32,3]{0,2,1:T(4,128)S(1)}, f32[82,32,3]{0,2,1:T(4,128)S(1)}, u32[]{:S(2)}, u32[]{:S(2)}) collective-permute-start(f32[82,32,3]{0,2,1:T(4,128)S(1)} %pad_maximum_fusion.4), channel_id=1, source_target_pairs={{496,0},{0,16},{16,32},{32,48},{48,64},{64,80},{80,96},{96,112},{1... | collective-permute-start | bytes 94472 | tf_op jit(solution)/shard_map/ppermute | solution.py:16
  19.7 5.9 %collective-permute-done = f32[82,32,3]{0,2,1:T(4,128)S(1)} collective-permute-done((f32[82,32,3]{0,2,1:T(4,128)S(1)}, f32[82,32,3]{0,2,1:T(4,128)S(1)}, u32[]{:S(2)}, u32[]{:S(2)}) %collective-permute-start) | collective-permute-done | bytes 31520 | tf_op jit(solution)/shard_map/ppermute | solution.py:16
  25.8 3.1 %collective-permute-start.3 = (f32[82,4,135]{0,2,1:T(8,128)S(1)}, f32[82,4,135]{0,2,1:T(8,128)S(1)}, u32[]{:S(2)}, u32[]{:S(2)}) collective-permute-start(f32[82,4,135]{0,2,1:T(8,128)S(1)} %pad_maximum_fusion.1), channel_id=1, source_target_pairs={{1,0},{2,1},{3,2},{4,3},{5,4},{6,5},{7,6},{8,7},{9,8},{10,9},{11,1... | collective-permute-start | bytes 531368 | tf_op jit(solution)/shard_map/ppermute | solution.py:19
  29.0 1.9 %collective-permute-start.2 = (f32[82,3,135]{0,2,1:T(8,128)S(1)}, f32[82,3,135]{0,2,1:T(8,128)S(1)}, u32[]{:S(2)}, u32[]{:S(2)}) collective-permute-start(f32[82,3,135]{0,2,1:T(8,128)S(1)} %pad_maximum_fusion.2), channel_id=1, source_target_pairs={{0,1},{1,2},{2,3},{3,4},{4,5},{5,6},{6,7},{7,8},{8,9},{9,10},{10,1... | collective-permute-start | bytes 398528 | tf_op jit(solution)/shard_map/ppermute | solution.py:19
  31.7 0.3 copy.60
  32.5 6.1 %collective-permute-done.2 = f32[82,3,135]{0,2,1:T(8,128)S(1)} collective-permute-done((f32[82,3,135]{0,2,1:T(8,128)S(1)}, f32[82,3,135]{0,2,1:T(8,128)S(1)}, u32[]{:S(2)}, u32[]{:S(2)}) %collective-permute-start.2) | collective-permute-done | bytes 132872 | tf_op jit(solution)/shard_map/ppermute | solution.py:19
  42.3 3.6 %fusion.1 = f32[80,37,133]{0,2,1:T(8,128)S(1)} fusion(f32[80,39,135]{0,2,1:T(8,128)S(1)} %pad_maximum_fusion, f32[37,133]{1,0:T(8,128)S(1)} %get-tuple-element.119, f32[37,133]{1,0:T(8,128)S(1)} %get-tuple-element.117, f32[37,133]{1,0:T(8,128)S(1)} %get-tuple-element.118, f32[37,133]{1,0:T(8,128)S(1)} %get-tuple-element.116), kind=kLoop, calls=%fused_computation.3 | loop fusion | flops 4724160 | bytes 9527056 | tf_op jit(solution)/shard_map/add | solution.py:85
  46.0 2.8 %fusion.9 = f32[80,33,129]{0,2,1:T(8,128)S(1)} fusion(f32[80,37,133]{0,2,1:T(8,128)S(1)} %fusion.1, f32[33,129]{1,0:T(8,128)S(1)} %slice.877, f32[33,129]{1,0:T(8,128)S(1)} %slice.875, f32[33,129]{1,0:T(8,128)S(1)} %slice.873, f32[33,129]{1,0:T(8,128)S(1)} %slice.871), kind=kLoop, calls=%fused_computation.34 | loop fusion | flops 4086720 | bytes 8241552 | tf_op jit(solution)/shard_map/add | solution.py:85
  48.9 5.8 %fusion.26 = f32[128,80]{0,1:T(8,128)S(1)} fusion(f32[80,33,129]{0,2,1:T(8,128)S(1)} %fusion.9, f32[33,128]{1,0:T(8,128)S(1)} %select_add_fusion.3, f32[128]{0:T(128)S(1)} %get-tuple-element.124, s32[128]{0:T(128)S(1)} %add_bitcast_fusion, f32[128]{0:T(128)S(1)} %get-tuple-element.122, s32[128]{0:T(128)S(1)} %bitcast.75), kind=kOutput, calls=%fused_computation.51 | convolution fusion | flops 523848320 | bytes 1422144 | tf_op jit(solution)/shard_map/rcz,co->roz/dot_general | solution.py:125
  54.7 0.6 fusion.121
  55.3 3.3 %fusion.24 = f32[80,33,129]{0,2,1:T(8,128)S(1)} fusion(f32[80,128]{1,0:T(8,128)S(1)} %get-tuple-element.115, f32[33,128]{1,0:T(8,128)S(1)} %select_add_fusion.3, f32[128]{0:T(128)S(1)} %get-tuple-element.124, s32[128]{0:T(128)S(1)} %add_bitcast_fusion, f32[128]{0:T(128)S(1)} %get-tuple-element.122, s32[128]{0:T(128)S(1)} %bitcast.76), kind=kOutput, calls=%fused_computation.49 | convolution fusion | flops 523520640 | bytes 1422144 | tf_op jit(solution)/shard_map/zro,co->zrc/dot_general | solution.py:134
  59.0 1.9 %collective-permute-start.4 = (f32[80,2,133]{0,2,1:T(8,128)S(1)}, f32[80,2,133]{0,2,1:T(8,128)S(1)}, u32[]{:S(2)}, u32[]{:S(2)}) collective-permute-start(f32[80,2,133]{0,2,1:T(8,128)S(1)} %fusion.64), channel_id=1, source_target_pairs={{1,0},{2,1},{3,2},{4,3},{5,4},{6,5},{7,6},{8,7},{9,8},{10,9},{11,1... | collective-permute-start | bytes 255368 | tf_op jit(solution)/shard_map/ppermute | solution.py:19
  61.5 2.4 %collective-permute-start.5 = (f32[80,3,133]{0,2,1:T(8,128)S(1)}, f32[80,3,133]{0,2,1:T(8,128)S(1)}, u32[]{:S(2)}, u32[]{:S(2)}) collective-permute-start(f32[80,3,133]{0,2,1:T(8,128)S(1)} %fusion.36), channel_id=1, source_target_pairs={{0,1},{1,2},{2,3},{3,4},{4,5},{5,6},{6,7},{7,8},{8,9},{9,10},{10,1... | collective-permute-start | bytes 383048 | tf_op jit(solution)/shard_map/ppermute | solution.py:19
  63.9 3.4 %multiply_add_fusion = f32[80,35,131]{0,2,1:T(8,128)S(1)} fusion(f32[80,33,129]{0,2,1:T(8,128)S(1)} %fusion.24, f32[35,131]{1,0:T(8,128)S(1)} %slice.882, f32[35,131]{1,0:T(8,128)S(1)} %slice.881, f32[35,131]{1,0:T(8,128)S(1)} %slice.880, f32[35,131]{1,0:T(8,128)S(1)} %slice.879), kind=kLoop, calls=%fused_computation.13 | loop fusion | flops 4401600 | bytes 2902800 | tf_op jit(solution)/shard_map/add | solution.py:85
  68.3 2.8 %collective-permute-done.5 = f32[80,3,133]{0,2,1:T(8,128)S(1)} collective-permute-done((f32[80,3,133]{0,2,1:T(8,128)S(1)}, f32[80,3,133]{0,2,1:T(8,128)S(1)}, u32[]{:S(2)}, u32[]{:S(2)}) %collective-permute-start.5) | collective-permute-done | bytes 127712 | tf_op jit(solution)/shard_map/ppermute | solution.py:19
  71.1 1.9 %collective-permute-start.6 = (f32[80,32,2]{0,2,1:T(2,128)S(1)}, f32[80,32,2]{0,2,1:T(2,128)S(1)}, u32[]{:S(2)}, u32[]{:S(2)}) collective-permute-start(f32[80,32,2]{0,2,1:T(2,128)S(1)} %fusion.125), channel_id=1, source_target_pairs={{16,0},{32,16},{48,32},{64,48},{80,64},{96,80},{112,96},{128,112},... | collective-permute-start | bytes 61448 | tf_op jit(solution)/shard_map/ppermute | solution.py:16
  73.0 3.9 %collective-permute-start.7 = (f32[80,32,3]{0,2,1:T(4,128)S(1)}, f32[80,32,3]{0,2,1:T(4,128)S(1)}, u32[]{:S(2)}, u32[]{:S(2)}) collective-permute-start(f32[80,32,3]{0,2,1:T(4,128)S(1)} %fusion.122), channel_id=1, source_target_pairs={{496,0},{0,16},{16,32},{32,48},{48,64},{64,80},{80,96},{96,112},{1... | collective-permute-start | bytes 92168 | tf_op jit(solution)/shard_map/ppermute | solution.py:16
  76.9 2.8 %multiply_add_fusion.1 = f32[80,32,128]{0,2,1:T(8,128)S(1)} fusion(f32[80,35,131]{0,2,1:T(8,128)S(1)} %multiply_add_fusion, f32[32,128]{1,0:T(8,128)S(1)} %slice.928, f32[32,128]{1,0:T(8,128)S(1)} %slice.927, f32[32,128]{1,0:T(8,128)S(1)} %slice.926, f32[32,128]{1,0:T(8,128)S(1)} %slice.925), kind=kLoop, calls=%fused_computation.46 | loop fusion | flops 3932160 | bytes 7929856 | tf_op jit(solution)/shard_map/add | solution.py:85
  79.9 1.3 %collective-permute-done.7 = f32[80,32,3]{0,2,1:T(4,128)S(1)} collective-permute-done((f32[80,32,3]{0,2,1:T(4,128)S(1)}, f32[80,32,3]{0,2,1:T(4,128)S(1)}, u32[]{:S(2)}, u32[]{:S(2)}) %collective-permute-start.7) | collective-permute-done | bytes 30752 | tf_op jit(solution)/shard_map/ppermute | solution.py:16
  81.6 1.7 %copy.64 = f32[80,32,128]{2,1,0:T(8,128)} copy(f32[80,32,128]{0,2,1:T(8,128)S(1)} %scatter-add.39) | data formatting | bytes 2621440
  (113 shorter events, 8.1 us)
Async XLA Ops:
  0.6 16.2 %copy-start = (f32[32,128]{1,0:T(8,128)S(1)}, f32[32,128]{1,0:T(8,128)}, u32[]{:S(2)}) copy-start(f32[32,128]{1,0:T(8,128)} %param.26) | copy-start | bytes 49156
  0.6 18.7 %copy-start.3 = (f32[1,2,128]{2,1,0:T(2,128)S(1)}, f32[1,2,128]{2,1,0:T(2,128)}, u32[]{:S(2)}) copy-start(f32[1,2,128]{2,1,0:T(2,128)} %param.32) | copy-start | bytes 3076
  0.7 18.7 %copy-start.5 = (s32[1,128]{1,0:T(1,128)S(1)}, s32[1,128]{1,0:T(1,128)}, u32[]{:S(2)}) copy-start(s32[1,128]{1,0:T(1,128)} %param.30) | copy-start | bytes 1540
  4.3 26.7 %copy-start.4 = (s32[1,128]{1,0:T(1,128)S(1)}, s32[1,128]{1,0:T(1,128)}, u32[]{:S(2)}) copy-start(s32[1,128]{1,0:T(1,128)} %param.31) | copy-start | bytes 1540
  4.4 21.2 %collective-permute-start.1 = (f32[82,32,4]{0,2,1:T(4,128)S(1)}, f32[82,32,4]{0,2,1:T(4,128)S(1)}, u32[]{:S(2)}, u32[]{:S(2)}) collective-permute-start(f32[82,32,4]{0,2,1:T(4,128)S(1)} %pad_maximum_fusion.5), channel_id=1, source_target_pairs={{16,0},{32,16},{48,32},{64,48},{80,64},{96,80},{112,96},{128,112},... | collective-permute-start | bytes 125960 | tf_op jit(solution)/shard_map/ppermute | solution.py:16
  17.4 8.3 %collective-permute-start = (f32[82,32,3]{0,2,1:T(4,128)S(1)}, f32[82,32,3]{0,2,1:T(4,128)S(1)}, u32[]{:S(2)}, u32[]{:S(2)}) collective-permute-start(f32[82,32,3]{0,2,1:T(4,128)S(1)} %pad_maximum_fusion.4), channel_id=1, source_target_pairs={{496,0},{0,16},{16,32},{32,48},{48,64},{64,80},{80,96},{96,112},{1... | collective-permute-start | bytes 94472 | tf_op jit(solution)/shard_map/ppermute | solution.py:16
  25.8 13.1 %collective-permute-start.3 = (f32[82,4,135]{0,2,1:T(8,128)S(1)}, f32[82,4,135]{0,2,1:T(8,128)S(1)}, u32[]{:S(2)}, u32[]{:S(2)}) collective-permute-start(f32[82,4,135]{0,2,1:T(8,128)S(1)} %pad_maximum_fusion.1), channel_id=1, source_target_pairs={{1,0},{2,1},{3,2},{4,3},{5,4},{6,5},{7,6},{8,7},{9,8},{10,9},{11,1... | collective-permute-start | bytes 531368 | tf_op jit(solution)/shard_map/ppermute | solution.py:19
  29.0 9.5 %collective-permute-start.2 = (f32[82,3,135]{0,2,1:T(8,128)S(1)}, f32[82,3,135]{0,2,1:T(8,128)S(1)}, u32[]{:S(2)}, u32[]{:S(2)}) collective-permute-start(f32[82,3,135]{0,2,1:T(8,128)S(1)} %pad_maximum_fusion.2), channel_id=1, source_target_pairs={{0,1},{1,2},{2,3},{3,4},{4,5},{5,6},{6,7},{7,8},{8,9},{9,10},{10,1... | collective-permute-start | bytes 398528 | tf_op jit(solution)/shard_map/ppermute | solution.py:19
  48.8 5.8 %copy-start.1 = (f32[1,80,128]{2,1,0:T(8,128)S(1)}, f32[1,80,128]{2,1,0:T(8,128)}, u32[]{:S(2)}) copy-start(f32[1,80,128]{2,1,0:T(8,128)} %param.28) | copy-start | bytes 122884
  48.8 5.8 %copy-start.2 = (f32[1,80,128]{2,1,0:T(8,128)S(1)}, f32[1,80,128]{2,1,0:T(8,128)}, u32[]{:S(2)}) copy-start(f32[1,80,128]{2,1,0:T(8,128)} %param.29) | copy-start | bytes 122884
  59.0 9.2 %collective-permute-start.4 = (f32[80,2,133]{0,2,1:T(8,128)S(1)}, f32[80,2,133]{0,2,1:T(8,128)S(1)}, u32[]{:S(2)}, u32[]{:S(2)}) collective-permute-start(f32[80,2,133]{0,2,1:T(8,128)S(1)} %fusion.64), channel_id=1, source_target_pairs={{1,0},{2,1},{3,2},{4,3},{5,4},{6,5},{7,6},{8,7},{9,8},{10,9},{11,1... | collective-permute-start | bytes 255368 | tf_op jit(solution)/shard_map/ppermute | solution.py:19
  61.5 9.5 %collective-permute-start.5 = (f32[80,3,133]{0,2,1:T(8,128)S(1)}, f32[80,3,133]{0,2,1:T(8,128)S(1)}, u32[]{:S(2)}, u32[]{:S(2)}) collective-permute-start(f32[80,3,133]{0,2,1:T(8,128)S(1)} %fusion.36), channel_id=1, source_target_pairs={{0,1},{1,2},{2,3},{3,4},{4,5},{5,6},{6,7},{7,8},{8,9},{9,10},{10,1... | collective-permute-start | bytes 383048 | tf_op jit(solution)/shard_map/ppermute | solution.py:19
  71.1 8.8 %collective-permute-start.6 = (f32[80,32,2]{0,2,1:T(2,128)S(1)}, f32[80,32,2]{0,2,1:T(2,128)S(1)}, u32[]{:S(2)}, u32[]{:S(2)}) collective-permute-start(f32[80,32,2]{0,2,1:T(2,128)S(1)} %fusion.125), channel_id=1, source_target_pairs={{16,0},{32,16},{48,32},{64,48},{80,64},{96,80},{112,96},{128,112},... | collective-permute-start | bytes 61448 | tf_op jit(solution)/shard_map/ppermute | solution.py:16
  73.0 8.3 %collective-permute-start.7 = (f32[80,32,3]{0,2,1:T(4,128)S(1)}, f32[80,32,3]{0,2,1:T(4,128)S(1)}, u32[]{:S(2)}, u32[]{:S(2)}) collective-permute-start(f32[80,32,3]{0,2,1:T(4,128)S(1)} %fusion.122), channel_id=1, source_target_pairs={{496,0},{0,16},{16,32},{32,48},{48,64},{64,80},{80,96},{96,112},{1... | collective-permute-start | bytes 92168 | tf_op jit(solution)/shard_map/ppermute | solution.py:16

commit v11 on v9

--- a/solution.py
+++ b/solution.py
@@ -26,15 +26,18 @@
     return lax.ppermute(block, ("lon", "lat"), pairs)
 
 
-def gather_halo(parts, hn, hs, hw, he):
+def gather_halo(parts, hn, hs, hw, he, gate):
     rows, cols = parts[0].shape[-2:]
     sizes = [p.shape[0] for p in parts]
 
     def joined(window):
         return jnp.concatenate([p[window] for p in parts], axis=0)
 
-    west = neighbour_shift(joined((Ellipsis, slice(None), slice(cols - hw, None))), 0, -1)
-    east = neighbour_shift(joined((Ellipsis, slice(None), slice(0, he))), 0, 1)
+    west_piece = joined((Ellipsis, slice(None), slice(cols - hw, None)))
+    east_piece = joined((Ellipsis, slice(None), slice(0, he)))
+    west_piece, east_piece, gate = lax.optimization_barrier((west_piece, east_piece, gate))
+    west = neighbour_shift(west_piece, 0, -1)
+    east = neighbour_shift(east_piece, 0, 1)
     edge_n = jnp.concatenate(
         [west[..., rows - hn :, :], joined((Ellipsis, slice(rows - hn, None), slice(None))),
          east[..., rows - hn :, :]], axis=-1)
@@ -99,13 +102,25 @@
 ):
     channels, rows, cols = control.shape
     coeff = jnp.stack([diffusivity, land_mask.astype(jnp.float32)])
-    field, coeff = gather_halo([control, coeff], HN, HS, HW, HE)
+    local_w = edge_weights(coeff[0], coeff[1])
+    inside = diffuse(diffuse(control, local_w), trim(local_w, 1))
+    field, coeff = gather_halo([control, coeff], HN, HS, HW, HE, inside)
     field = with_layout_constraint(field, Layout(major_to_minor=(1, 2, 0)))
     weights = edge_weights(coeff[0], coeff[1])
 
-    once = diffuse(field, weights)
-    state = diffuse(
-        once[:, 1 : rows + 4, 1 : cols + 4], [w[2 : rows + 3, 2 : cols + 3] for w in weights]
+    def state_on(r0, r1, c0, c1):
+        first = diffuse(
+            field[:, r0 - 2 + HN : r1 + 2 + HN, c0 - 2 + HW : c1 + 2 + HW],
+            [w[r0 + 1 : r1 + 3, c0 + 1 : c1 + 3] for w in weights],
+        )
+        return diffuse(first, [w[r0 + 2 : r1 + 2, c0 + 2 : c1 + 2] for w in weights])
+
+    top = state_on(0, 2, 0, cols + 1)
+    bottom = state_on(rows - 2, rows + 1, 0, cols + 1)
+    left = state_on(2, rows - 2, 0, 2)
+    right = state_on(2, rows - 2, cols - 2, cols + 1)
+    state = jnp.concatenate(
+        [top, jnp.concatenate([left, inside, right], axis=-1), bottom], axis=-2
     )
     state = lax.optimization_barrier(state)
 

time: 83.7 us -> 137 us (1.64)
  local copies, waits for them, and re-layouts: 8.76 us -> 46.7 us
  other arithmetic: 18 us -> 33.6 us
  starting transfers between devices: 29.5 us -> 39.3 us
  waiting for transfers between devices: 16.1 us -> 7.41 us
  matrix products: 8.93 us -> 6.3 us
    add x12 -> x20, other arithmetic: 14.6 us -> 24.1 us  [diffuse(): result = result + weight * (near - center)]
    ppermute x4, starting transfers between devices: 9.33 us -> 16.5 us  [neighbour_shift(): return lax.ppermute(block, 'lat', pairs)]
    slice x4 -> x32, local copies, waits for them, and re-layouts: 0.32 us -> 6.83 us  [the longest x16 3.57 us: state_on(): w[r0 + 1:r1 + 3, c0 + 1:c1 + 3]]
    slice x4 -> x8, local copies, waits for them, and re-layouts: 0.32 us -> 5.46 us  [trim(): return [w[k:w.shape[0] - k, k:w.shape[1] - k] for w in weights]]
    add x0 -> x4, local copies, waits for them, and re-layouts: none -> 4.95 us  [diffuse(): result = result + weight * (near - center)]
    ppermute x4, waiting for transfers between devices: 8.84 us -> 4.09 us  [neighbour_shift(): return lax.ppermute(block, 'lat', pairs)]
    ppermute x4, waiting for transfers between devices: 7.24 us -> 3.32 us  [neighbour_shift(): return lax.ppermute(block, 'lon', pairs)]
    concatenate x0 -> x1, other arithmetic: none -> 3.14 us  [on_device(): jnp.concatenate([top, jnp.concatenate([left, inside, right], axis=-1), bo...]
  transfers between devices with their start and end apart: 8 -> 8, of which waited for: 4 -> 3; matrix products, arithmetic and copies ran while one was open for 12% -> 9% of each run, Pallas kernels for 0% -> 0%
where the time goes in v11:
time: 137 us; the launch traced here: 136 us
  local copies, waits for them, and re-layouts  46.7 us (34%)
  starting transfers between devices  39.3 us (29%)
  other arithmetic  33.6 us (25%)
  waiting for transfers between devices  7.41 us (5%)
  matrix products  6.3 us (5%)
  between operations  2.66 us (2%)
    add x20, other arithmetic, diffuse(): result = result + weight * (near - center)  24.1 us
    ppermute x4, starting transfers between devices, neighbour_shift(): return lax.ppermute(block, 'lon', pairs)  22.7 us
    ppermute x4, starting transfers between devices, neighbour_shift(): return lax.ppermute(block, 'lat', pairs)  16.5 us
    slice x8, local copies, waits for them, and re-layouts, trim(): return [w[k:w.shape[0] - k, k:w.shape[1] - k] for w in weights]  5.46 us
    add x4, local copies, waits for them, and re-layouts, diffuse(): result = result + weight * (near - center)  4.95 us
    unnamed x124, local copies, waits for them, and re-layouts  4.2 us
    ppermute x4, waiting for transfers between devices, neighbour_shift(): return lax.ppermute(block, 'lat', pairs)  4.09 us
    slice x16, local copies, waits for them, and re-layouts, state_on(): w[r0 + 1:r1 + 3, c0 + 1:c1 + 3]  3.57 us
  transfers between devices with their start and end apart: 8, of which 3 were waited for; matrix products, arithmetic and copies ran while one was open for 9% of the time, Pallas kernels for 0%

profile of v11, /device:TPU:6, one launch (start us, length us, event | category | flops | bytes accessed | tf_op | source)
XLA Modules:
  0.0 136.0 jit_solution(1359849656790628668)
XLA Ops:
  1.4 1.0 slice_multiply_fusion.7
  5.0 6.2 %multiply_add_fusion.2 = f32[80,30,126]{2,1,0:T(8,128)} fusion(f32[80,32,128]{2,1,0:T(8,128)} %param.25, f32[30,126]{1,0:T(8,128)S(1)} %get-tuple-element.126, f32[30,126]{1,0:T(8,128)S(1)} %get-tuple-element.127, f32[30,126]{1,0:T(8,128)S(1)} %get-tuple-element.125, f32[30,126]{1,0:T(8,128)S(1)} %get-tuple-element.124), kind=kLoop, calls=%fused_computation.38 | loop fusion | flops 3628800 | bytes 7318080 | tf_op jit(solution)/shard_map/add | solution.py:88
  13.1 6.1 %fusion.8 = f32[80,28,124]{2,1,0:T(8,128)} fusion(f32[80,30,126]{2,1,0:T(8,128)} %multiply_add_fusion.2, f32[28,124]{1,0:T(8,128)} %slice.1225, f32[28,124]{1,0:T(8,128)} %slice.1223, f32[28,124]{1,0:T(8,128)} %slice.1221, f32[28,124]{1,0:T(8,128)} %slice.1219), kind=kLoop, calls=%fused_computation.28 | loop fusion | flops 3333120 | bytes 6721792 | tf_op jit(solution)/shard_map/add | solution.py:88
  19.2 3.9 %collective-permute-start = (f32[82,32,3]{0,2,1:T(4,128)S(1)}, f32[82,32,3]{0,2,1:T(4,128)S(1)}, u32[]{:S(2)}, u32[]{:S(2)}) collective-permute-start(f32[82,32,3]{0,2,1:T(4,128)S(1)} %pad_maximum_fusion.13), channel_id=1, source_target_pairs={{496,0},{0,16},{16,32},{32,48},{48,64},{64,80},{80,96},{96,112},{1... | collective-permute-start | bytes 94472 | tf_op jit(solution)/shard_map/ppermute | solution.py:16
  23.2 10.5 %collective-permute-start.1 = (f32[82,32,4]{0,2,1:T(4,128)S(1)}, f32[82,32,4]{0,2,1:T(4,128)S(1)}, u32[]{:S(2)}, u32[]{:S(2)}) collective-permute-start(f32[82,32,4]{0,2,1:T(4,128)S(1)} %pad_maximum_fusion.14), channel_id=1, source_target_pairs={{16,0},{32,16},{48,32},{64,48},{80,64},{96,80},{112,96},{128,112},... | collective-permute-start | bytes 125960 | tf_op jit(solution)/shard_map/ppermute | solution.py:16
  35.9 0.8 pad_maximum_fusion.10
  36.7 1.9 %collective-permute-start.2 = (f32[82,3,135]{0,2,1:T(8,128)}, f32[82,3,135]{0,2,1:T(8,128)S(1)}, u32[]{:S(2)}, u32[]{:S(2)}) collective-permute-start(f32[82,3,135]{0,2,1:T(8,128)} %pad_maximum_fusion.10), channel_id=1, source_target_pairs={{0,1},{1,2},{2,3},{3,4},{4,5},{5,6},{6,7},{7,8},{8,9},{9,10},{10,1... | collective-permute-start | bytes 398528 | tf_op jit(solution)/shard_map/ppermute | solution.py:19
  38.8 6.2 %collective-permute-start.3 = (f32[82,4,135]{0,2,1:T(8,128)S(1)}, f32[82,4,135]{0,2,1:T(8,128)S(1)}, u32[]{:S(2)}, u32[]{:S(2)}) collective-permute-start(f32[82,4,135]{0,2,1:T(8,128)S(1)} %pad_maximum_fusion.9), channel_id=1, source_target_pairs={{1,0},{2,1},{3,2},{4,3},{5,4},{6,5},{7,6},{8,7},{9,8},{10,9},{11,1... | collective-permute-start | bytes 531368 | tf_op jit(solution)/shard_map/ppermute | solution.py:19
  47.9 0.9 collective-permute-done.3
  83.5 2.1 %copy.84 = f32[80,28,2]{2,1,0:T(8,128)} copy(f32[80,28,2]{0,2,1:T(2,128)S(1)} %fusion.171) | data formatting | bytes 35840 | tf_op jit(solution)/shard_map/add | solution.py:88
  86.6 1.9 %copy.85 = f32[80,28,3]{2,1,0:T(8,128)S(1)} copy(f32[80,28,3]{0,2,1:T(4,128)} %fusion.128) | data formatting | bytes 53760 | tf_op jit(solution)/shard_map/add | solution.py:88
  88.5 1.7 %fusion.22 = f32[80,5,131]{0,2,1:T(8,128)S(1)} fusion(f32[80,4,135]{0,2,1:T(8,128)} %bitcast.55, f32[80,32,4]{0,2,1:T(4,128)S(1)} %bitcast.54, f32[80,32,128]{0,2,1:T(8,128)S(1)} %copy.71, f32[80,32,3]{0,2,1:T(4,128)S(1)} %bitcast.51, f32[5,131]{1,0:T(8,128)} %slice.1298, f32[5,131]{1,0:T(8,128)} %slice.1297, f32[5,131]{1,0:T(8,128)} %slice.1296, ...), kind=kLoop, calls=%fused_computation.54 | loop fusion | flops 1414800 | bytes 1775280 | tf_op jit(solution)/shard_map/add | solution.py:88
  91.6 3.1 %pad_maximum_fusion = f32[80,33,129]{2,1,0:T(8,128)S(1)} fusion(f32[80,3,129]{2,1,0:T(4,128)S(1)} %copy.87, f32[80,28,3]{2,1,0:T(8,128)S(1)} %copy.85, f32[80,28,124]{2,1,0:T(8,128)} %fusion.8, f32[80,28,2]{2,1,0:T(8,128)S(1)} %copy-done.1, f32[80,2,129]{2,1,0:T(2,128)} %copy.86), kind=kLoop, calls=%fused_computation | loop fusion | flops 1362240 | bytes 2724480 | tf_op jit(solution)/shard_map/concatenate | solution.py:122
  94.9 2.8 %fusion.15 = f32[80,128]{1,0:T(8,128)S(1)} fusion(f32[80,33,129]{2,1,0:T(8,128)S(1)} %pad_maximum_fusion, f32[33,128]{1,0:T(8,128)S(1)} %copy-done.6, f32[128]{0:T(128)S(1)} %copy-done.53, s32[128]{0:T(128)S(1)} %copy-done.58, f32[128]{0:T(128)S(1)} %copy-done.52, s32[128]{0:T(128)S(1)} %bitcast.57), kind=kOutput, calls=%fused_computation.39 | convolution fusion | flops 523848320 | bytes 1422144 | tf_op jit(solution)/shard_map/zrc,co->zro/dot_general | solution.py:140
  98.4 3.5 %fusion.5 = f32[80,33,129]{0,2,1:T(8,128)S(1)} fusion(f32[80,128]{1,0:T(8,128)S(1)} %bitcast_divide_fusion, f32[33,128]{1,0:T(8,128)S(1)} %copy-done.6, f32[128]{0:T(128)S(1)} %copy-done.53, s32[128]{0:T(128)S(1)} %copy-done.58, f32[128]{0:T(128)S(1)} %copy-done.52, s32[128]{0:T(128)S(1)} %bitcast.58), kind=kOutput, calls=%fused_computation.24 | convolution fusion | flops 523520640 | bytes 1422144 | tf_op jit(solution)/shard_map/zro,co->zrc/dot_general | solution.py:149
  102.6 6.4 %collective-permute-start.4 = (f32[80,2,133]{0,2,1:T(8,128)S(1)}, f32[80,2,133]{0,2,1:T(8,128)S(1)}, u32[]{:S(2)}, u32[]{:S(2)}) collective-permute-start(f32[80,2,133]{0,2,1:T(8,128)S(1)} %fusion.80), channel_id=1, source_target_pairs={{1,0},{2,1},{3,2},{4,3},{5,4},{6,5},{7,6},{8,7},{9,8},{10,9},{11,1... | collective-permute-start | bytes 255368 | tf_op jit(solution)/shard_map/ppermute | solution.py:19
  109.6 2.1 %collective-permute-start.5 = (f32[80,3,133]{0,2,1:T(8,128)S(1)}, f32[80,3,133]{0,2,1:T(8,128)S(1)}, u32[]{:S(2)}, u32[]{:S(2)}) collective-permute-start(f32[80,3,133]{0,2,1:T(8,128)S(1)} %fusion.44), channel_id=1, source_target_pairs={{0,1},{1,2},{2,3},{3,4},{4,5},{5,6},{6,7},{7,8},{8,9},{9,10},{10,1... | collective-permute-start | bytes 383048 | tf_op jit(solution)/shard_map/ppermute | solution.py:19
  112.4 3.2 %multiply_add_fusion = f32[80,35,131]{0,2,1:T(8,128)S(1)} fusion(f32[80,33,129]{0,2,1:T(8,128)S(1)} %fusion.5, f32[35,131]{1,0:T(8,128)S(1)} %copy-done.10, f32[35,131]{1,0:T(8,128)S(1)} %copy-done.9, f32[35,131]{1,0:T(8,128)S(1)} %copy-done.8, f32[35,131]{1,0:T(8,128)S(1)} %copy-done.7), kind=kLoop, calls=%fused_computation.3 | loop fusion | flops 4401600 | bytes 2902800 | tf_op jit(solution)/shard_map/add | solution.py:88
  116.1 3.2 %collective-permute-done.5 = f32[80,3,133]{0,2,1:T(8,128)S(1)} collective-permute-done((f32[80,3,133]{0,2,1:T(8,128)S(1)}, f32[80,3,133]{0,2,1:T(8,128)S(1)}, u32[]{:S(2)}, u32[]{:S(2)}) %collective-permute-start.5) | collective-permute-done | bytes 127712 | tf_op jit(solution)/shard_map/ppermute | solution.py:19
  119.3 6.4 %collective-permute-start.6 = (f32[80,32,2]{0,2,1:T(2,128)S(1)}, f32[80,32,2]{0,2,1:T(2,128)S(1)}, u32[]{:S(2)}, u32[]{:S(2)}) collective-permute-start(f32[80,32,2]{0,2,1:T(2,128)S(1)} %fusion.181), channel_id=1, source_target_pairs={{16,0},{32,16},{48,32},{64,48},{80,64},{96,80},{112,96},{128,112},... | collective-permute-start | bytes 61448 | tf_op jit(solution)/shard_map/ppermute | solution.py:16
  125.7 1.9 %collective-permute-start.7 = (f32[80,32,3]{0,2,1:T(4,128)S(1)}, f32[80,32,3]{0,2,1:T(4,128)S(1)}, u32[]{:S(2)}, u32[]{:S(2)}) collective-permute-start(f32[80,32,3]{0,2,1:T(4,128)S(1)} %fusion.178), channel_id=1, source_target_pairs={{496,0},{0,16},{16,32},{32,48},{48,64},{64,80},{80,96},{96,112},{1... | collective-permute-start | bytes 92168 | tf_op jit(solution)/shard_map/ppermute | solution.py:16
  127.6 2.8 %multiply_add_fusion.1 = f32[80,32,128]{0,2,1:T(8,128)S(1)} fusion(f32[80,35,131]{0,2,1:T(8,128)S(1)} %multiply_add_fusion, f32[32,128]{1,0:T(8,128)S(1)} %copy-done.22, f32[32,128]{1,0:T(8,128)S(1)} %copy-done.21, f32[32,128]{1,0:T(8,128)S(1)} %copy-done.20, f32[32,128]{1,0:T(8,128)S(1)} %slice.1354), kind=kLoop, calls=%fused_computation.22 | loop fusion | flops 3932160 | bytes 7929856 | tf_op jit(solution)/shard_map/add | solution.py:88
  130.6 3.3 %collective-permute-done.7 = f32[80,32,3]{0,2,1:T(4,128)S(1)} collective-permute-done((f32[80,32,3]{0,2,1:T(4,128)S(1)}, f32[80,32,3]{0,2,1:T(4,128)S(1)}, u32[]{:S(2)}, u32[]{:S(2)}) %collective-permute-start.7) | collective-permute-done | bytes 30752 | tf_op jit(solution)/shard_map/ppermute | solution.py:16
  134.3 1.7 %copy.89 = f32[80,32,128]{2,1,0:T(8,128)} copy(f32[80,32,128]{0,2,1:T(8,128)S(1)} %scatter-add.39) | data formatting | bytes 2621440
  (267 shorter events, 49.6 us)
Async XLA Ops:
  1.4 10.8 %copy-start.4 = (f32[1,32,128]{2,1,0:T(8,128)}, f32[1,32,128]{2,1,0:T(8,128)S(1)}, u32[]{:S(2)}) copy-start(f32[1,32,128]{2,1,0:T(8,128)S(1)} %get-tuple-element.129) | copy-start | bytes 49156
  13.0 20.6 %copy-start.5 = (f32[1,32,128]{2,1,0:T(8,128)S(1)}, f32[1,32,128]{2,1,0:T(8,128)}, u32[]{:S(2)}) copy-start(f32[1,32,128]{2,1,0:T(8,128)} %copy-done.4) | copy-start | bytes 49156
  13.1 20.7 %copy-start.54 = (f32[1,2,128]{2,1,0:T(2,128)S(1)}, f32[1,2,128]{2,1,0:T(2,128)}, u32[]{:S(2)}) copy-start(f32[1,2,128]{2,1,0:T(2,128)} %param.32) | copy-start | bytes 3076
  13.1 21.8 %copy-start.59 = (s32[1,128]{1,0:T(1,128)S(1)}, s32[1,128]{1,0:T(1,128)}, u32[]{:S(2)}) copy-start(s32[1,128]{1,0:T(1,128)} %param.30) | copy-start | bytes 1540
  19.2 25.8 %copy-start.56 = (s32[1,128]{1,0:T(1,128)S(1)}, s32[1,128]{1,0:T(1,128)}, u32[]{:S(2)}) copy-start(s32[1,128]{1,0:T(1,128)} %param.31) | copy-start | bytes 1540
  19.2 16.6 %collective-permute-start = (f32[82,32,3]{0,2,1:T(4,128)S(1)}, f32[82,32,3]{0,2,1:T(4,128)S(1)}, u32[]{:S(2)}, u32[]{:S(2)}) collective-permute-start(f32[82,32,3]{0,2,1:T(4,128)S(1)} %pad_maximum_fusion.13), channel_id=1, source_target_pairs={{496,0},{0,16},{16,32},{32,48},{48,64},{64,80},{80,96},{96,112},{1... | collective-permute-start | bytes 94472 | tf_op jit(solution)/shard_map/ppermute | solution.py:16
  23.2 12.7 %collective-permute-start.1 = (f32[82,32,4]{0,2,1:T(4,128)S(1)}, f32[82,32,4]{0,2,1:T(4,128)S(1)}, u32[]{:S(2)}, u32[]{:S(2)}) collective-permute-start(f32[82,32,4]{0,2,1:T(4,128)S(1)} %pad_maximum_fusion.14), channel_id=1, source_target_pairs={{16,0},{32,16},{48,32},{64,48},{80,64},{96,80},{112,96},{128,112},... | collective-permute-start | bytes 125960 | tf_op jit(solution)/shard_map/ppermute | solution.py:16
  36.7 10.9 %collective-permute-start.2 = (f32[82,3,135]{0,2,1:T(8,128)}, f32[82,3,135]{0,2,1:T(8,128)S(1)}, u32[]{:S(2)}, u32[]{:S(2)}) collective-permute-start(f32[82,3,135]{0,2,1:T(8,128)} %pad_maximum_fusion.10), channel_id=1, source_target_pairs={{0,1},{1,2},{2,3},{3,4},{4,5},{5,6},{6,7},{7,8},{8,9},{9,10},{10,1... | collective-permute-start | bytes 398528 | tf_op jit(solution)/shard_map/ppermute | solution.py:19
  38.8 10.1 %collective-permute-start.3 = (f32[82,4,135]{0,2,1:T(8,128)S(1)}, f32[82,4,135]{0,2,1:T(8,128)S(1)}, u32[]{:S(2)}, u32[]{:S(2)}) collective-permute-start(f32[82,4,135]{0,2,1:T(8,128)S(1)} %pad_maximum_fusion.9), channel_id=1, source_target_pairs={{1,0},{2,1},{3,2},{4,3},{5,4},{6,5},{7,6},{8,7},{9,8},{10,9},{11,1... | collective-permute-start | bytes 531368 | tf_op jit(solution)/shard_map/ppermute | solution.py:19
  48.9 33.2 %copy-start.3 = (f32[82,4,135]{0,2,1:T(8,128)}, f32[82,4,135]{0,2,1:T(8,128)S(1)}, u32[]{:S(2)}) copy-start(f32[82,4,135]{0,2,1:T(8,128)S(1)} %collective-permute-done.3) | copy-start | bytes 531364
  98.4 10.6 %copy-start.36 = (f32[3,131]{1,0:T(4,128)S(1)}, f32[3,131]{1,0:T(4,128)}, u32[]{:S(2)}) copy-start(f32[3,131]{1,0:T(4,128)} %slice.1332) | copy-start | bytes 4720
  98.4 10.6 %copy-start.37 = (f32[3,131]{1,0:T(4,128)S(1)}, f32[3,131]{1,0:T(4,128)}, u32[]{:S(2)}) copy-start(f32[3,131]{1,0:T(4,128)} %slice.1333) | copy-start | bytes 4720
  98.4 10.6 %copy-start.38 = (f32[3,131]{1,0:T(4,128)S(1)}, f32[3,131]{1,0:T(4,128)}, u32[]{:S(2)}) copy-start(f32[3,131]{1,0:T(4,128)} %slice.1334) | copy-start | bytes 4720
  98.4 10.6 %copy-start.39 = (f32[3,131]{1,0:T(4,128)S(1)}, f32[3,131]{1,0:T(4,128)}, u32[]{:S(2)}) copy-start(f32[3,131]{1,0:T(4,128)} %slice.1335) | copy-start | bytes 4720
  102.5 9.4 %copy-start.16 = (f32[34,2]{1,0:T(8,128)S(1)}, f32[34,2]{1,0:T(8,128)}, u32[]{:S(2)}) copy-start(f32[34,2]{1,0:T(8,128)} %slice.1312) | copy-start | bytes 820
  102.5 9.4 %copy-start.17 = (f32[34,2]{1,0:T(8,128)S(1)}, f32[34,2]{1,0:T(8,128)}, u32[]{:S(2)}) copy-start(f32[34,2]{1,0:T(8,128)} %slice.1313) | copy-start | bytes 820
  102.5 9.4 %copy-start.18 = (f32[34,2]{1,0:T(8,128)S(1)}, f32[34,2]{1,0:T(8,128)}, u32[]{:S(2)}) copy-start(f32[34,2]{1,0:T(8,128)} %slice.1314) | copy-start | bytes 820
  102.6 13.5 %collective-permute-start.4 = (f32[80,2,133]{0,2,1:T(8,128)S(1)}, f32[80,2,133]{0,2,1:T(8,128)S(1)}, u32[]{:S(2)}, u32[]{:S(2)}) collective-permute-start(f32[80,2,133]{0,2,1:T(8,128)S(1)} %fusion.80), channel_id=1, source_target_pairs={{1,0},{2,1},{3,2},{4,3},{5,4},{6,5},{7,6},{8,7},{9,8},{10,9},{11,1... | collective-permute-start | bytes 255368 | tf_op jit(solution)/shard_map/ppermute | solution.py:19
  109.6 9.7 %collective-permute-start.5 = (f32[80,3,133]{0,2,1:T(8,128)S(1)}, f32[80,3,133]{0,2,1:T(8,128)S(1)}, u32[]{:S(2)}, u32[]{:S(2)}) collective-permute-start(f32[80,3,133]{0,2,1:T(8,128)S(1)} %fusion.44), channel_id=1, source_target_pairs={{0,1},{1,2},{2,3},{3,4},{4,5},{5,6},{6,7},{7,8},{8,9},{9,10},{10,1... | collective-permute-start | bytes 383048 | tf_op jit(solution)/shard_map/ppermute | solution.py:19
  112.3 15.3 %copy-start.20 = (f32[32,128]{1,0:T(8,128)S(1)}, f32[32,128]{1,0:T(8,128)}, u32[]{:S(2)}) copy-start(f32[32,128]{1,0:T(8,128)} %slice.1355) | copy-start | bytes 49156
  112.3 15.3 %copy-start.21 = (f32[32,128]{1,0:T(8,128)S(1)}, f32[32,128]{1,0:T(8,128)}, u32[]{:S(2)}) copy-start(f32[32,128]{1,0:T(8,128)} %slice.1356) | copy-start | bytes 49156
  112.4 15.3 %copy-start.22 = (f32[32,128]{1,0:T(8,128)S(1)}, f32[32,128]{1,0:T(8,128)}, u32[]{:S(2)}) copy-start(f32[32,128]{1,0:T(8,128)} %slice.1357) | copy-start | bytes 49156
  119.3 11.3 %collective-permute-start.6 = (f32[80,32,2]{0,2,1:T(2,128)S(1)}, f32[80,32,2]{0,2,1:T(2,128)S(1)}, u32[]{:S(2)}, u32[]{:S(2)}) collective-permute-start(f32[80,32,2]{0,2,1:T(2,128)S(1)} %fusion.181), channel_id=1, source_target_pairs={{16,0},{32,16},{48,32},{64,48},{80,64},{96,80},{112,96},{128,112},... | collective-permute-start | bytes 61448 | tf_op jit(solution)/shard_map/ppermute | solution.py:16
  125.7 8.3 %collective-permute-start.7 = (f32[80,32,3]{0,2,1:T(4,128)S(1)}, f32[80,32,3]{0,2,1:T(4,128)S(1)}, u32[]{:S(2)}, u32[]{:S(2)}) collective-permute-start(f32[80,32,3]{0,2,1:T(4,128)S(1)} %fusion.178), channel_id=1, source_target_pairs={{496,0},{0,16},{16,32},{32,48},{48,64},{64,80},{80,96},{96,112},{1... | collective-permute-start | bytes 92168 | tf_op jit(solution)/shard_map/ppermute | solution.py:16
  (44 other events, 199.1 us)

commit v12 on v9

--- a/solution.py
+++ b/solution.py
@@ -33,21 +33,21 @@
     def joined(window):
         return jnp.concatenate([p[window] for p in parts], axis=0)
 
-    west = neighbour_shift(joined((Ellipsis, slice(None), slice(cols - hw, None))), 0, -1)
-    east = neighbour_shift(joined((Ellipsis, slice(None), slice(0, he))), 0, 1)
-    edge_n = jnp.concatenate(
-        [west[..., rows - hn :, :], joined((Ellipsis, slice(rows - hn, None), slice(None))),
-         east[..., rows - hn :, :]], axis=-1)
-    edge_s = jnp.concatenate(
-        [west[..., :hs, :], joined((Ellipsis, slice(0, hs), slice(None))), east[..., :hs, :]], axis=-1)
-    north = neighbour_shift(edge_n, -1, 0)
-    south = neighbour_shift(edge_s, 1, 0)
+    north = neighbour_shift(joined((Ellipsis, slice(rows - hn, None), slice(None))), -1, 0)
+    south = neighbour_shift(joined((Ellipsis, slice(0, hs), slice(None))), 1, 0)
+    edge_w = jnp.concatenate(
+        [north[..., cols - hw :], joined((Ellipsis, slice(None), slice(cols - hw, None))),
+         south[..., cols - hw :]], axis=-2)
+    edge_e = jnp.concatenate(
+        [north[..., :he], joined((Ellipsis, slice(None), slice(0, he))), south[..., :he]], axis=-2)
+    west = neighbour_shift(edge_w, 0, -1)
+    east = neighbour_shift(edge_e, 0, 1)
 
     out, at = [], 0
     for part, size in zip(parts, sizes):
         span = slice(at, at + size)
-        middle = jnp.concatenate([west[span], part, east[span]], axis=-1)
-        out.append(jnp.concatenate([north[span], middle, south[span]], axis=-2))
+        middle = jnp.concatenate([north[span], part, south[span]], axis=-2)
+        out.append(jnp.concatenate([west[span], middle, east[span]], axis=-1))
         at += size
     return out
 

time: 83.7 us -> 84.4 us (level)
    ppermute x4, starting transfers between devices: 9.33 us -> 11.1 us  [neighbour_shift(): return lax.ppermute(block, 'lat', pairs)]
    ppermute x4, starting transfers between devices: 20.2 us -> 19.3 us  [neighbour_shift(): return lax.ppermute(block, 'lon', pairs)]
where the time goes in v12:
time: 84.4 us; the launch traced here: 83.9 us
  starting transfers between devices  30.3 us (36%)
  other arithmetic  18 us (21%)
  waiting for transfers between devices  16.1 us (19%)
  matrix products  8.93 us (11%)
  local copies, waits for them, and re-layouts  8.7 us (10%)
  between operations  1.88 us (2%)
    ppermute x4, starting transfers between devices, neighbour_shift(): return lax.ppermute(block, 'lon', pairs)  19.3 us
    add x12, other arithmetic, diffuse(): result = result + weight * (near - center)  14.6 us
    ppermute x4, starting transfers between devices, neighbour_shift(): return lax.ppermute(block, 'lat', pairs)  11.1 us
    ppermute x4, waiting for transfers between devices, neighbour_shift(): return lax.ppermute(block, 'lat', pairs)  8.74 us
    ppermute x4, waiting for transfers between devices, neighbour_shift(): return lax.ppermute(block, 'lon', pairs)  7.34 us
    dot_general x1, matrix products, on_device(): along = jnp.einsum('zrc,co->zro', state, wx, precision=hi)  5.65 us
    unnamed x16, local copies, waits for them, and re-layouts  4.22 us
    dot_general x1, matrix products, on_device(): adjoint = jnp.einsum('zro,co->zrc', spread, wx, precision=hi)  3.29 us
  transfers between devices with their start and end apart: 8, of which 4 were waited for; matrix products, arithmetic and copies ran while one was open for 12% of the time, Pallas kernels for 0%

profile of v12, /device:TPU:6, one launch (start us, length us, event | category | flops | bytes accessed | tf_op | source)
XLA Modules:
  0.0 83.9 jit_solution(1077876034886915809)
XLA Ops:
  0.6 0.7 convert_bitcast_fusion
  1.4 0.7 fusion.112
  2.2 1.8 %copy.67 = f32[80,32,128]{0,2,1:T(8,128)S(1)} copy(f32[80,32,128]{2,1,0:T(8,128)} %param.25) | data formatting | bytes 2621440 | tf_op args[0]
  4.3 4.8 %collective-permute-start.1 = (f32[82,4,128]{0,2,1:T(8,128)S(1)}, f32[82,4,128]{0,2,1:T(8,128)S(1)}, u32[]{:S(2)}, u32[]{:S(2)}) collective-permute-start(f32[82,4,128]{0,2,1:T(8,128)S(1)} %pad_maximum_fusion.1), channel_id=1, source_target_pairs={{1,0},{2,1},{3,2},{4,3},{5,4},{6,5},{7,6},{8,7},{9,8},{10,9},{11,1... | collective-permute-start | bytes 503816 | tf_op jit(solution)/shard_map/ppermute | solution.py:19
  9.4 1.9 %collective-permute-start = (f32[82,3,128]{0,2,1:T(8,128)S(1)}, f32[82,3,128]{0,2,1:T(8,128)S(1)}, u32[]{:S(2)}, u32[]{:S(2)}) collective-permute-start(f32[82,3,128]{0,2,1:T(8,128)S(1)} %pad_maximum_fusion.2), channel_id=1, source_target_pairs={{0,1},{1,2},{2,3},{3,4},{4,5},{5,6},{6,7},{7,8},{8,9},{9,10},{10,1... | collective-permute-start | bytes 377864 | tf_op jit(solution)/shard_map/ppermute | solution.py:19
  12.8 6.0 %collective-permute-done = f32[82,3,128]{0,2,1:T(8,128)S(1)} collective-permute-done((f32[82,3,128]{0,2,1:T(8,128)S(1)}, f32[82,3,128]{0,2,1:T(8,128)S(1)}, u32[]{:S(2)}, u32[]{:S(2)}) %collective-permute-start) | collective-permute-done | bytes 125984 | tf_op jit(solution)/shard_map/ppermute | solution.py:19
  18.9 11.5 %collective-permute-start.3 = (f32[82,39,4]{0,2,1:T(4,128)S(1)}, f32[82,39,4]{0,2,1:T(4,128)S(1)}, u32[]{:S(2)}, u32[]{:S(2)}) collective-permute-start(f32[82,39,4]{0,2,1:T(4,128)S(1)} %pad_maximum_fusion.5), channel_id=1, source_target_pairs={{16,0},{32,16},{48,32},{64,48},{80,64},{96,80},{112,96},{128,112},... | collective-permute-start | bytes 153512 | tf_op jit(solution)/shard_map/ppermute | solution.py:16
  30.6 1.9 %collective-permute-start.2 = (f32[82,39,3]{0,2,1:T(4,128)S(1)}, f32[82,39,3]{0,2,1:T(4,128)S(1)}, u32[]{:S(2)}, u32[]{:S(2)}) collective-permute-start(f32[82,39,3]{0,2,1:T(4,128)S(1)} %pad_maximum_fusion.4), channel_id=1, source_target_pairs={{496,0},{0,16},{16,32},{32,48},{48,64},{64,80},{80,96},{96,112},{1... | collective-permute-start | bytes 115136 | tf_op jit(solution)/shard_map/ppermute | solution.py:16
  33.0 6.0 %collective-permute-done.2 = f32[82,39,3]{0,2,1:T(4,128)S(1)} collective-permute-done((f32[82,39,3]{0,2,1:T(4,128)S(1)}, f32[82,39,3]{0,2,1:T(4,128)S(1)}, u32[]{:S(2)}, u32[]{:S(2)}) %collective-permute-start.2) | collective-permute-done | bytes 38408 | tf_op jit(solution)/shard_map/ppermute | solution.py:16
  39.1 0.3 copy.78
  43.1 3.6 %fusion.1 = f32[80,37,133]{0,2,1:T(8,128)S(1)} fusion(f32[80,39,135]{0,2,1:T(8,128)S(1)} %pad_maximum_fusion, f32[37,133]{1,0:T(8,128)S(1)} %get-tuple-element.119, f32[37,133]{1,0:T(8,128)S(1)} %get-tuple-element.117, f32[37,133]{1,0:T(8,128)S(1)} %get-tuple-element.118, f32[37,133]{1,0:T(8,128)S(1)} %get-tuple-element.116), kind=kLoop, calls=%fused_computation.3 | loop fusion | flops 4724160 | bytes 9527056 | tf_op jit(solution)/shard_map/add | solution.py:85
  46.7 2.8 %fusion.9 = f32[80,33,129]{0,2,1:T(8,128)S(1)} fusion(f32[80,37,133]{0,2,1:T(8,128)S(1)} %fusion.1, f32[33,129]{1,0:T(8,128)S(1)} %slice.875, f32[33,129]{1,0:T(8,128)S(1)} %slice.873, f32[33,129]{1,0:T(8,128)S(1)} %slice.871, f32[33,129]{1,0:T(8,128)S(1)} %slice.869), kind=kLoop, calls=%fused_computation.34 | loop fusion | flops 4086720 | bytes 8241552 | tf_op jit(solution)/shard_map/add | solution.py:85
  49.6 5.6 %fusion.18 = f32[80,128]{1,0:T(8,128)S(1)} fusion(f32[80,33,129]{0,2,1:T(8,128)S(1)} %fusion.9, f32[33,128]{1,0:T(8,128)S(1)} %select_add_fusion.3, f32[128]{0:T(128)S(1)} %get-tuple-element.124, s32[128]{0:T(128)S(1)} %add_bitcast_fusion, f32[128]{0:T(128)S(1)} %get-tuple-element.122, s32[128]{0:T(128)S(1)} %bitcast.54), kind=kOutput, calls=%fused_computation.48 | convolution fusion | flops 523848320 | bytes 1422144 | tf_op jit(solution)/shard_map/zrc,co->zro/dot_general | solution.py:125
  55.3 0.6 fusion.85
  55.9 3.3 %fusion.16 = f32[80,33,129]{0,2,1:T(8,128)S(1)} fusion(f32[80,128]{1,0:T(8,128)S(1)} %bitcast_divide_fusion, f32[33,128]{1,0:T(8,128)S(1)} %select_add_fusion.3, f32[128]{0:T(128)S(1)} %get-tuple-element.124, s32[128]{0:T(128)S(1)} %add_bitcast_fusion, f32[128]{0:T(128)S(1)} %get-tuple-element.122, s32[128]{0:T(128)S(1)} %bitcast.55), kind=kOutput, calls=%fused_computation.46 | convolution fusion | flops 523520640 | bytes 1422144 | tf_op jit(solution)/shard_map/zro,co->zrc/dot_general | solution.py:134
  59.6 1.9 %collective-permute-start.4 = (f32[80,2,133]{0,2,1:T(8,128)S(1)}, f32[80,2,133]{0,2,1:T(8,128)S(1)}, u32[]{:S(2)}, u32[]{:S(2)}) collective-permute-start(f32[80,2,133]{0,2,1:T(8,128)S(1)} %fusion.54), channel_id=1, source_target_pairs={{1,0},{2,1},{3,2},{4,3},{5,4},{6,5},{7,6},{8,7},{9,8},{10,9},{11,1... | collective-permute-start | bytes 255368 | tf_op jit(solution)/shard_map/ppermute | solution.py:19
  62.2 2.4 %collective-permute-start.5 = (f32[80,3,133]{0,2,1:T(8,128)S(1)}, f32[80,3,133]{0,2,1:T(8,128)S(1)}, u32[]{:S(2)}, u32[]{:S(2)}) collective-permute-start(f32[80,3,133]{0,2,1:T(8,128)S(1)} %fusion.26), channel_id=1, source_target_pairs={{0,1},{1,2},{2,3},{3,4},{4,5},{5,6},{6,7},{7,8},{8,9},{9,10},{10,1... | collective-permute-start | bytes 383048 | tf_op jit(solution)/shard_map/ppermute | solution.py:19
  64.6 3.4 %multiply_add_fusion = f32[80,35,131]{0,2,1:T(8,128)S(1)} fusion(f32[80,33,129]{0,2,1:T(8,128)S(1)} %fusion.16, f32[35,131]{1,0:T(8,128)S(1)} %slice.880, f32[35,131]{1,0:T(8,128)S(1)} %slice.879, f32[35,131]{1,0:T(8,128)S(1)} %slice.878, f32[35,131]{1,0:T(8,128)S(1)} %slice.877), kind=kLoop, calls=%fused_computation.13 | loop fusion | flops 4401600 | bytes 2902800 | tf_op jit(solution)/shard_map/add | solution.py:85
  68.9 2.8 %collective-permute-done.5 = f32[80,3,133]{0,2,1:T(8,128)S(1)} collective-permute-done((f32[80,3,133]{0,2,1:T(8,128)S(1)}, f32[80,3,133]{0,2,1:T(8,128)S(1)}, u32[]{:S(2)}, u32[]{:S(2)}) %collective-permute-start.5) | collective-permute-done | bytes 127712 | tf_op jit(solution)/shard_map/ppermute | solution.py:19
  71.7 1.9 %collective-permute-start.6 = (f32[80,32,2]{0,2,1:T(2,128)S(1)}, f32[80,32,2]{0,2,1:T(2,128)S(1)}, u32[]{:S(2)}, u32[]{:S(2)}) collective-permute-start(f32[80,32,2]{0,2,1:T(2,128)S(1)} %fusion.114), channel_id=1, source_target_pairs={{16,0},{32,16},{48,32},{64,48},{80,64},{96,80},{112,96},{128,112},... | collective-permute-start | bytes 61448 | tf_op jit(solution)/shard_map/ppermute | solution.py:16
  73.6 3.9 %collective-permute-start.7 = (f32[80,32,3]{0,2,1:T(4,128)S(1)}, f32[80,32,3]{0,2,1:T(4,128)S(1)}, u32[]{:S(2)}, u32[]{:S(2)}) collective-permute-start(f32[80,32,3]{0,2,1:T(4,128)S(1)} %fusion.111), channel_id=1, source_target_pairs={{496,0},{0,16},{16,32},{32,48},{48,64},{64,80},{80,96},{96,112},{1... | collective-permute-start | bytes 92168 | tf_op jit(solution)/shard_map/ppermute | solution.py:16
  77.6 2.8 %multiply_add_fusion.1 = f32[80,32,128]{0,2,1:T(8,128)S(1)} fusion(f32[80,35,131]{0,2,1:T(8,128)S(1)} %multiply_add_fusion, f32[32,128]{1,0:T(8,128)S(1)} %slice.926, f32[32,128]{1,0:T(8,128)S(1)} %slice.925, f32[32,128]{1,0:T(8,128)S(1)} %slice.924, f32[32,128]{1,0:T(8,128)S(1)} %slice.923), kind=kLoop, calls=%fused_computation.44 | loop fusion | flops 3932160 | bytes 7929856 | tf_op jit(solution)/shard_map/add | solution.py:85
  80.6 1.3 %collective-permute-done.7 = f32[80,32,3]{0,2,1:T(4,128)S(1)} collective-permute-done((f32[80,32,3]{0,2,1:T(4,128)S(1)}, f32[80,32,3]{0,2,1:T(4,128)S(1)}, u32[]{:S(2)}, u32[]{:S(2)}) %collective-permute-start.7) | collective-permute-done | bytes 30752 | tf_op jit(solution)/shard_map/ppermute | solution.py:16
  82.2 1.7 %copy.80 = f32[80,32,128]{2,1,0:T(8,128)} copy(f32[80,32,128]{0,2,1:T(8,128)S(1)} %scatter-add.39) | data formatting | bytes 2621440
  (114 shorter events, 8.0 us)
Async XLA Ops:
  2.2 6.9 %copy-start = (f32[32,128]{1,0:T(8,128)S(1)}, f32[32,128]{1,0:T(8,128)}, u32[]{:S(2)}) copy-start(f32[32,128]{1,0:T(8,128)} %param.26) | copy-start | bytes 49156
  4.0 7.4 %copy-start.3 = (f32[1,2,128]{2,1,0:T(2,128)S(1)}, f32[1,2,128]{2,1,0:T(2,128)}, u32[]{:S(2)}) copy-start(f32[1,2,128]{2,1,0:T(2,128)} %param.32) | copy-start | bytes 3076
  4.1 8.1 %copy-start.5 = (s32[1,128]{1,0:T(1,128)S(1)}, s32[1,128]{1,0:T(1,128)}, u32[]{:S(2)}) copy-start(s32[1,128]{1,0:T(1,128)} %param.30) | copy-start | bytes 1540
  4.1 8.7 %copy-start.4 = (s32[1,128]{1,0:T(1,128)S(1)}, s32[1,128]{1,0:T(1,128)}, u32[]{:S(2)}) copy-start(s32[1,128]{1,0:T(1,128)} %param.31) | copy-start | bytes 1540
  4.3 14.5 %collective-permute-start.1 = (f32[82,4,128]{0,2,1:T(8,128)S(1)}, f32[82,4,128]{0,2,1:T(8,128)S(1)}, u32[]{:S(2)}, u32[]{:S(2)}) collective-permute-start(f32[82,4,128]{0,2,1:T(8,128)S(1)} %pad_maximum_fusion.1), channel_id=1, source_target_pairs={{1,0},{2,1},{3,2},{4,3},{5,4},{6,5},{7,6},{8,7},{9,8},{10,9},{11,1... | collective-permute-start | bytes 503816 | tf_op jit(solution)/shard_map/ppermute | solution.py:19
  9.4 9.4 %collective-permute-start = (f32[82,3,128]{0,2,1:T(8,128)S(1)}, f32[82,3,128]{0,2,1:T(8,128)S(1)}, u32[]{:S(2)}, u32[]{:S(2)}) collective-permute-start(f32[82,3,128]{0,2,1:T(8,128)S(1)} %pad_maximum_fusion.2), channel_id=1, source_target_pairs={{0,1},{1,2},{2,3},{3,4},{4,5},{5,6},{6,7},{7,8},{8,9},{9,10},{10,1... | collective-permute-start | bytes 377864 | tf_op jit(solution)/shard_map/ppermute | solution.py:19
  18.9 20.5 %collective-permute-start.3 = (f32[82,39,4]{0,2,1:T(4,128)S(1)}, f32[82,39,4]{0,2,1:T(4,128)S(1)}, u32[]{:S(2)}, u32[]{:S(2)}) collective-permute-start(f32[82,39,4]{0,2,1:T(4,128)S(1)} %pad_maximum_fusion.5), channel_id=1, source_target_pairs={{16,0},{32,16},{48,32},{64,48},{80,64},{96,80},{112,96},{128,112},... | collective-permute-start | bytes 153512 | tf_op jit(solution)/shard_map/ppermute | solution.py:16
  30.6 8.4 %collective-permute-start.2 = (f32[82,39,3]{0,2,1:T(4,128)S(1)}, f32[82,39,3]{0,2,1:T(4,128)S(1)}, u32[]{:S(2)}, u32[]{:S(2)}) collective-permute-start(f32[82,39,3]{0,2,1:T(4,128)S(1)} %pad_maximum_fusion.4), channel_id=1, source_target_pairs={{496,0},{0,16},{16,32},{32,48},{48,64},{64,80},{80,96},{96,112},{1... | collective-permute-start | bytes 115136 | tf_op jit(solution)/shard_map/ppermute | solution.py:16
  49.6 5.7 %copy-start.1 = (f32[1,80,128]{2,1,0:T(8,128)S(1)}, f32[1,80,128]{2,1,0:T(8,128)}, u32[]{:S(2)}) copy-start(f32[1,80,128]{2,1,0:T(8,128)} %param.28) | copy-start | bytes 122884
  49.6 6.3 %copy-start.2 = (f32[1,80,128]{2,1,0:T(8,128)S(1)}, f32[1,80,128]{2,1,0:T(8,128)}, u32[]{:S(2)}) copy-start(f32[1,80,128]{2,1,0:T(8,128)} %param.29) | copy-start | bytes 122884
  59.6 9.2 %collective-permute-start.4 = (f32[80,2,133]{0,2,1:T(8,128)S(1)}, f32[80,2,133]{0,2,1:T(8,128)S(1)}, u32[]{:S(2)}, u32[]{:S(2)}) collective-permute-start(f32[80,2,133]{0,2,1:T(8,128)S(1)} %fusion.54), channel_id=1, source_target_pairs={{1,0},{2,1},{3,2},{4,3},{5,4},{6,5},{7,6},{8,7},{9,8},{10,9},{11,1... | collective-permute-start | bytes 255368 | tf_op jit(solution)/shard_map/ppermute | solution.py:19
  62.2 9.5 %collective-permute-start.5 = (f32[80,3,133]{0,2,1:T(8,128)S(1)}, f32[80,3,133]{0,2,1:T(8,128)S(1)}, u32[]{:S(2)}, u32[]{:S(2)}) collective-permute-start(f32[80,3,133]{0,2,1:T(8,128)S(1)} %fusion.26), channel_id=1, source_target_pairs={{0,1},{1,2},{2,3},{3,4},{4,5},{5,6},{6,7},{7,8},{8,9},{9,10},{10,1... | collective-permute-start | bytes 383048 | tf_op jit(solution)/shard_map/ppermute | solution.py:19
  71.7 8.8 %collective-permute-start.6 = (f32[80,32,2]{0,2,1:T(2,128)S(1)}, f32[80,32,2]{0,2,1:T(2,128)S(1)}, u32[]{:S(2)}, u32[]{:S(2)}) collective-permute-start(f32[80,32,2]{0,2,1:T(2,128)S(1)} %fusion.114), channel_id=1, source_target_pairs={{16,0},{32,16},{48,32},{64,48},{80,64},{96,80},{112,96},{128,112},... | collective-permute-start | bytes 61448 | tf_op jit(solution)/shard_map/ppermute | solution.py:16
  73.6 8.3 %collective-permute-start.7 = (f32[80,32,3]{0,2,1:T(4,128)S(1)}, f32[80,32,3]{0,2,1:T(4,128)S(1)}, u32[]{:S(2)}, u32[]{:S(2)}) collective-permute-start(f32[80,32,3]{0,2,1:T(4,128)S(1)} %fusion.111), channel_id=1, source_target_pairs={{496,0},{0,16},{16,32},{32,48},{48,64},{64,80},{80,96},{96,112},{1... | collective-permute-start | bytes 92168 | tf_op jit(solution)/shard_map/ppermute | solution.py:16

commit v13 on v10

--- a/solution.py
+++ b/solution.py
@@ -122,16 +122,15 @@
         col_ids == base_c + 1, frac_x[None], 0.0
     )
     hi = lax.Precision.HIGHEST
-    along = jnp.einsum("rcz,co->roz", jnp.transpose(state, (1, 2, 0)), wx, precision=hi)
-    sample = jnp.sum(along * wy[:, :, None], axis=0).T
+    stencil = wy[:, None, :] * wx[None, :, :]
+    sample = jnp.einsum("zrc,rco->zo", state, stencil, precision=hi)
 
     slots = jnp.arange(obs_row.shape[1], dtype=jnp.int32)
     valid = (slots < obs_counts[0, 0]).astype(jnp.float32)
     departure = valid * (sample - innovations[0])
     weighted = departure / (obs_sigma[0] * obs_sigma[0])
 
-    spread = wy[None] * weighted[:, None, :]
-    adjoint = jnp.einsum("zro,co->zrc", spread, wx, precision=hi)
+    adjoint = jnp.einsum("zo,rco->zrc", weighted, stencil, precision=hi)
     adjoint = lax.optimization_barrier(adjoint)
 
     spread_a = pad2(adjoint, 2)

time: 83.8 us -> 82.4 us (0.983)
  matrix products: 9.06 us -> 7.62 us
    dot_general x2, matrix products: 9.06 us -> 7.62 us  [the longest x1 3.88 us: on_device(): sample = jnp.einsum('zrc,rco->zo', state, stencil, precision=hi)]
    unnamed x16 -> x18, local copies, waits for them, and re-layouts: 4.21 us -> 4.21 us
where the time goes in v13:
time: 82.4 us; the launch traced here: 81.9 us
  starting transfers between devices  29.7 us (36%)
  other arithmetic  17.7 us (21%)
  waiting for transfers between devices  16.3 us (20%)
  local copies, waits for them, and re-layouts  8.77 us (11%)
  matrix products  7.62 us (9%)
  between operations  1.91 us (2%)
    ppermute x4, starting transfers between devices, neighbour_shift(): return lax.ppermute(block, 'lon', pairs)  20.2 us
    add x12, other arithmetic, diffuse(): result = result + weight * (near - center)  14.2 us
    ppermute x4, starting transfers between devices, neighbour_shift(): return lax.ppermute(block, 'lat', pairs)  9.5 us
    ppermute x4, waiting for transfers between devices, neighbour_shift(): return lax.ppermute(block, 'lat', pairs)  9.07 us
    ppermute x4, waiting for transfers between devices, neighbour_shift(): return lax.ppermute(block, 'lon', pairs)  7.2 us
    unnamed x18, local copies, waits for them, and re-layouts  4.21 us
    dot_general x1, matrix products, on_device(): sample = jnp.einsum('zrc,rco->zo', state, stencil, precision=hi)  3.88 us
    dot_general x1, matrix products, on_device(): adjoint = jnp.einsum('zo,rco->zrc', weighted, stencil, precision=hi)  3.73 us
  transfers between devices with their start and end apart: 8, of which 4 were waited for; matrix products, arithmetic and copies ran while one was open for 12% of the time, Pallas kernels for 0%

profile of v13, /device:TPU:6, one launch (start us, length us, event | category | flops | bytes accessed | tf_op | source)
XLA Modules:
  0.0 81.9 jit_solution(9245437560223070358)
XLA Ops:
  0.7 0.7 convert_bitcast_fusion
  1.4 0.7 fusion.100
  2.4 1.8 %copy.51 = f32[80,32,128]{0,2,1:T(8,128)S(1)} copy(f32[80,32,128]{2,1,0:T(8,128)} %param.25) | data formatting | bytes 2621440 | tf_op args[0]
  4.4 12.4 %collective-permute-start.1 = (f32[82,32,4]{0,2,1:T(4,128)S(1)}, f32[82,32,4]{0,2,1:T(4,128)S(1)}, u32[]{:S(2)}, u32[]{:S(2)}) collective-permute-start(f32[82,32,4]{0,2,1:T(4,128)S(1)} %pad_maximum_fusion.5), channel_id=1, source_target_pairs={{16,0},{32,16},{48,32},{64,48},{80,64},{96,80},{112,96},{128,112},... | collective-permute-start | bytes 125960 | tf_op jit(solution)/shard_map/ppermute | solution.py:16
  17.4 1.9 %collective-permute-start = (f32[82,32,3]{0,2,1:T(4,128)S(1)}, f32[82,32,3]{0,2,1:T(4,128)S(1)}, u32[]{:S(2)}, u32[]{:S(2)}) collective-permute-start(f32[82,32,3]{0,2,1:T(4,128)S(1)} %pad_maximum_fusion.4), channel_id=1, source_target_pairs={{496,0},{0,16},{16,32},{32,48},{48,64},{64,80},{80,96},{96,112},{1... | collective-permute-start | bytes 94472 | tf_op jit(solution)/shard_map/ppermute | solution.py:16
  19.8 5.9 %collective-permute-done = f32[82,32,3]{0,2,1:T(4,128)S(1)} collective-permute-done((f32[82,32,3]{0,2,1:T(4,128)S(1)}, f32[82,32,3]{0,2,1:T(4,128)S(1)}, u32[]{:S(2)}, u32[]{:S(2)}) %collective-permute-start) | collective-permute-done | bytes 31520 | tf_op jit(solution)/shard_map/ppermute | solution.py:16
  25.7 0.9 %pad_maximum_fusion.1 = f32[82,4,135]{0,2,1:T(8,128)} fusion(f32[82,4,4]{0,2,1:T(4,128)S(1)} %slice.847, f32[2,4,128]{0,2,1:T(8,128)S(1)} %copy.59, f32[80,4,128]{0,2,1:T(8,128)S(1)} %slice.846, f32[82,4,3]{0,2,1:T(4,128)S(1)} %slice.845), kind=kLoop, calls=%fused_computation.65 | loop fusion | flops 132840 | bytes 354240 | tf_op jit(solution)/shard_map/concatenate | solution.py:41
  26.5 3.1 %collective-permute-start.3 = (f32[82,4,135]{0,2,1:T(8,128)}, f32[82,4,135]{0,2,1:T(8,128)S(1)}, u32[]{:S(2)}, u32[]{:S(2)}) collective-permute-start(f32[82,4,135]{0,2,1:T(8,128)} %pad_maximum_fusion.1), channel_id=1, source_target_pairs={{1,0},{2,1},{3,2},{4,3},{5,4},{6,5},{7,6},{8,7},{9,8},{10,9},{11,1... | collective-permute-start | bytes 531368 | tf_op jit(solution)/shard_map/ppermute | solution.py:19
  29.7 1.9 %collective-permute-start.2 = (f32[82,3,135]{0,2,1:T(8,128)S(1)}, f32[82,3,135]{0,2,1:T(8,128)S(1)}, u32[]{:S(2)}, u32[]{:S(2)}) collective-permute-start(f32[82,3,135]{0,2,1:T(8,128)S(1)} %pad_maximum_fusion.2), channel_id=1, source_target_pairs={{0,1},{1,2},{2,3},{3,4},{4,5},{5,6},{6,7},{7,8},{8,9},{9,10},{10,1... | collective-permute-start | bytes 398528 | tf_op jit(solution)/shard_map/ppermute | solution.py:19
  32.9 0.3 copy.61
  33.2 6.1 %collective-permute-done.2 = f32[82,3,135]{0,2,1:T(8,128)S(1)} collective-permute-done((f32[82,3,135]{0,2,1:T(8,128)S(1)}, f32[82,3,135]{0,2,1:T(8,128)S(1)}, u32[]{:S(2)}, u32[]{:S(2)}) %collective-permute-start.2) | collective-permute-done | bytes 132872 | tf_op jit(solution)/shard_map/ppermute | solution.py:19
  43.0 3.5 %fusion.5 = f32[80,37,133]{0,2,1:T(8,128)S(1)} fusion(f32[80,39,135]{0,2,1:T(8,128)S(1)} %pad_maximum_fusion, f32[37,133]{1,0:T(8,128)S(1)} %get-tuple-element.117, f32[37,133]{1,0:T(8,128)S(1)} %get-tuple-element.115, f32[37,133]{1,0:T(8,128)S(1)} %get-tuple-element.116, f32[37,133]{1,0:T(8,128)S(1)} %get-tuple-element.114), kind=kLoop, calls=%fused_computation.7 | loop fusion | flops 4724160 | bytes 9527056 | tf_op jit(solution)/shard_map/add | solution.py:85
  46.5 2.8 %fusion.13 = f32[80,33,129]{0,2,1:T(8,128)S(1)} fusion(f32[80,37,133]{0,2,1:T(8,128)S(1)} %fusion.5, f32[33,129]{1,0:T(8,128)S(1)} %slice.877, f32[33,129]{1,0:T(8,128)S(1)} %slice.875, f32[33,129]{1,0:T(8,128)S(1)} %slice.873, f32[33,129]{1,0:T(8,128)S(1)} %slice.871), kind=kLoop, calls=%fused_computation.38 | loop fusion | flops 4086720 | bytes 8241552 | tf_op jit(solution)/shard_map/add | solution.py:85
  49.4 3.9 %fusion.30 = f32[80,128]{1,0:T(8,128)S(1)} fusion(f32[80,33,129]{0,2,1:T(8,128)S(1)} %fusion.13, f32[129,128]{1,0:T(8,128)S(1)} %select_add_fusion, f32[33,128]{1,0:T(8,128)S(1)} %select_add_fusion.1, f32[1,80,128]{2,1,0:T(8,128)S(1)} %copy-done.2, f32[128]{0:T(128)S(1)} %compare_convert_fusion), kind=kOutput, calls=%fused_computation.55 | convolution fusion | flops 523665536 | bytes 1527616 | tf_op jit(solution)/shard_map/zrc,rco->zo/dot_general | solution.py:126
  53.3 3.7 %fusion = f32[80,33,129]{0,2,1:T(8,128)S(1)} fusion(f32[129,128]{1,0:T(8,128)S(1)} %select_add_fusion, f32[33,128]{1,0:T(8,128)S(1)} %select_add_fusion.1, f32[80,128]{1,0:T(8,128)S(1)} %fusion.30, f32[1,80,128]{2,1,0:T(8,128)S(1)} %copy-done.3), kind=kOutput, calls=%fused_computation | convolution fusion | flops 523665536 | bytes 1527104 | tf_op jit(solution)/shard_map/zo,rco->zrc/dot_general | solution.py:133
  57.5 2.1 %collective-permute-start.4 = (f32[80,2,133]{0,2,1:T(8,128)S(1)}, f32[80,2,133]{0,2,1:T(8,128)S(1)}, u32[]{:S(2)}, u32[]{:S(2)}) collective-permute-start(f32[80,2,133]{0,2,1:T(8,128)S(1)} %fusion.66), channel_id=1, source_target_pairs={{1,0},{2,1},{3,2},{4,3},{5,4},{6,5},{7,6},{8,7},{9,8},{10,9},{11,1... | collective-permute-start | bytes 255368 | tf_op jit(solution)/shard_map/ppermute | solution.py:19
  60.2 2.4 %collective-permute-start.5 = (f32[80,3,133]{0,2,1:T(8,128)S(1)}, f32[80,3,133]{0,2,1:T(8,128)S(1)}, u32[]{:S(2)}, u32[]{:S(2)}) collective-permute-start(f32[80,3,133]{0,2,1:T(8,128)S(1)} %fusion.38), channel_id=1, source_target_pairs={{0,1},{1,2},{2,3},{3,4},{4,5},{5,6},{6,7},{7,8},{8,9},{9,10},{10,1... | collective-permute-start | bytes 383048 | tf_op jit(solution)/shard_map/ppermute | solution.py:19
  62.6 3.2 %multiply_add_fusion = f32[80,35,131]{0,2,1:T(8,128)S(1)} fusion(f32[80,33,129]{0,2,1:T(8,128)S(1)} %fusion, f32[35,131]{1,0:T(8,128)S(1)} %slice.882, f32[35,131]{1,0:T(8,128)S(1)} %slice.881, f32[35,131]{1,0:T(8,128)S(1)} %slice.880, f32[35,131]{1,0:T(8,128)S(1)} %slice.879), kind=kLoop, calls=%fused_computation.17 | loop fusion | flops 4401600 | bytes 2902800 | tf_op jit(solution)/shard_map/add | solution.py:85
  66.7 3.0 %collective-permute-done.5 = f32[80,3,133]{0,2,1:T(8,128)S(1)} collective-permute-done((f32[80,3,133]{0,2,1:T(8,128)S(1)}, f32[80,3,133]{0,2,1:T(8,128)S(1)}, u32[]{:S(2)}, u32[]{:S(2)}) %collective-permute-start.5) | collective-permute-done | bytes 127712 | tf_op jit(solution)/shard_map/ppermute | solution.py:19
  69.7 1.9 %collective-permute-start.6 = (f32[80,32,2]{0,2,1:T(2,128)S(1)}, f32[80,32,2]{0,2,1:T(2,128)S(1)}, u32[]{:S(2)}, u32[]{:S(2)}) collective-permute-start(f32[80,32,2]{0,2,1:T(2,128)S(1)} %fusion.115), channel_id=1, source_target_pairs={{16,0},{32,16},{48,32},{64,48},{80,64},{96,80},{112,96},{128,112},... | collective-permute-start | bytes 61448 | tf_op jit(solution)/shard_map/ppermute | solution.py:16
  71.6 3.9 %collective-permute-start.7 = (f32[80,32,3]{0,2,1:T(4,128)S(1)}, f32[80,32,3]{0,2,1:T(4,128)S(1)}, u32[]{:S(2)}, u32[]{:S(2)}) collective-permute-start(f32[80,32,3]{0,2,1:T(4,128)S(1)} %fusion.112), channel_id=1, source_target_pairs={{496,0},{0,16},{16,32},{32,48},{48,64},{64,80},{80,96},{96,112},{1... | collective-permute-start | bytes 92168 | tf_op jit(solution)/shard_map/ppermute | solution.py:16
  75.6 2.8 %multiply_add_fusion.1 = f32[80,32,128]{0,2,1:T(8,128)S(1)} fusion(f32[80,35,131]{0,2,1:T(8,128)S(1)} %multiply_add_fusion, f32[32,128]{1,0:T(8,128)S(1)} %slice.928, f32[32,128]{1,0:T(8,128)S(1)} %slice.927, f32[32,128]{1,0:T(8,128)S(1)} %slice.926, f32[32,128]{1,0:T(8,128)S(1)} %slice.925), kind=kLoop, calls=%fused_computation.48 | loop fusion | flops 3932160 | bytes 7929856 | tf_op jit(solution)/shard_map/add | solution.py:85
  78.6 1.3 %collective-permute-done.7 = f32[80,32,3]{0,2,1:T(4,128)S(1)} collective-permute-done((f32[80,32,3]{0,2,1:T(4,128)S(1)}, f32[80,32,3]{0,2,1:T(4,128)S(1)}, u32[]{:S(2)}, u32[]{:S(2)}) %collective-permute-start.7) | collective-permute-done | bytes 30752 | tf_op jit(solution)/shard_map/ppermute | solution.py:16
  80.2 1.7 %copy.64 = f32[80,32,128]{2,1,0:T(8,128)} copy(f32[80,32,128]{0,2,1:T(8,128)S(1)} %scatter-add.39) | data formatting | bytes 2621440
  (115 shorter events, 7.9 us)
Async XLA Ops:
  0.6 16.2 %copy-start = (f32[32,128]{1,0:T(8,128)S(1)}, f32[32,128]{1,0:T(8,128)}, u32[]{:S(2)}) copy-start(f32[32,128]{1,0:T(8,128)} %param.26) | copy-start | bytes 49156
  0.6 18.7 %copy-start.4 = (f32[1,2,128]{2,1,0:T(2,128)S(1)}, f32[1,2,128]{2,1,0:T(2,128)}, u32[]{:S(2)}) copy-start(f32[1,2,128]{2,1,0:T(2,128)} %param.32) | copy-start | bytes 3076
  0.7 18.7 %copy-start.5 = (s32[1,128]{1,0:T(1,128)S(1)}, s32[1,128]{1,0:T(1,128)}, u32[]{:S(2)}) copy-start(s32[1,128]{1,0:T(1,128)} %param.31) | copy-start | bytes 1540
  0.7 18.7 %copy-start.6 = (s32[1,128]{1,0:T(1,128)S(1)}, s32[1,128]{1,0:T(1,128)}, u32[]{:S(2)}) copy-start(s32[1,128]{1,0:T(1,128)} %param.30) | copy-start | bytes 1540
  4.4 21.2 %collective-permute-start.1 = (f32[82,32,4]{0,2,1:T(4,128)S(1)}, f32[82,32,4]{0,2,1:T(4,128)S(1)}, u32[]{:S(2)}, u32[]{:S(2)}) collective-permute-start(f32[82,32,4]{0,2,1:T(4,128)S(1)} %pad_maximum_fusion.5), channel_id=1, source_target_pairs={{16,0},{32,16},{48,32},{64,48},{80,64},{96,80},{112,96},{128,112},... | collective-permute-start | bytes 125960 | tf_op jit(solution)/shard_map/ppermute | solution.py:16
  17.4 8.3 %collective-permute-start = (f32[82,32,3]{0,2,1:T(4,128)S(1)}, f32[82,32,3]{0,2,1:T(4,128)S(1)}, u32[]{:S(2)}, u32[]{:S(2)}) collective-permute-start(f32[82,32,3]{0,2,1:T(4,128)S(1)} %pad_maximum_fusion.4), channel_id=1, source_target_pairs={{496,0},{0,16},{16,32},{32,48},{48,64},{64,80},{80,96},{96,112},{1... | collective-permute-start | bytes 94472 | tf_op jit(solution)/shard_map/ppermute | solution.py:16
  26.5 13.1 %collective-permute-start.3 = (f32[82,4,135]{0,2,1:T(8,128)}, f32[82,4,135]{0,2,1:T(8,128)S(1)}, u32[]{:S(2)}, u32[]{:S(2)}) collective-permute-start(f32[82,4,135]{0,2,1:T(8,128)} %pad_maximum_fusion.1), channel_id=1, source_target_pairs={{1,0},{2,1},{3,2},{4,3},{5,4},{6,5},{7,6},{8,7},{9,8},{10,9},{11,1... | collective-permute-start | bytes 531368 | tf_op jit(solution)/shard_map/ppermute | solution.py:19
  29.7 9.5 %collective-permute-start.2 = (f32[82,3,135]{0,2,1:T(8,128)S(1)}, f32[82,3,135]{0,2,1:T(8,128)S(1)}, u32[]{:S(2)}, u32[]{:S(2)}) collective-permute-start(f32[82,3,135]{0,2,1:T(8,128)S(1)} %pad_maximum_fusion.2), channel_id=1, source_target_pairs={{0,1},{1,2},{2,3},{3,4},{4,5},{5,6},{6,7},{7,8},{8,9},{9,10},{10,1... | collective-permute-start | bytes 398528 | tf_op jit(solution)/shard_map/ppermute | solution.py:19
  46.5 2.9 %copy-start.2 = (f32[1,80,128]{2,1,0:T(8,128)S(1)}, f32[1,80,128]{2,1,0:T(8,128)}, u32[]{:S(2)}) copy-start(f32[1,80,128]{2,1,0:T(8,128)} %param.28) | copy-start | bytes 122884
  49.4 3.9 %copy-start.3 = (f32[1,80,128]{2,1,0:T(8,128)S(1)}, f32[1,80,128]{2,1,0:T(8,128)}, u32[]{:S(2)}) copy-start(f32[1,80,128]{2,1,0:T(8,128)} %param.29) | copy-start | bytes 122884
  53.3 4.0 %copy-start.1 = (f32[80,128]{1,0:T(8,128)}, f32[80,128]{1,0:T(8,128)S(1)}, u32[]{:S(2)}) copy-start(f32[80,128]{1,0:T(8,128)S(1)} %fusion.30) | copy-start | bytes 122884
  57.5 9.2 %collective-permute-start.4 = (f32[80,2,133]{0,2,1:T(8,128)S(1)}, f32[80,2,133]{0,2,1:T(8,128)S(1)}, u32[]{:S(2)}, u32[]{:S(2)}) collective-permute-start(f32[80,2,133]{0,2,1:T(8,128)S(1)} %fusion.66), channel_id=1, source_target_pairs={{1,0},{2,1},{3,2},{4,3},{5,4},{6,5},{7,6},{8,7},{9,8},{10,9},{11,1... | collective-permute-start | bytes 255368 | tf_op jit(solution)/shard_map/ppermute | solution.py:19
  60.2 9.5 %collective-permute-start.5 = (f32[80,3,133]{0,2,1:T(8,128)S(1)}, f32[80,3,133]{0,2,1:T(8,128)S(1)}, u32[]{:S(2)}, u32[]{:S(2)}) collective-permute-start(f32[80,3,133]{0,2,1:T(8,128)S(1)} %fusion.38), channel_id=1, source_target_pairs={{0,1},{1,2},{2,3},{3,4},{4,5},{5,6},{6,7},{7,8},{8,9},{9,10},{10,1... | collective-permute-start | bytes 383048 | tf_op jit(solution)/shard_map/ppermute | solution.py:19
  69.7 8.8 %collective-permute-start.6 = (f32[80,32,2]{0,2,1:T(2,128)S(1)}, f32[80,32,2]{0,2,1:T(2,128)S(1)}, u32[]{:S(2)}, u32[]{:S(2)}) collective-permute-start(f32[80,32,2]{0,2,1:T(2,128)S(1)} %fusion.115), channel_id=1, source_target_pairs={{16,0},{32,16},{48,32},{64,48},{80,64},{96,80},{112,96},{128,112},... | collective-permute-start | bytes 61448 | tf_op jit(solution)/shard_map/ppermute | solution.py:16
  71.6 8.3 %collective-permute-start.7 = (f32[80,32,3]{0,2,1:T(4,128)S(1)}, f32[80,32,3]{0,2,1:T(4,128)S(1)}, u32[]{:S(2)}, u32[]{:S(2)}) collective-permute-start(f32[80,32,3]{0,2,1:T(4,128)S(1)} %fusion.112), channel_id=1, source_target_pairs={{496,0},{0,16},{16,32},{32,48},{48,64},{64,80},{80,96},{96,112},{1... | collective-permute-start | bytes 92168 | tf_op jit(solution)/shard_map/ppermute | solution.py:16

commit v14 on v13

--- a/solution.py
+++ b/solution.py
@@ -130,7 +130,8 @@
     departure = valid * (sample - innovations[0])
     weighted = departure / (obs_sigma[0] * obs_sigma[0])
 
-    adjoint = jnp.einsum("zo,rco->zrc", weighted, stencil, precision=hi)
+    spread = wy[None] * weighted[:, None, :]
+    adjoint = jnp.einsum("zro,co->zrc", spread, wx, precision=hi)
     adjoint = lax.optimization_barrier(adjoint)
 
     spread_a = pad2(adjoint, 2)

time: 82.4 us -> 82.4 us (level)
    unnamed x18 -> x16, local copies, waits for them, and re-layouts: 4.21 us -> 4.2 us
where the time goes in v14:
time: 82.4 us; the launch traced here: 81.9 us
  starting transfers between devices  29.7 us (36%)
  other arithmetic  17.7 us (21%)
  waiting for transfers between devices  16.1 us (20%)
  local copies, waits for them, and re-layouts  8.76 us (11%)
  matrix products  7.8 us (9%)
  between operations  1.89 us (2%)
    ppermute x4, starting transfers between devices, neighbour_shift(): return lax.ppermute(block, 'lon', pairs)  20.2 us
    add x12, other arithmetic, diffuse(): result = result + weight * (near - center)  14.2 us
    ppermute x4, starting transfers between devices, neighbour_shift(): return lax.ppermute(block, 'lat', pairs)  9.5 us
    ppermute x4, waiting for transfers between devices, neighbour_shift(): return lax.ppermute(block, 'lat', pairs)  8.89 us
    ppermute x4, waiting for transfers between devices, neighbour_shift(): return lax.ppermute(block, 'lon', pairs)  7.2 us
    dot_general x1, matrix products, on_device(): sample = jnp.einsum('zrc,rco->zo', state, stencil, precision=hi)  4.51 us
    unnamed x16, local copies, waits for them, and re-layouts  4.2 us
    dot_general x1, matrix products, on_device(): adjoint = jnp.einsum('zro,co->zrc', spread, wx, precision=hi)  3.29 us
  transfers between devices with their start and end apart: 8, of which 4 were waited for; matrix products, arithmetic and copies ran while one was open for 12% of the time, Pallas kernels for 0%

profile of v14, /device:TPU:6, one launch (start us, length us, event | category | flops | bytes accessed | tf_op | source)
XLA Modules:
  0.0 81.9 jit_solution(852371598961256610)
XLA Ops:
  0.7 0.7 convert_bitcast_fusion
  1.4 0.7 fusion.99
  2.4 1.8 %copy.51 = f32[80,32,128]{0,2,1:T(8,128)S(1)} copy(f32[80,32,128]{2,1,0:T(8,128)} %param.25) | data formatting | bytes 2621440 | tf_op args[0]
  4.4 12.4 %collective-permute-start.1 = (f32[82,32,4]{0,2,1:T(4,128)S(1)}, f32[82,32,4]{0,2,1:T(4,128)S(1)}, u32[]{:S(2)}, u32[]{:S(2)}) collective-permute-start(f32[82,32,4]{0,2,1:T(4,128)S(1)} %pad_maximum_fusion.5), channel_id=1, source_target_pairs={{16,0},{32,16},{48,32},{64,48},{80,64},{96,80},{112,96},{128,112},... | collective-permute-start | bytes 125960 | tf_op jit(solution)/shard_map/ppermute | solution.py:16
  17.4 1.9 %collective-permute-start = (f32[82,32,3]{0,2,1:T(4,128)S(1)}, f32[82,32,3]{0,2,1:T(4,128)S(1)}, u32[]{:S(2)}, u32[]{:S(2)}) collective-permute-start(f32[82,32,3]{0,2,1:T(4,128)S(1)} %pad_maximum_fusion.4), channel_id=1, source_target_pairs={{496,0},{0,16},{16,32},{32,48},{48,64},{64,80},{80,96},{96,112},{1... | collective-permute-start | bytes 94472 | tf_op jit(solution)/shard_map/ppermute | solution.py:16
  19.8 5.9 %collective-permute-done = f32[82,32,3]{0,2,1:T(4,128)S(1)} collective-permute-done((f32[82,32,3]{0,2,1:T(4,128)S(1)}, f32[82,32,3]{0,2,1:T(4,128)S(1)}, u32[]{:S(2)}, u32[]{:S(2)}) %collective-permute-start) | collective-permute-done | bytes 31520 | tf_op jit(solution)/shard_map/ppermute | solution.py:16
  25.7 0.9 %pad_maximum_fusion.1 = f32[82,4,135]{0,2,1:T(8,128)} fusion(f32[82,4,4]{0,2,1:T(4,128)S(1)} %slice.847, f32[2,4,128]{0,2,1:T(8,128)S(1)} %copy.59, f32[80,4,128]{0,2,1:T(8,128)S(1)} %slice.846, f32[82,4,3]{0,2,1:T(4,128)S(1)} %slice.845), kind=kLoop, calls=%fused_computation.65 | loop fusion | flops 132840 | bytes 354240 | tf_op jit(solution)/shard_map/concatenate | solution.py:41
  26.5 3.1 %collective-permute-start.3 = (f32[82,4,135]{0,2,1:T(8,128)}, f32[82,4,135]{0,2,1:T(8,128)S(1)}, u32[]{:S(2)}, u32[]{:S(2)}) collective-permute-start(f32[82,4,135]{0,2,1:T(8,128)} %pad_maximum_fusion.1), channel_id=1, source_target_pairs={{1,0},{2,1},{3,2},{4,3},{5,4},{6,5},{7,6},{8,7},{9,8},{10,9},{11,1... | collective-permute-start | bytes 531368 | tf_op jit(solution)/shard_map/ppermute | solution.py:19
  29.7 1.9 %collective-permute-start.2 = (f32[82,3,135]{0,2,1:T(8,128)S(1)}, f32[82,3,135]{0,2,1:T(8,128)S(1)}, u32[]{:S(2)}, u32[]{:S(2)}) collective-permute-start(f32[82,3,135]{0,2,1:T(8,128)S(1)} %pad_maximum_fusion.2), channel_id=1, source_target_pairs={{0,1},{1,2},{2,3},{3,4},{4,5},{5,6},{6,7},{7,8},{8,9},{9,10},{10,1... | collective-permute-start | bytes 398528 | tf_op jit(solution)/shard_map/ppermute | solution.py:19
  32.9 0.3 copy.61
  33.2 6.1 %collective-permute-done.2 = f32[82,3,135]{0,2,1:T(8,128)S(1)} collective-permute-done((f32[82,3,135]{0,2,1:T(8,128)S(1)}, f32[82,3,135]{0,2,1:T(8,128)S(1)}, u32[]{:S(2)}, u32[]{:S(2)}) %collective-permute-start.2) | collective-permute-done | bytes 132872 | tf_op jit(solution)/shard_map/ppermute | solution.py:19
  43.0 3.5 %fusion.1 = f32[80,37,133]{0,2,1:T(8,128)S(1)} fusion(f32[80,39,135]{0,2,1:T(8,128)S(1)} %pad_maximum_fusion, f32[37,133]{1,0:T(8,128)S(1)} %get-tuple-element.117, f32[37,133]{1,0:T(8,128)S(1)} %get-tuple-element.115, f32[37,133]{1,0:T(8,128)S(1)} %get-tuple-element.116, f32[37,133]{1,0:T(8,128)S(1)} %get-tuple-element.114), kind=kLoop, calls=%fused_computation.3 | loop fusion | flops 4724160 | bytes 9527056 | tf_op jit(solution)/shard_map/add | solution.py:85
  46.5 2.8 %fusion.9 = f32[80,33,129]{0,2,1:T(8,128)S(1)} fusion(f32[80,37,133]{0,2,1:T(8,128)S(1)} %fusion.1, f32[33,129]{1,0:T(8,128)S(1)} %slice.877, f32[33,129]{1,0:T(8,128)S(1)} %slice.875, f32[33,129]{1,0:T(8,128)S(1)} %slice.873, f32[33,129]{1,0:T(8,128)S(1)} %slice.871), kind=kLoop, calls=%fused_computation.34 | loop fusion | flops 4086720 | bytes 8241552 | tf_op jit(solution)/shard_map/add | solution.py:85
  49.4 4.5 %bitcast_divide_fusion = (f32[80,128]{1,0:T(8,128)S(1)}, f32[80,128]{1,0:T(8,128)}) fusion(f32[1,80,128]{2,1,0:T(8,128)S(1)} %copy-done.1, f32[1,80,128]{2,1,0:T(8,128)S(1)} %copy-done.2, f32[80,33,129]{0,2,1:T(8,128)S(1)} %fusion.9, f32[129,128]{1,0:T(8,128)S(1)} %select_add_fusion, f32[33,128]{1,0:T(8,128)S(1)} %select_add_fusion.1, ...), kind=kOutput, calls=%fused_computation.165 | convolution fusion | flops 523686016 | bytes 1609536 | tf_op jit(solution)/shard_map/zrc,rco->zo/dot_general | solution.py:126
  53.9 3.3 %fusion.18 = f32[80,33,129]{0,2,1:T(8,128)S(1)} fusion(f32[80,128]{1,0:T(8,128)S(1)} %get-tuple-element.124, f32[33,128]{1,0:T(8,128)S(1)} %select_add_fusion.1, f32[128]{0:T(128)S(1)} %get-tuple-element.123, s32[128]{0:T(128)S(1)} %add_bitcast_fusion, f32[128]{0:T(128)S(1)} %get-tuple-element.121, s32[128]{0:T(128)S(1)} %bitcast.53), kind=kOutput, calls=%fused_computation.47 | convolution fusion | flops 523520640 | bytes 1422144 | tf_op jit(solution)/shard_map/zro,co->zrc/dot_general | solution.py:134
  57.6 1.9 %collective-permute-start.4 = (f32[80,2,133]{0,2,1:T(8,128)S(1)}, f32[80,2,133]{0,2,1:T(8,128)S(1)}, u32[]{:S(2)}, u32[]{:S(2)}) collective-permute-start(f32[80,2,133]{0,2,1:T(8,128)S(1)} %fusion.66), channel_id=1, source_target_pairs={{1,0},{2,1},{3,2},{4,3},{5,4},{6,5},{7,6},{8,7},{9,8},{10,9},{11,1... | collective-permute-start | bytes 255368 | tf_op jit(solution)/shard_map/ppermute | solution.py:19
  60.1 2.6 %collective-permute-start.5 = (f32[80,3,133]{0,2,1:T(8,128)S(1)}, f32[80,3,133]{0,2,1:T(8,128)S(1)}, u32[]{:S(2)}, u32[]{:S(2)}) collective-permute-start(f32[80,3,133]{0,2,1:T(8,128)S(1)} %fusion.38), channel_id=1, source_target_pairs={{0,1},{1,2},{2,3},{3,4},{4,5},{5,6},{6,7},{7,8},{8,9},{9,10},{10,1... | collective-permute-start | bytes 383048 | tf_op jit(solution)/shard_map/ppermute | solution.py:19
  62.7 3.2 %multiply_add_fusion = f32[80,35,131]{0,2,1:T(8,128)S(1)} fusion(f32[80,33,129]{0,2,1:T(8,128)S(1)} %fusion.18, f32[35,131]{1,0:T(8,128)S(1)} %slice.882, f32[35,131]{1,0:T(8,128)S(1)} %slice.881, f32[35,131]{1,0:T(8,128)S(1)} %slice.880, f32[35,131]{1,0:T(8,128)S(1)} %slice.879), kind=kLoop, calls=%fused_computation.13 | loop fusion | flops 4401600 | bytes 2902800 | tf_op jit(solution)/shard_map/add | solution.py:85
  66.9 2.8 %collective-permute-done.5 = f32[80,3,133]{0,2,1:T(8,128)S(1)} collective-permute-done((f32[80,3,133]{0,2,1:T(8,128)S(1)}, f32[80,3,133]{0,2,1:T(8,128)S(1)}, u32[]{:S(2)}, u32[]{:S(2)}) %collective-permute-start.5) | collective-permute-done | bytes 127712 | tf_op jit(solution)/shard_map/ppermute | solution.py:19
  69.7 1.9 %collective-permute-start.6 = (f32[80,32,2]{0,2,1:T(2,128)S(1)}, f32[80,32,2]{0,2,1:T(2,128)S(1)}, u32[]{:S(2)}, u32[]{:S(2)}) collective-permute-start(f32[80,32,2]{0,2,1:T(2,128)S(1)} %fusion.114), channel_id=1, source_target_pairs={{16,0},{32,16},{48,32},{64,48},{80,64},{96,80},{112,96},{128,112},... | collective-permute-start | bytes 61448 | tf_op jit(solution)/shard_map/ppermute | solution.py:16
  71.6 3.9 %collective-permute-start.7 = (f32[80,32,3]{0,2,1:T(4,128)S(1)}, f32[80,32,3]{0,2,1:T(4,128)S(1)}, u32[]{:S(2)}, u32[]{:S(2)}) collective-permute-start(f32[80,32,3]{0,2,1:T(4,128)S(1)} %fusion.111), channel_id=1, source_target_pairs={{496,0},{0,16},{16,32},{32,48},{48,64},{64,80},{80,96},{96,112},{1... | collective-permute-start | bytes 92168 | tf_op jit(solution)/shard_map/ppermute | solution.py:16
  75.5 2.8 %multiply_add_fusion.1 = f32[80,32,128]{0,2,1:T(8,128)S(1)} fusion(f32[80,35,131]{0,2,1:T(8,128)S(1)} %multiply_add_fusion, f32[32,128]{1,0:T(8,128)S(1)} %slice.928, f32[32,128]{1,0:T(8,128)S(1)} %slice.927, f32[32,128]{1,0:T(8,128)S(1)} %slice.926, f32[32,128]{1,0:T(8,128)S(1)} %slice.925), kind=kLoop, calls=%fused_computation.46 | loop fusion | flops 3932160 | bytes 7929856 | tf_op jit(solution)/shard_map/add | solution.py:85
  78.5 1.3 %collective-permute-done.7 = f32[80,32,3]{0,2,1:T(4,128)S(1)} collective-permute-done((f32[80,32,3]{0,2,1:T(4,128)S(1)}, f32[80,32,3]{0,2,1:T(4,128)S(1)}, u32[]{:S(2)}, u32[]{:S(2)}) %collective-permute-start.7) | collective-permute-done | bytes 30752 | tf_op jit(solution)/shard_map/ppermute | solution.py:16
  80.2 1.7 %copy.64 = f32[80,32,128]{2,1,0:T(8,128)} copy(f32[80,32,128]{0,2,1:T(8,128)S(1)} %scatter-add.39) | data formatting | bytes 2621440
  (113 shorter events, 7.9 us)
Async XLA Ops:
  0.6 16.2 %copy-start = (f32[32,128]{1,0:T(8,128)S(1)}, f32[32,128]{1,0:T(8,128)}, u32[]{:S(2)}) copy-start(f32[32,128]{1,0:T(8,128)} %param.26) | copy-start | bytes 49156
  0.6 18.7 %copy-start.3 = (f32[1,2,128]{2,1,0:T(2,128)S(1)}, f32[1,2,128]{2,1,0:T(2,128)}, u32[]{:S(2)}) copy-start(f32[1,2,128]{2,1,0:T(2,128)} %param.32) | copy-start | bytes 3076
  0.7 18.7 %copy-start.4 = (s32[1,128]{1,0:T(1,128)S(1)}, s32[1,128]{1,0:T(1,128)}, u32[]{:S(2)}) copy-start(s32[1,128]{1,0:T(1,128)} %param.31) | copy-start | bytes 1540
  0.7 18.7 %copy-start.5 = (s32[1,128]{1,0:T(1,128)S(1)}, s32[1,128]{1,0:T(1,128)}, u32[]{:S(2)}) copy-start(s32[1,128]{1,0:T(1,128)} %param.30) | copy-start | bytes 1540
  4.4 21.2 %collective-permute-start.1 = (f32[82,32,4]{0,2,1:T(4,128)S(1)}, f32[82,32,4]{0,2,1:T(4,128)S(1)}, u32[]{:S(2)}, u32[]{:S(2)}) collective-permute-start(f32[82,32,4]{0,2,1:T(4,128)S(1)} %pad_maximum_fusion.5), channel_id=1, source_target_pairs={{16,0},{32,16},{48,32},{64,48},{80,64},{96,80},{112,96},{128,112},... | collective-permute-start | bytes 125960 | tf_op jit(solution)/shard_map/ppermute | solution.py:16
  17.4 8.3 %collective-permute-start = (f32[82,32,3]{0,2,1:T(4,128)S(1)}, f32[82,32,3]{0,2,1:T(4,128)S(1)}, u32[]{:S(2)}, u32[]{:S(2)}) collective-permute-start(f32[82,32,3]{0,2,1:T(4,128)S(1)} %pad_maximum_fusion.4), channel_id=1, source_target_pairs={{496,0},{0,16},{16,32},{32,48},{48,64},{64,80},{80,96},{96,112},{1... | collective-permute-start | bytes 94472 | tf_op jit(solution)/shard_map/ppermute | solution.py:16
  26.5 13.1 %collective-permute-start.3 = (f32[82,4,135]{0,2,1:T(8,128)}, f32[82,4,135]{0,2,1:T(8,128)S(1)}, u32[]{:S(2)}, u32[]{:S(2)}) collective-permute-start(f32[82,4,135]{0,2,1:T(8,128)} %pad_maximum_fusion.1), channel_id=1, source_target_pairs={{1,0},{2,1},{3,2},{4,3},{5,4},{6,5},{7,6},{8,7},{9,8},{10,9},{11,1... | collective-permute-start | bytes 531368 | tf_op jit(solution)/shard_map/ppermute | solution.py:19
  29.7 9.5 %collective-permute-start.2 = (f32[82,3,135]{0,2,1:T(8,128)S(1)}, f32[82,3,135]{0,2,1:T(8,128)S(1)}, u32[]{:S(2)}, u32[]{:S(2)}) collective-permute-start(f32[82,3,135]{0,2,1:T(8,128)S(1)} %pad_maximum_fusion.2), channel_id=1, source_target_pairs={{0,1},{1,2},{2,3},{3,4},{4,5},{5,6},{6,7},{7,8},{8,9},{9,10},{10,1... | collective-permute-start | bytes 398528 | tf_op jit(solution)/shard_map/ppermute | solution.py:19
  46.5 2.9 %copy-start.1 = (f32[1,80,128]{2,1,0:T(8,128)S(1)}, f32[1,80,128]{2,1,0:T(8,128)}, u32[]{:S(2)}) copy-start(f32[1,80,128]{2,1,0:T(8,128)} %param.29) | copy-start | bytes 122884
  46.5 2.9 %copy-start.2 = (f32[1,80,128]{2,1,0:T(8,128)S(1)}, f32[1,80,128]{2,1,0:T(8,128)}, u32[]{:S(2)}) copy-start(f32[1,80,128]{2,1,0:T(8,128)} %param.28) | copy-start | bytes 122884
  57.6 9.2 %collective-permute-start.4 = (f32[80,2,133]{0,2,1:T(8,128)S(1)}, f32[80,2,133]{0,2,1:T(8,128)S(1)}, u32[]{:S(2)}, u32[]{:S(2)}) collective-permute-start(f32[80,2,133]{0,2,1:T(8,128)S(1)} %fusion.66), channel_id=1, source_target_pairs={{1,0},{2,1},{3,2},{4,3},{5,4},{6,5},{7,6},{8,7},{9,8},{10,9},{11,1... | collective-permute-start | bytes 255368 | tf_op jit(solution)/shard_map/ppermute | solution.py:19
  60.1 9.5 %collective-permute-start.5 = (f32[80,3,133]{0,2,1:T(8,128)S(1)}, f32[80,3,133]{0,2,1:T(8,128)S(1)}, u32[]{:S(2)}, u32[]{:S(2)}) collective-permute-start(f32[80,3,133]{0,2,1:T(8,128)S(1)} %fusion.38), channel_id=1, source_target_pairs={{0,1},{1,2},{2,3},{3,4},{4,5},{5,6},{6,7},{7,8},{8,9},{9,10},{10,1... | collective-permute-start | bytes 383048 | tf_op jit(solution)/shard_map/ppermute | solution.py:19
  69.7 8.8 %collective-permute-start.6 = (f32[80,32,2]{0,2,1:T(2,128)S(1)}, f32[80,32,2]{0,2,1:T(2,128)S(1)}, u32[]{:S(2)}, u32[]{:S(2)}) collective-permute-start(f32[80,32,2]{0,2,1:T(2,128)S(1)} %fusion.114), channel_id=1, source_target_pairs={{16,0},{32,16},{48,32},{64,48},{80,64},{96,80},{112,96},{128,112},... | collective-permute-start | bytes 61448 | tf_op jit(solution)/shard_map/ppermute | solution.py:16
  71.6 8.3 %collective-permute-start.7 = (f32[80,32,3]{0,2,1:T(4,128)S(1)}, f32[80,32,3]{0,2,1:T(4,128)S(1)}, u32[]{:S(2)}, u32[]{:S(2)}) collective-permute-start(f32[80,32,3]{0,2,1:T(4,128)S(1)} %fusion.111), channel_id=1, source_target_pairs={{496,0},{0,16},{16,32},{32,48},{48,64},{64,80},{80,96},{96,112},{1... | collective-permute-start | bytes 92168 | tf_op jit(solution)/shard_map/ppermute | solution.py:16
